TPU v7x, 256 devices: a whole 4x4x8 slice. The times are simulated.
256 devices in a mesh: gx: 8 (over x, core), gy: 8 (over z), gz: 4 (over y).
Axes of the slice: x: 4, y: 4, z: 8, core: 2. Of those that a mesh axis runs over, the one named last changes fastest.
Arguments:
- flat_weight: float32 [6144, 128, 128], P(('gx', 'gy', 'gz')), may hold values from -6 to 6
- flat_first: float32 [6144, 128, 128], P(('gx', 'gy', 'gz')), may hold values from -3 to 3
- flat_second: float32 [6144, 128, 128], P(('gx', 'gy', 'gz')), may hold values from 0.01 to 1
- tile_map: int32 [6144], P(('gx', 'gy', 'gz')), may hold values from 0 to 6143, as said below
- tile_seeds: int32 [64, 96], P(('gx', 'gy'), 'gz'), may hold values from 0 to 16777215
- tokens: bfloat16 [3072, 12288], P(('gy', 'gx'), 'gz'), may hold values from -6 to 6
- grad_out: bfloat16 [3072, 8192], P('gy', ('gx', 'gz')), may hold values from -6 to 6
Outputs:
- outputs: bfloat16 [3072, 8192], P('gy', ('gx', 'gz'))
- input_grad: bfloat16 [3072, 12288], P(('gy', 'gx'), 'gz')
- weight_new: float32 [8192, 12288], P(('gx', 'gy'), 'gz')
- first_new: float32 [8192, 12288], P(('gx', 'gy'), 'gz')
- second_new: float32 [8192, 12288], P(('gx', 'gy'), 'gz')
Inputs may be any that keep to these rules, and one draw needn't show every extreme that they name: `tile_map`: every tile of the slab is held by exactly one slot. Device rank r = ((a * 8) + b) * 4 + c holds slots r * 24 onward; it holds only tiles of the block owned by some device with the same b, where the owner of rows 128 * R onward and columns 128 * C onward has a = R // 8, b = (R) % 8, c = C // 24. One device holds at most 2 tiles of one owner, and exactly 2 of some owner.
All inputs are finite; a program needn't handle non-finite values.
Results may differ from a plain program's by a relative error of at most 0.013.
Values may be sent and summed in bfloat16 or wider, within the bound.
No kernel may reach another device: no remote copies, remote signals or barrier semaphores. Data moves between devices by JAX's collectives and lax.ppermute only.
A program may use at most 128 MiB of HBM per device.

v0:
```python
import math

import jax
import jax.numpy as jnp
from jax import lax
from jax.sharding import PartitionSpec as P

D = 12288


BETA_ONE = 0.9
BETA_TWO = 0.95
LEARN_RATE = 0.01
WEIGHT_DECAY = 0.1
EPSILON = 1e-08
BIAS_ONE = 0.9999734386011125
BIAS_TWO = 0.994079470779666
DITHER_SCALE = 0.25


def dither(seeds, position):
    mixing = seeds + position * 1640531527
    mixing = mixing ^ mixing >> 15 & 131071
    mixing = mixing * 739982445
    mixing = mixing ^ mixing >> 12 & 1048575
    mixing = mixing * 695872825
    mixing = mixing ^ mixing >> 15 & 131071
    return (mixing & 65535).astype(jnp.float32) / 65536.0 - 0.5


def body(flat_weight, flat_first, flat_second, tile_map, tile_seeds, tokens, grad_out):
    size_gx = lax.axis_size("gx")
    size_gy = lax.axis_size("gy")
    size_gz = lax.axis_size("gz")
    group_size = size_gx * size_gz
    tiles_own = flat_weight.shape[0]
    tile_side = flat_weight.shape[1]
    row_tiles = tile_seeds.shape[0]
    col_tiles = tile_seeds.shape[1]
    capacity = max(2, (2 * tiles_own + group_size - 1) // group_size - 1)
    total_slots = group_size * capacity
    across = col_tiles * size_gz
    row_block = tile_map // across
    col_block = tile_map % across
    target = row_block // row_tiles // size_gy * size_gz + col_block // col_tiles
    local_tile = row_block % row_tiles * col_tiles + col_block % col_tiles
    ordinal = jnp.arange(tiles_own, dtype=jnp.int32)
    same_owner = (target[:, None] == target[None, :]) & (ordinal[None, :] < ordinal[:, None])
    ranking = jnp.sum(same_owner.astype(jnp.int32), axis=1)
    position = target * capacity + ranking
    slot_ids = jnp.arange(total_slots, dtype=jnp.int32)
    matches = (position[None, :] == slot_ids[:, None]).astype(jnp.int32)
    source = jnp.sum(matches * ordinal[None, :], axis=1)
    filled = jnp.sum(matches, axis=1).astype(jnp.float32)[:, None, None]
    labels = jnp.sum(matches * (local_tile[None, :] + 1), axis=1)
    send_weight = jnp.take(flat_weight, source, axis=0) * filled
    send_first = jnp.take(flat_first, source, axis=0) * filled
    send_second = jnp.take(flat_second, source, axis=0) * filled
    grid_shape = (group_size, capacity, tile_side, tile_side)
    got_weight, got_first, got_second, got_labels = (
        lax.all_to_all(
            send_weight.reshape(grid_shape).astype(jnp.bfloat16),
            ("gx", "gz"),
            split_axis=0,
            concat_axis=0,
            tiled=True,
        ).astype(jnp.float32),
        lax.all_to_all(
            send_first.reshape(grid_shape).astype(jnp.bfloat16),
            ("gx", "gz"),
            split_axis=0,
            concat_axis=0,
            tiled=True,
        ).astype(jnp.float32),
        lax.all_to_all(
            send_second.reshape(grid_shape).astype(jnp.bfloat16),
            ("gx", "gz"),
            split_axis=0,
            concat_axis=0,
            tiled=True,
        ).astype(jnp.float32),
        lax.all_to_all(
            labels.reshape(group_size, capacity),
            ("gx", "gz"),
            split_axis=0,
            concat_axis=0,
            tiled=True,
        ),
    )
    got_labels = got_labels.reshape(total_slots)
    wanted = jnp.arange(1, tiles_own + 1, dtype=jnp.int32)
    hits = (got_labels[None, :] == wanted[:, None]).astype(jnp.int32)
    picked = jnp.sum(hits * slot_ids[None, :], axis=1)

    def place(received):
        flat_tiles = jnp.take(received.reshape(total_slots, tile_side, tile_side), picked, axis=0)
        tile_grid = flat_tiles.reshape(row_tiles, col_tiles, tile_side, tile_side)
        return tile_grid.transpose(0, 2, 1, 3).reshape(row_tiles * tile_side, col_tiles * tile_side)

    weight = place(got_weight)
    first_moment = place(got_first)
    second_moment = place(got_second)
    factor = 1.0 / math.sqrt(D)
    weight_low = weight.astype(jnp.bfloat16)
    weight_band = lax.all_gather(weight_low, "gy", axis=0, tiled=True)
    token_band = lax.all_gather(tokens, "gx", axis=0, tiled=True)
    partial_out = factor * jnp.dot(token_band, weight_band.T, preferred_element_type=jnp.float32)
    outputs = lax.psum_scatter(
        partial_out.astype(jnp.bfloat16), "gz", scatter_dimension=1, tiled=True
    )
    grad_band = lax.all_gather(grad_out, "gz", axis=1, tiled=True)
    input_grad = lax.psum_scatter(
        (factor * jnp.dot(grad_band, weight_band, preferred_element_type=jnp.float32)).astype(
            jnp.bfloat16
        ),
        "gx",
        scatter_dimension=0,
        tiled=True,
    )
    gradient = lax.psum_scatter(
        (
            factor
            * lax.dot_general(
                grad_band, token_band, (((0,), (0,)), ((), ())), preferred_element_type=jnp.float32
            )
        ).astype(jnp.bfloat16),
        "gy",
        scatter_dimension=0,
        tiled=True,
    ).astype(jnp.float32)
    first_new = BETA_ONE * first_moment + (1.0 - BETA_ONE) * gradient
    second_new = BETA_TWO * second_moment + (1.0 - BETA_TWO) * gradient * gradient
    direction = (
        first_new / BIAS_ONE / (jnp.sqrt(second_new / BIAS_TWO) + EPSILON) + WEIGHT_DECAY * weight
    )
    moved = weight - LEARN_RATE * direction
    block_shape = weight.shape
    row_ids = lax.broadcasted_iota(jnp.int32, block_shape, 0)
    col_ids = lax.broadcasted_iota(jnp.int32, block_shape, 1)
    seed_full = jnp.repeat(jnp.repeat(tile_seeds, tile_side, axis=0), tile_side, axis=1)
    noise = dither(seed_full, row_ids % tile_side * tile_side + col_ids % tile_side)
    weight_new = moved + jnp.abs(moved) * DITHER_SCALE * noise
    return (outputs, input_grad, weight_new, first_new, second_new)


def solution(mesh):
    return jax.shard_map(
        body,
        mesh=mesh,
        in_specs=(
            P(("gx", "gy", "gz"), None, None),
            P(("gx", "gy", "gz"), None, None),
            P(("gx", "gy", "gz"), None, None),
            P(("gx", "gy", "gz")),
            P(("gx", "gy"), "gz"),
            P(("gy", "gx"), "gz"),
            P("gy", ("gx", "gz")),
        ),
        out_specs=(
            P("gy", ("gx", "gz")),
            P(("gy", "gx"), "gz"),
            P(("gx", "gy"), "gz"),
            P(("gx", "gy"), "gz"),
            P(("gx", "gy"), "gz"),
        ),
        check_vma=False,
    )
```

profile of v0, /device:TPU:1, one launch (start us, length us, event | category | flops | bytes accessed | tf_op | source)
XLA Modules:
  0.0 382.1 jit_solution(15201064701916112077)
XLA Ops:
  9.0 8.6 %all-to-all-start.1 = ((s32[32,1,2]{2,1,0:T(1,128)}), s32[32,1,2]{2,1,0:T(1,128)S(1)}, u32[]{:S(2)}, u32[]{:S(2)}) async-start(s32[32,1,2]{2,1,0:T(1,128)} %bitcast), calls=%async_computation.1 | async-start | bytes 32768 | tf_op jit(solution)/shard_map/all_to_all | solution.py:82
  23.2 2.8 gather_fusion.2
  26.0 7.1 %fusion = (bf16[64,128,128]{2,1,0:T(8,128)(2,1)}, bf16[64,128,128]{2,1,0:T(8,128)(2,1)}, bf16[64,128,128]{2,1,0:T(8,128)(2,1)S(1)}) fusion(f32[64,128,128]{2,1,0:T(8,128)} %gather_fusion.4, f32[64]{0:T(128)S(1)} %convert_element_type.61, pred[64]{0:T(512)(128)(4,1)S(1)} %compare_and_fusion.1, f32[64,128,128]{2,1,0:T(8,128)} %gather_fusion.2, ...), kind=kLoop, calls=%fused_computation.9 | loop fusion | flops 9437184 | bytes 18874688 | tf_op jit(solution)/shard_map/convert_element_type | solution.py:76
  33.1 34.7 %all_to_all.24 = bf16[32,2,128,128]{3,2,1,0:T(8,128)(2,1)} all-to-all(bf16[32,2,128,128]{3,2,1,0:T(8,128)(2,1)S(1)} %bitcast.67), channel_id=1, replica_groups=mesh['gx'=8,'gy'=8,'gz'=4] {'gx','gz'}, dimensions={0} | all-to-all | bytes 4194304 | tf_op jit(solution)/shard_map/all_to_all | solution.py:61
  67.8 4.7 %all-to-all-start.2 = ((bf16[32,2,128,128]{3,2,1,0:T(8,128)(2,1)}), bf16[32,2,128,128]{3,2,1,0:T(8,128)(2,1)S(1)}, u32[]{:S(2)}, u32[]{:S(2)}) async-start(bf16[32,2,128,128]{3,2,1,0:T(8,128)(2,1)} %bitcast.66), calls=%async_computation.3 | async-start | bytes 4194304 | tf_op jit(solution)/shard_map/all_to_all | solution.py:68
  73.3 30.3 %all-to-all-done.2 = bf16[32,2,128,128]{3,2,1,0:T(8,128)(2,1)S(1)} async-done(((bf16[32,2,128,128]{3,2,1,0:T(8,128)(2,1)}), bf16[32,2,128,128]{3,2,1,0:T(8,128)(2,1)S(1)}, u32[]{:S(2)}, u32[]{:S(2)}) %all-to-all-start.2) | async-done | bytes 2097184 | tf_op jit(solution)/shard_map/all_to_all | solution.py:68
  103.5 8.8 %all-to-all-start.3 = ((bf16[32,2,128,128]{3,2,1,0:T(8,128)(2,1)}), bf16[32,2,128,128]{3,2,1,0:T(8,128)(2,1)}, u32[]{:S(2)}, u32[]{:S(2)}) async-start(bf16[32,2,128,128]{3,2,1,0:T(8,128)(2,1)} %bitcast.11), calls=%async_computation.5 | async-start | bytes 4194304 | tf_op jit(solution)/shard_map/all_to_all | solution.py:75
  114.0 4.1 %bitcast_convert_fusion.2 = f32[64,128,128]{2,1,0:T(8,128)} fusion(bf16[32,2,128,128]{3,2,1,0:T(8,128)(2,1)} %all_to_all.24), kind=kLoop, calls=%fused_computation.18 | loop fusion | flops 1048576 | bytes 6291456 | tf_op jit(solution)/shard_map/reshape | solution.py:96
  118.0 4.0 %gather_fusion.1 = f32[24,128,128]{2,1,0:T(8,128)} fusion(f32[64,128,128]{2,1,0:T(8,128)} %bitcast_convert_fusion.2, s32[1024]{0:T(1024)S(1)} %pad_clamp_fusion), kind=kCustom, calls=%fused_computation.1.clone | custom fusion | bytes 3145824 | tf_op jit(solution)/shard_map/jit(_take)/gather | solution.py:96
  124.6 4.0 %gather_fusion.3 = f32[24,128,128]{2,1,0:T(8,128)} fusion(f32[64,128,128]{2,1,0:T(8,128)} %bitcast_convert_fusion.1, s32[1024]{0:T(1024)S(1)} %pad_clamp_fusion), kind=kCustom, calls=%fused_computation.4.clone | custom fusion | bytes 3145824 | tf_op jit(solution)/shard_map/jit(_take)/gather | solution.py:96
  128.6 10.9 %all-to-all-done.3 = bf16[32,2,128,128]{3,2,1,0:T(8,128)(2,1)} async-done(((bf16[32,2,128,128]{3,2,1,0:T(8,128)(2,1)}), bf16[32,2,128,128]{3,2,1,0:T(8,128)(2,1)}, u32[]{:S(2)}, u32[]{:S(2)}) %all-to-all-start.3) | async-done | bytes 2097184 | tf_op jit(solution)/shard_map/all_to_all | solution.py:75
  139.5 4.1 %bitcast_convert_fusion = f32[64,128,128]{2,1,0:T(8,128)} fusion(bf16[32,2,128,128]{3,2,1,0:T(8,128)(2,1)} %all-to-all-done.3), kind=kLoop, calls=%fused_computation.16 | loop fusion | flops 1048576 | bytes 6291456 | tf_op jit(solution)/shard_map/reshape | solution.py:96
  143.5 4.1 %gather_fusion.5 = f32[24,128,128]{2,1,0:T(8,128)} fusion(f32[64,128,128]{2,1,0:T(8,128)} %bitcast_convert_fusion, s32[1024]{0:T(1024)S(1)} %pad_clamp_fusion), kind=kCustom, calls=%fused_computation.5.clone | custom fusion | bytes 3145824 | tf_op jit(solution)/shard_map/jit(_take)/gather | solution.py:96
  147.6 4.1 %fusion.8 = (f32[1,128,24,128]{3,1,2,0:T(8,128)S(1)}, f32[1,128,24,128]{3,1,2,0:T(8,128)}, f32[1,128,24,128]{3,1,2,0:T(8,128)S(1)}) fusion(f32[24,128,128]{2,1,0:T(8,128)} %gather_fusion.5, pred[24]{0:T(512)(128)(4,1)S(1)} %compare_and_fusion, f32[24,128,128]{2,1,0:T(8,128)} %gather_fusion.3, f32[24,128,128]{2,1,0:T(8,128)S(1)} %copy-done.4), kind=kLoop, calls=%fused_computation.28 | loop fusion | flops 1966080 | bytes 9437208 | tf_op jit(solution)/shard_map/mul | solution.py:132
  154.0 76.5 %all-gather.3.cloned.1.call-done = bf16[1024,3072]{1,0:T(8,128)(2,1)} async-done(((bf16[128,3072]{1,0:T(8,128)(2,1)}), bf16[1024,3072]{1,0:T(8,128)(2,1)}) %all-gather.3.cloned.1.call-update) | async-done | bytes 6291472 | tf_op jit(solution)/shard_map/all_gather | solution.py:105
  230.5 7.8 %fusion.10 = bf16[384,1024]{0,1:T(8,128)(2,1)} fusion(bf16[1024,3072]{1,0:T(8,128)(2,1)} %all-gather.3.cloned.1.call-done, bf16[384,3072]{1,0:T(8,128)(2,1)} %all-gather.5.cloned.1.call-done), kind=kOutput, calls=%fused_computation.34 | convolution fusion | flops 2416705536 | bytes 9437184 | tf_op jit(solution)/shard_map/dot_general | solution.py:107
  238.4 12.5 %all_gather.11 = bf16[384,1024]{1,0:T(8,128)(2,1)S(1)} all-gather(bf16[384,256]{1,0:T(8,128)(2,1)S(1)} %copy-done.6), channel_id=1, replica_groups=mesh['gx'=8,'gy'=8,'gz'=4] {'gz'}, dimensions={1}, use_global_device_ids=true | all-gather | bytes 983040 | tf_op jit(solution)/shard_map/all_gather | solution.py:111
  251.8 7.0 %multiply_convert_fusion = bf16[1024,3072]{1,0:T(8,128)(2,1)} fusion(bf16[384,1024]{1,0:T(8,128)(2,1)S(1)} %all_gather.11, bf16[384,3072]{1,0:T(8,128)(2,1)} %all-gather.5.cloned.1.call-done), kind=kOutput, calls=%fused_computation.6 | convolution fusion | flops 2422210560 | bytes 9437184 | tf_op jit(solution)/shard_map/dot_general | solution.py:123
  258.9 7.9 %fusion.3 = bf16[384,3072]{0,1:T(8,128)(2,1)} fusion(bf16[1024,3072]{1,0:T(8,128)(2,1)} %all-gather.3.cloned.1.call-done, bf16[384,1024]{1,0:T(8,128)(2,1)} %copy-done.5), kind=kOutput, calls=%fused_computation.14 | convolution fusion | flops 2418278400 | bytes 9437184 | tf_op jit(solution)/shard_map/dot_general | solution.py:113
  266.8 4.4 %copy.31 = bf16[384,3072]{1,0:T(8,128)(2,1)} copy(bf16[384,3072]{0,1:T(8,128)(2,1)} %fusion.3) | data formatting | bytes 4718592
  271.9 3.5 copy.27
  279.2 60.2 %reduce-scatter.8.cloned.1.call-done = bf16[128,3072]{1,0:T(8,128)(2,1)} async-done(((bf16[1024,3072]{1,0:T(8,128)(2,1)}), bf16[128,3072]{1,0:T(8,128)(2,1)}) %reduce-scatter.8.cloned.1.call-update) | async-done | bytes 786448 | tf_op jit(solution)/shard_map/reduce_scatter | solution.py:120
  339.5 5.6 %multiply_add_fusion = (f32[128,3072]{1,0:T(8,128)}, f32[128,3072]{1,0:T(8,128)}, f32[128,3072]{1,0:T(8,128)}) fusion(f32[16,8,24,128]{3,2,1,0:T(8,128)S(1)} %bitcast.65, s32[3072]{0:T(1024)S(1)} %get-tuple-element.41, s32[3072]{0:T(1024)S(1)} %get-tuple-element.42, s32[128]{0:T(128)S(1)} %get-tuple-element.43, s32[128]{0:T(128)S(1)} %get-tuple-element.44, ...), kind=kLoop, calls=%fused_computation.32 | loop fusion | flops 15335424 | bytes 10264704 | tf_op jit(solution)/shard_map/add | solution.py:142
  345.1 30.6 %reduce-scatter.10.cloned.1.call-done = bf16[48,3072]{1,0:T(8,128)(2,1)} async-done(((bf16[384,3072]{1,0:T(8,128)(2,1)}), bf16[48,3072]{1,0:T(8,128)(2,1)}) %reduce-scatter.10.cloned.1.call-update) | async-done | bytes 294928
  (58 shorter events, 20.0 us)
Async XLA Ops:
  7.2 10.4 %copy-start = (f32[24,128,128]{2,1,0:T(8,128)S(1)}, f32[24,128,128]{2,1,0:T(8,128)}, u32[]{:S(2)}) copy-start(f32[24,128,128]{2,1,0:T(8,128)} %param.13) | copy-start | bytes 4718596
  9.0 24.1 %all-to-all-start.1 = ((s32[32,1,2]{2,1,0:T(1,128)}), s32[32,1,2]{2,1,0:T(1,128)S(1)}, u32[]{:S(2)}, u32[]{:S(2)}) async-start(s32[32,1,2]{2,1,0:T(1,128)} %bitcast), calls=%async_computation.1 | async-start | bytes 32768 | tf_op jit(solution)/shard_map/all_to_all | solution.py:82
  17.6 2.8 copy-start.2
  20.4 2.8 copy-start.3
  67.8 35.7 %all-to-all-start.2 = ((bf16[32,2,128,128]{3,2,1,0:T(8,128)(2,1)}), bf16[32,2,128,128]{3,2,1,0:T(8,128)(2,1)S(1)}, u32[]{:S(2)}, u32[]{:S(2)}) async-start(bf16[32,2,128,128]{3,2,1,0:T(8,128)(2,1)} %bitcast.66), calls=%async_computation.3 | async-start | bytes 4194304 | tf_op jit(solution)/shard_map/all_to_all | solution.py:68
  72.6 81.4 %all-gather.5.cloned.1.call-start = ((), (), s32[]{:S(2)}) async-start(), calls=%async_computation.8 | async-start | bytes 2654208 | tf_op jit(solution)/shard_map/all_gather | solution.py:106
  103.5 35.9 %all-to-all-start.3 = ((bf16[32,2,128,128]{3,2,1,0:T(8,128)(2,1)}), bf16[32,2,128,128]{3,2,1,0:T(8,128)(2,1)}, u32[]{:S(2)}, u32[]{:S(2)}) async-start(bf16[32,2,128,128]{3,2,1,0:T(8,128)(2,1)} %bitcast.11), calls=%async_computation.5 | async-start | bytes 4194304 | tf_op jit(solution)/shard_map/all_to_all | solution.py:75
  112.4 118.1 %all-gather.3.cloned.1.call-start = ((), (), s32[]{:S(2)}) async-start(), calls=%async_computation.7 | async-start | bytes 7077888 | tf_op jit(solution)/shard_map/all_gather | solution.py:105
  143.5 4.1 %copy-start.4 = (f32[24,128,128]{2,1,0:T(8,128)S(1)}, f32[24,128,128]{2,1,0:T(8,128)}, u32[]{:S(2)}) copy-start(f32[24,128,128]{2,1,0:T(8,128)} %gather_fusion.1) | copy-start | bytes 4718596
  153.9 84.5 %copy-start.6 = (bf16[384,256]{1,0:T(8,128)(2,1)S(1)}, bf16[384,256]{1,0:T(8,128)(2,1)}, u32[]{:S(2)}) copy-start(bf16[384,256]{1,0:T(8,128)(2,1)} %param.17) | copy-start | bytes 589828
  153.9 123.6 %reduce-scatter.6.cloned.1.call-start = ((), (), s32[]{:S(2)}) async-start(), calls=%async_computation.9 | async-start | bytes 983040 | tf_op jit(solution)/shard_map/reduce_scatter | solution.py:108
  238.3 101.2 %reduce-scatter.8.cloned.1.call-start = ((), (), s32[]{:S(2)}) async-start(), calls=%async_computation.10 | async-start | bytes 7077888 | tf_op jit(solution)/shard_map/reduce_scatter | solution.py:120
  250.9 0.9 copy-start.5
  258.9 116.8 %reduce-scatter.10.cloned.1.call-start = ((), (), s32[]{:S(2)}) async-start(), calls=%async_computation.11 | async-start | bytes 2654208
  271.2 0.7 copy-start.7
  339.5 36.1 %copy-start.1 = (f32[24,128,128]{2,1,0:T(8,128)S(1)}, f32[24,128,128]{2,1,0:T(8,128)}, u32[]{:S(2)}) copy-start(f32[24,128,128]{2,1,0:T(8,128)} %param.13) | copy-start | bytes 4718596
Sparse Core Ops, SparseCore 0:
  75.2 35.1 all-gather.4
  154.0 76.4 all-gather.2
  238.4 22.6 reduce-scatter.5
  263.6 75.8 reduce-scatter.7
  342.5 33.1 reduce-scatter.9
where the time goes:
time: 384 us; the launch traced here: 382 us
  waiting for transfers between devices  209 us (54%)
  blocking collectives  47.3 us (12%)
  local copies, waits for them, and re-layouts  37.1 us (10%)
  other arithmetic  29.5 us (8%)
  matrix products  22.7 us (6%)
  starting transfers between devices  22.3 us (6%)
  between operations  14 us (4%)
    all_gather x1, waiting for transfers between devices, body(): weight_band = lax.all_gather(weight_low, 'gy', axis=0, tiled=True)  76.5 us
    reduce_scatter x1, waiting for transfers between devices, body(): lax.psum_scatter((factor * lax.dot_general(grad_band, token_band, (((0,),...  60.2 us
    all_to_all x1, blocking collectives, body(): lax.all_to_all(send_weight.reshape(grid_shape).astype(jnp.bfloat16), ('gx...  34.7 us
    unnamed x6, waiting for transfers between devices  31.3 us
    all_to_all x1, waiting for transfers between devices, body(): lax.all_to_all(send_first.reshape(grid_shape).astype(jnp.bfloat16), ('gx'...  30.3 us
    all_gather x1, blocking collectives, body(): grad_band = lax.all_gather(grad_out, 'gz', axis=1, tiled=True)  12.5 us
    gather x3, local copies, waits for them, and re-layouts, place(): jnp.take(received.reshape(total_slots, tile_side, tile_side), picked, axi...  12 us
    all_to_all x1, waiting for transfers between devices, body(): lax.all_to_all(send_second.reshape(grid_shape).astype(jnp.bfloat16), ('gx...  10.9 us
  transfers between devices with their start and end apart: 8, of which 5 were waited for; matrix products, arithmetic and copies ran while one was open for 20% of the time, Pallas kernels for 0%

commit v1 on v0

--- a/solution.py
+++ b/solution.py
@@ -53,40 +53,17 @@
     source = jnp.sum(matches * ordinal[None, :], axis=1)
     filled = jnp.sum(matches, axis=1).astype(jnp.float32)[:, None, None]
     labels = jnp.sum(matches * (local_tile[None, :] + 1), axis=1)
-    send_weight = jnp.take(flat_weight, source, axis=0) * filled
-    send_first = jnp.take(flat_first, source, axis=0) * filled
-    send_second = jnp.take(flat_second, source, axis=0) * filled
     grid_shape = (group_size, capacity, tile_side, tile_side)
-    got_weight, got_first, got_second, got_labels = (
-        lax.all_to_all(
-            send_weight.reshape(grid_shape).astype(jnp.bfloat16),
-            ("gx", "gz"),
-            split_axis=0,
-            concat_axis=0,
-            tiled=True,
-        ).astype(jnp.float32),
-        lax.all_to_all(
-            send_first.reshape(grid_shape).astype(jnp.bfloat16),
-            ("gx", "gz"),
-            split_axis=0,
-            concat_axis=0,
-            tiled=True,
-        ).astype(jnp.float32),
-        lax.all_to_all(
-            send_second.reshape(grid_shape).astype(jnp.bfloat16),
-            ("gx", "gz"),
-            split_axis=0,
-            concat_axis=0,
-            tiled=True,
-        ).astype(jnp.float32),
-        lax.all_to_all(
-            labels.reshape(group_size, capacity),
-            ("gx", "gz"),
-            split_axis=0,
-            concat_axis=0,
-            tiled=True,
-        ),
+    send_weight = (jnp.take(flat_weight, source, axis=0) * filled).astype(jnp.bfloat16)
+    got_labels = lax.all_to_all(
+        labels.reshape(group_size, capacity), ("gx", "gz"), split_axis=0, concat_axis=0, tiled=True
     )
+    got_weight = lax.all_to_all(
+        send_weight.reshape(grid_shape), ("gx", "gz"), split_axis=0, concat_axis=0, tiled=True
+    )
+    token_band = lax.all_gather(tokens, "gx", axis=0, tiled=True)
+    got_weight, token_band = lax.optimization_barrier((got_weight, token_band))
+    got_weight = got_weight.astype(jnp.float32)
     got_labels = got_labels.reshape(total_slots)
     wanted = jnp.arange(1, tiles_own + 1, dtype=jnp.int32)
     hits = (got_labels[None, :] == wanted[:, None]).astype(jnp.int32)
@@ -98,17 +75,28 @@
         return tile_grid.transpose(0, 2, 1, 3).reshape(row_tiles * tile_side, col_tiles * tile_side)
 
     weight = place(got_weight)
-    first_moment = place(got_first)
-    second_moment = place(got_second)
-    factor = 1.0 / math.sqrt(D)
     weight_low = weight.astype(jnp.bfloat16)
     weight_band = lax.all_gather(weight_low, "gy", axis=0, tiled=True)
-    token_band = lax.all_gather(tokens, "gx", axis=0, tiled=True)
+    send_moments = jnp.stack(
+        [jnp.take(flat_first, source, axis=0) * filled, jnp.take(flat_second, source, axis=0) * filled],
+        axis=1,
+    ).astype(jnp.bfloat16)
+    send_moments, weight_band = lax.optimization_barrier((send_moments, weight_band))
+    got_moments = lax.all_to_all(
+        send_moments.reshape(group_size, capacity, 2, tile_side, tile_side),
+        ("gx", "gz"),
+        split_axis=0,
+        concat_axis=0,
+        tiled=True,
+    ).astype(jnp.float32).reshape(total_slots, 2, tile_side, tile_side)
+    first_moment = place(got_moments[:, 0])
+    second_moment = place(got_moments[:, 1])
+    factor = 1.0 / math.sqrt(D)
     partial_out = factor * jnp.dot(token_band, weight_band.T, preferred_element_type=jnp.float32)
     outputs = lax.psum_scatter(
         partial_out.astype(jnp.bfloat16), "gz", scatter_dimension=1, tiled=True
     )
-    grad_band = lax.all_gather(grad_out, "gz", axis=1, tiled=True)
+    grad_band = lax.all_gather(grad_out.T, "gz", axis=0, tiled=True).T
     input_grad = lax.psum_scatter(
         (factor * jnp.dot(grad_band, weight_band, preferred_element_type=jnp.float32)).astype(
             jnp.bfloat16

time: 384 us -> 308 us (0.80)
  waiting for transfers between devices: 209 us -> 138 us
  blocking collectives: 47.3 us -> 12.2 us
  local copies, waits for them, and re-layouts: 37.1 us -> 59.6 us
  starting transfers between devices: 22.3 us -> 26.9 us
    reduce_scatter x1 -> x0, waiting for transfers between devices: 60.2 us -> none  [body(): lax.psum_scatter((factor * lax.dot_general(grad_band, token_band, (((0,),...]
    unnamed x6 -> x7, waiting for transfers between devices: 31.3 us -> 67.1 us
    all_to_all x1 -> x0, blocking collectives: 34.7 us -> none  [body(): lax.all_to_all(send_weight.reshape(grid_shape).astype(jnp.bfloat16), ('gx...]
    all_gather x1, waiting for transfers between devices: 76.5 us -> 45.5 us  [body(): weight_band = lax.all_gather(weight_low, 'gy', axis=0, tiled=True)]
    all_to_all x2, waiting for transfers between devices: 41.1 us -> 25.5 us  [the longest x1 25.5 us: body(): lax.all_to_all(send_weight.reshape(grid_shape), ('gx', 'gz'), split_axis=...]
    unnamed x19 -> x20, local copies, waits for them, and re-layouts: 8.79 us -> 22.2 us
    another operation x0 -> x2, other arithmetic: none -> 12.3 us  [body(): jnp.stack([jnp.take(flat_first, source, axis=0) * filled, jnp.take(flat_s...]
    reshape x0 -> x2, local copies, waits for them, and re-layouts: none -> 7.93 us  [the longest x1 4.7 us: body(): send_moments.reshape(group_size, capacity, 2, tile_side, tile_side)]
  transfers between devices with their start and end apart: 8 -> 8, of which waited for: 5 -> 4; matrix products, arithmetic and copies ran while one was open for 20% -> 34% of each run, Pallas kernels for 0% -> 0%
where the time goes in v1:
time: 308 us; the launch traced here: 305 us
  waiting for transfers between devices  138 us (45%)
  local copies, waits for them, and re-layouts  59.6 us (19%)
  other arithmetic  32.5 us (11%)
  starting transfers between devices  26.9 us (9%)
  matrix products  21.9 us (7%)
  between operations  14 us (5%)
  blocking collectives  12.2 us (4%)
    unnamed x7, waiting for transfers between devices  67.1 us
    all_gather x1, waiting for transfers between devices, body(): weight_band = lax.all_gather(weight_low, 'gy', axis=0, tiled=True)  45.5 us
    all_to_all x1, waiting for transfers between devices, body(): lax.all_to_all(send_weight.reshape(grid_shape), ('gx', 'gz'), split_axis=...  25.5 us
    unnamed x20, local copies, waits for them, and re-layouts  22.2 us
    another operation x2, other arithmetic, body(): jnp.stack([jnp.take(flat_first, source, axis=0) * filled, jnp.take(flat_s...  12.3 us
    all_gather x1, blocking collectives, body(): grad_band = lax.all_gather(grad_out.T, 'gz', axis=0, tiled=True).T  12.2 us
    gather x3, local copies, waits for them, and re-layouts, place(): jnp.take(received.reshape(total_slots, tile_side, tile_side), picked, axi...  10.8 us
    all_to_all x1, starting transfers between devices, body(): lax.all_to_all(send_moments.reshape(group_size, capacity, 2, tile_side, t...  10.4 us
  transfers between devices with their start and end apart: 8, of which 4 were waited for; matrix products, arithmetic and copies ran while one was open for 34% of the time, Pallas kernels for 0%

profile of v1, /device:TPU:1, one launch (start us, length us, event | category | flops | bytes accessed | tf_op | source)
XLA Modules:
  0.0 305.2 jit_solution(18281767544763607784)
XLA Ops:
  9.6 8.6 %all-to-all-start.1 = ((s32[32,1,2]{2,1,0:T(1,128)}), s32[32,1,2]{2,1,0:T(1,128)S(1)}, u32[]{:S(2)}, u32[]{:S(2)}) async-start(s32[32,1,2]{2,1,0:T(1,128)} %bitcast.4), calls=%async_computation.1 | async-start | bytes 32768 | tf_op jit(solution)/shard_map/all_to_all | solution.py:58
  26.6 7.6 %fusion.5 = (bf16[64,1,128,128]{3,2,1,0:T(8,128)(2,1)}, bf16[64,1,128,128]{3,2,1,0:T(8,128)(2,1)}, bf16[64,128,128]{2,1,0:T(8,128)(2,1)}) fusion(f32[64,128,128]{2,1,0:T(8,128)} %gather_fusion.1, f32[64]{0:T(128)S(1)} %convert_element_type.46, pred[64]{0:T(512)(128)(4,1)S(1)} %compare_and_fusion.1, f32[64,128,128]{2,1,0:T(8,128)} %gather_fusion.2, ...), kind=kLoop, calls=%fused_computation.20 | loop fusion | flops 9437184 | bytes 18874688 | tf_op jit(solution)/shard_map/stack | solution.py:80
  34.3 7.6 %all-to-all-start = ((bf16[32,2,128,128]{3,2,1,0:T(8,128)(2,1)}), bf16[32,2,128,128]{3,2,1,0:T(8,128)(2,1)}, u32[]{:S(2)}, u32[]{:S(2)}) async-start(bf16[32,2,128,128]{3,2,1,0:T(8,128)(2,1)} %bitcast.65), calls=%async_computation | async-start | bytes 4194304 | tf_op jit(solution)/shard_map/all_to_all | solution.py:61
  43.5 25.5 %all-to-all-done = bf16[32,2,128,128]{3,2,1,0:T(8,128)(2,1)} async-done(((bf16[32,2,128,128]{3,2,1,0:T(8,128)(2,1)}), bf16[32,2,128,128]{3,2,1,0:T(8,128)(2,1)}, u32[]{:S(2)}, u32[]{:S(2)}) %all-to-all-start) | async-done | bytes 2097184 | tf_op jit(solution)/shard_map/all_to_all | solution.py:61
  69.0 4.1 %bitcast_convert_fusion = f32[64,128,128]{2,1,0:T(8,128)} fusion(bf16[32,2,128,128]{3,2,1,0:T(8,128)(2,1)} %all-to-all-done), kind=kLoop, calls=%fused_computation.22 | loop fusion | flops 1048576 | bytes 6291456 | tf_op jit(solution)/shard_map/reshape | solution.py:73
  77.6 12.2 %all_gather.11 = bf16[1024,384]{0,1:T(8,128)(2,1)S(1)} all-gather(bf16[256,384]{0,1:T(8,128)(2,1)S(1)} %bitcast.66), channel_id=1, replica_groups=mesh['gx'=8,'gy'=8,'gz'=4] {'gz'}, dimensions={0}, use_global_device_ids=true | all-gather | bytes 983040 | tf_op jit(solution)/shard_map/all_gather | solution.py:99
  89.7 7.2 %fusion = bf16[1024,3072]{0,1:T(8,128)(2,1)} fusion(bf16[384,3072]{1,0:T(8,128)(2,1)} %all-gather.3.cloned.1.call-done, bf16[1024,384]{0,1:T(8,128)(2,1)S(1)} %all_gather.11), kind=kOutput, calls=%fused_computation.7 | convolution fusion | flops 2422210560 | bytes 9437184 | tf_op jit(solution)/shard_map/dot_general | solution.py:111
  96.9 8.6 %copy.53 = bf16[1024,3072]{1,0:T(8,128)(2,1)} copy(bf16[1024,3072]{0,1:T(8,128)(2,1)} %fusion) | data formatting | bytes 12582912
  105.6 4.7 %pad_maximum_fusion = bf16[64,2,128,128]{3,2,1,0:T(8,128)(2,1)} fusion(bf16[64,1,128,128]{3,2,1,0:T(8,128)(2,1)} %get-tuple-element.49, bf16[64,1,128,128]{3,2,1,0:T(8,128)(2,1)} %get-tuple-element.48), kind=kLoop, calls=%fused_computation.11 | loop fusion | flops 2097152 | bytes 8388608 | tf_op jit(solution)/shard_map/stack | solution.py:80
  110.3 45.5 %all-gather.5.cloned.1.call-done = bf16[1024,3072]{0,1:T(8,128)(2,1)} async-done(((bf16[128,3072]{0,1:T(8,128)(2,1)}), bf16[1024,3072]{0,1:T(8,128)(2,1)}) %all-gather.5.cloned.1.call-update) | async-done | bytes 6291472 | tf_op jit(solution)/shard_map/all_gather | solution.py:79
  155.8 7.0 %multiply_convert_fusion.2 = bf16[384,1024]{1,0:T(8,128)(2,1)} fusion(bf16[384,3072]{1,0:T(8,128)(2,1)} %all-gather.3.cloned.1.call-done, bf16[1024,3072]{0,1:T(8,128)(2,1)} %all-gather.5.cloned.1.call-done), kind=kOutput, calls=%fused_computation.37 | convolution fusion | flops 2416705536 | bytes 9437184 | tf_op jit(solution)/shard_map/dot_general | solution.py:95
  162.8 4.7 %copy.43 = bf16[32,2,2,128,128]{4,3,1,2,0:T(8,128)(2,1)} copy(bf16[32,2,2,128,128]{4,3,2,1,0:T(8,128)(2,1)} %bitcast.64) | data formatting | bytes 8388608 | tf_op jit(solution)/shard_map/reshape | solution.py:86
  167.5 10.4 %all-to-all-start.2 = ((bf16[32,2,2,128,128]{4,3,1,2,0:T(8,128)(2,1)}), bf16[32,2,2,128,128]{4,3,1,2,0:T(8,128)(2,1)}, u32[]{:S(2)}, u32[]{:S(2)}) async-start(bf16[32,2,2,128,128]{4,3,1,2,0:T(8,128)(2,1)} %copy.43), calls=%async_computation.3 | async-start | bytes 8388608 | tf_op jit(solution)/shard_map/all_to_all | solution.py:85
  178.1 7.8 %fusion.4 = bf16[384,3072]{0,1:T(8,128)(2,1)} fusion(bf16[1024,3072]{0,1:T(8,128)(2,1)} %all-gather.5.cloned.1.call-done, bf16[1024,384]{0,1:T(8,128)(2,1)S(1)} %all_gather.11), kind=kOutput, calls=%fused_computation.18 | convolution fusion | flops 2418278400 | bytes 9437184 | tf_op jit(solution)/shard_map/dot_general | solution.py:101
  185.9 4.3 %copy.51 = bf16[384,3072]{1,0:T(8,128)(2,1)} copy(bf16[384,3072]{0,1:T(8,128)(2,1)} %fusion.4) | data formatting | bytes 4718592
  190.9 43.6 %reduce-scatter.12.cloned.1.call-done = bf16[128,3072]{1,0:T(8,128)(2,1)} async-done(((bf16[1024,3072]{1,0:T(8,128)(2,1)}), bf16[128,3072]{1,0:T(8,128)(2,1)}) %reduce-scatter.12.cloned.1.call-update) | async-done | bytes 786448
  236.8 3.2 %copy.44 = f32[32,2,2,128,128]{4,3,1,0,2:T(8,128)S(1)} copy(bf16[32,2,2,128,128]{4,3,1,2,0:T(8,128)(2,1)} %all-to-all-done.2) | data formatting | bytes 12582912 | tf_op jit(solution)/shard_map/reshape | solution.py:91
  240.0 3.8 %slice_bitcast_fusion = (f32[64,128,128]{2,1,0:T(8,128)}, f32[64,128,128]{2,1,0:T(8,128)}) fusion(f32[64,2,128,128]{3,2,0,1:T(8,128)S(1)} %bitcast.63), kind=kLoop, calls=%fused_computation.9 | loop fusion | bytes 16777216 | tf_op jit(solution)/shard_map/squeeze | solution.py:93
  243.8 4.0 %gather_fusion.5 = f32[24,128,128]{2,1,0:T(8,128)} fusion(f32[64,128,128]{2,1,0:T(8,128)} %get-tuple-element.46, s32[1024]{0:T(1024)S(1)} %pad_clamp_fusion), kind=kCustom, calls=%fused_computation.5.clone | custom fusion | bytes 3145824 | tf_op jit(solution)/shard_map/jit(_take)/gather | solution.py:73
  247.8 4.0 %gather_fusion.4 = f32[24,128,128]{2,1,0:T(8,128)} fusion(f32[64,128,128]{2,1,0:T(8,128)} %get-tuple-element.47, s32[1024]{0:T(1024)S(1)} %pad_clamp_fusion), kind=kCustom, calls=%fused_computation.4.clone | custom fusion | bytes 3145824 | tf_op jit(solution)/shard_map/jit(_take)/gather | solution.py:73
  251.8 3.6 %fusion.11 = (f32[1,128,24,128]{3,1,2,0:T(8,128)S(1)}, f32[1,128,24,128]{3,1,2,0:T(8,128)}) fusion(f32[24,128,128]{2,1,0:T(8,128)} %gather_fusion.5, pred[24]{0:T(512)(128)(4,1)S(1)} %compare_and_fusion, f32[24,128,128]{2,1,0:T(8,128)} %gather_fusion.4), kind=kLoop, calls=%fused_computation.32 | loop fusion | flops 1572864 | bytes 6291480 | tf_op jit(solution)/shard_map/mul | solution.py:120
  260.1 9.5 %multiply_add_fusion = (f32[128,3072]{0,1:T(8,128)}, f32[128,3072]{0,1:T(8,128)}, f32[128,3072]{0,1:T(8,128)S(1)}) fusion(f32[1,128,24,128]{1,3,2,0:T(8,128)S(1)} %copy.42, s32[3072]{0:T(1024)S(1)} %get-tuple-element.55, s32[3072]{0:T(1024)S(1)} %get-tuple-element.56, s32[128]{0:T(128)S(1)} %get-tuple-element.57, s32[128]{0:T(128)S(1)} %get-tuple-element.58, ...), kind=kLoop, calls=%fused_computation.36 | loop fusion | flops 15335424 | bytes 10264704 | tf_op jit(solution)/shard_map/add | solution.py:130
  269.6 3.1 %copy.48 = f32[128,3072]{1,0:T(8,128)} copy(f32[128,3072]{0,1:T(8,128)} %get-tuple-element.43) | data formatting | bytes 3145728
  276.0 22.7 %reduce-scatter.10.cloned.1.call-done = bf16[48,3072]{1,0:T(8,128)(2,1)} async-done(((bf16[384,3072]{1,0:T(8,128)(2,1)}), bf16[48,3072]{1,0:T(8,128)(2,1)}) %reduce-scatter.10.cloned.1.call-update) | async-done | bytes 294928
  (62 shorter events, 28.0 us)
Async XLA Ops:
  7.2 11.1 %copy-start = (f32[24,128,128]{2,1,0:T(8,128)S(1)}, f32[24,128,128]{2,1,0:T(8,128)}, u32[]{:S(2)}) copy-start(f32[24,128,128]{2,1,0:T(8,128)} %param.12) | copy-start | bytes 4718596
  7.2 61.8 %all-gather.3.cloned.1.call-start = ((), (), s32[]{:S(2)}) async-start(), calls=%async_computation.6 | async-start | bytes 2654208 | tf_op jit(solution)/shard_map/all_gather | solution.py:64
  9.6 24.7 %all-to-all-start.1 = ((s32[32,1,2]{2,1,0:T(1,128)}), s32[32,1,2]{2,1,0:T(1,128)S(1)}, u32[]{:S(2)}, u32[]{:S(2)}) async-start(s32[32,1,2]{2,1,0:T(1,128)} %bitcast.4), calls=%async_computation.1 | async-start | bytes 32768 | tf_op jit(solution)/shard_map/all_to_all | solution.py:58
  18.2 2.8 copy-start.2
  21.0 2.8 copy-start.3
  34.3 34.7 %all-to-all-start = ((bf16[32,2,128,128]{3,2,1,0:T(8,128)(2,1)}), bf16[32,2,128,128]{3,2,1,0:T(8,128)(2,1)}, u32[]{:S(2)}, u32[]{:S(2)}) async-start(bf16[32,2,128,128]{3,2,1,0:T(8,128)(2,1)} %bitcast.65), calls=%async_computation | async-start | bytes 4194304 | tf_op jit(solution)/shard_map/all_to_all | solution.py:61
  41.9 113.9 %all-gather.5.cloned.1.call-start = ((), (), s32[]{:S(2)}) async-start(), calls=%async_computation.7 | async-start | bytes 7077888 | tf_op jit(solution)/shard_map/all_gather | solution.py:79
  76.5 1.0 copy-start.5
  77.5 157.0 %reduce-scatter.12.cloned.1.call-start = ((), (), s32[]{:S(2)}) async-start(), calls=%async_computation.10 | async-start | bytes 7077888
  105.6 170.4 %reduce-scatter.8.cloned.1.call-start = ((), (), s32[]{:S(2)}) async-start(), calls=%async_computation.8 | async-start | bytes 983040 | tf_op jit(solution)/shard_map/reduce_scatter | solution.py:96
  167.5 69.3 %all-to-all-start.2 = ((bf16[32,2,2,128,128]{4,3,1,2,0:T(8,128)(2,1)}), bf16[32,2,2,128,128]{4,3,1,2,0:T(8,128)(2,1)}, u32[]{:S(2)}, u32[]{:S(2)}) async-start(bf16[32,2,2,128,128]{4,3,1,2,0:T(8,128)(2,1)} %copy.43), calls=%async_computation.3 | async-start | bytes 8388608 | tf_op jit(solution)/shard_map/all_to_all | solution.py:85
  177.9 120.8 %reduce-scatter.10.cloned.1.call-start = ((), (), s32[]{:S(2)}) async-start(), calls=%async_computation.9 | async-start | bytes 2654208
  190.2 0.7 copy-start.6
  269.6 3.1 %copy-start.4 = (f32[128,3072]{0,1:T(8,128)S(1)}, f32[128,3072]{0,1:T(8,128)}, u32[]{:S(2)}) copy-start(f32[128,3072]{0,1:T(8,128)} %get-tuple-element.44) | copy-start | bytes 4718596
  274.3 24.4 %copy-start.1 = (f32[24,128,128]{2,1,0:T(8,128)S(1)}, f32[24,128,128]{2,1,0:T(8,128)}, u32[]{:S(2)}) copy-start(f32[24,128,128]{2,1,0:T(8,128)} %param.12) | copy-start | bytes 4718596
Sparse Core Ops, SparseCore 0:
  9.8 32.2 all-gather.2
  77.6 78.1 all-gather.4
  158.4 76.0 reduce-scatter.11
  237.5 21.7 reduce-scatter.7
  262.2 36.4 reduce-scatter.9

commit v2 on v1

--- a/solution.py
+++ b/solution.py
@@ -76,19 +76,21 @@
 
     weight = place(got_weight)
     weight_low = weight.astype(jnp.bfloat16)
-    weight_band = lax.all_gather(weight_low, "gy", axis=0, tiled=True)
     send_moments = jnp.stack(
         [jnp.take(flat_first, source, axis=0) * filled, jnp.take(flat_second, source, axis=0) * filled],
         axis=1,
     ).astype(jnp.bfloat16)
-    send_moments, weight_band = lax.optimization_barrier((send_moments, weight_band))
+    send_moments, weight_low = lax.optimization_barrier((send_moments, weight_low))
     got_moments = lax.all_to_all(
         send_moments.reshape(group_size, capacity, 2, tile_side, tile_side),
         ("gx", "gz"),
         split_axis=0,
         concat_axis=0,
         tiled=True,
-    ).astype(jnp.float32).reshape(total_slots, 2, tile_side, tile_side)
+    )
+    weight_band = lax.all_gather(weight_low, "gy", axis=0, tiled=True)
+    got_moments, weight_band = lax.optimization_barrier((got_moments, weight_band))
+    got_moments = got_moments.astype(jnp.float32).reshape(total_slots, 2, tile_side, tile_side)
     first_moment = place(got_moments[:, 0])
     second_moment = place(got_moments[:, 1])
     factor = 1.0 / math.sqrt(D)

time: 308 us -> 308 us (level)
  blocking collectives: 12.2 us -> 70.2 us
  waiting for transfers between devices: 138 us -> 94.1 us
  starting transfers between devices: 26.9 us -> 16.6 us
    all_to_all x0 -> x1, blocking collectives: none -> 58 us  [body(): lax.all_to_all(send_moments.reshape(group_size, capacity, 2, tile_side, t...]
    all_gather x1, waiting for transfers between devices: 45.5 us -> 0.01 us  [body(): weight_band = lax.all_gather(weight_low, 'gy', axis=0, tiled=True)]
    all_to_all x1 -> x0, starting transfers between devices: 10.4 us -> none  [body(): lax.all_to_all(send_moments.reshape(group_size, capacity, 2, tile_side, t...]
    reduce_scatter x1, waiting for transfers between devices: 0.01 us -> 8.5 us  [body(): lax.psum_scatter(partial_out.astype(jnp.bfloat16), 'gz', scatter_dimensio...]
    all_to_all x1, waiting for transfers between devices: 25.5 us -> 20.8 us  [body(): lax.all_to_all(send_weight.reshape(grid_shape), ('gx', 'gz'), split_axis=...]
    unnamed x20 -> x24, local copies, waits for them, and re-layouts: 22.2 us -> 22.2 us
  transfers between devices with their start and end apart: 8 -> 7, of which waited for: 4 -> 4; matrix products, arithmetic and copies ran while one was open for 34% -> 33% of each run, Pallas kernels for 0% -> 0%
where the time goes in v2:
time: 308 us; the launch traced here: 305 us
  waiting for transfers between devices  94.1 us (31%)
  blocking collectives  70.2 us (23%)
  local copies, waits for them, and re-layouts  57.8 us (19%)
  other arithmetic  30.6 us (10%)
  matrix products  21.9 us (7%)
  starting transfers between devices  16.6 us (5%)
  between operations  14 us (5%)
    unnamed x7, waiting for transfers between devices  64.8 us
    all_to_all x1, blocking collectives, body(): lax.all_to_all(send_moments.reshape(group_size, capacity, 2, tile_side, t...  58 us
    unnamed x24, local copies, waits for them, and re-layouts  22.2 us
    all_to_all x1, waiting for transfers between devices, body(): lax.all_to_all(send_weight.reshape(grid_shape), ('gx', 'gz'), split_axis=...  20.8 us
    another operation x2, other arithmetic, body(): jnp.stack([jnp.take(flat_first, source, axis=0) * filled, jnp.take(flat_s...  12.4 us
    all_gather x1, blocking collectives, body(): grad_band = lax.all_gather(grad_out.T, 'gz', axis=0, tiled=True).T  12.2 us
    gather x3, local copies, waits for them, and re-layouts, place(): jnp.take(received.reshape(total_slots, tile_side, tile_side), picked, axi...  10.9 us
    all_to_all x1, starting transfers between devices, body(): lax.all_to_all(labels.reshape(group_size, capacity), ('gx', 'gz'), split_...  8.58 us
  transfers between devices with their start and end apart: 7, of which 4 were waited for; matrix products, arithmetic and copies ran while one was open for 33% of the time, Pallas kernels for 0%

profile of v2, /device:TPU:1, one launch (start us, length us, event | category | flops | bytes accessed | tf_op | source)
XLA Modules:
  0.0 305.2 jit_solution(2563999287490013612)
XLA Ops:
  9.6 8.6 %all-to-all-start.1 = ((s32[32,1,2]{2,1,0:T(1,128)}), s32[32,1,2]{2,1,0:T(1,128)S(1)}, u32[]{:S(2)}, u32[]{:S(2)}) async-start(s32[32,1,2]{2,1,0:T(1,128)} %bitcast.4), calls=%async_computation.1 | async-start | bytes 32768 | tf_op jit(solution)/shard_map/all_to_all | solution.py:58
  26.6 7.7 %fusion.5 = (bf16[64,1,128,128]{3,2,1,0:T(8,128)(2,1)}, bf16[64,1,128,128]{3,2,1,0:T(8,128)(2,1)}, bf16[64,128,128]{2,1,0:T(8,128)(2,1)}) fusion(f32[64,128,128]{2,1,0:T(8,128)} %gather_fusion.1, f32[64]{0:T(128)S(1)} %convert_element_type.46, pred[64]{0:T(512)(128)(4,1)S(1)} %compare_and_fusion.1, f32[64,128,128]{2,1,0:T(8,128)} %gather_fusion.2, ...), kind=kLoop, calls=%fused_computation.20 | loop fusion | flops 9437184 | bytes 18874688 | tf_op jit(solution)/shard_map/stack | solution.py:79
  34.3 7.6 %all-to-all-start = ((bf16[32,2,128,128]{3,2,1,0:T(8,128)(2,1)}), bf16[32,2,128,128]{3,2,1,0:T(8,128)(2,1)}, u32[]{:S(2)}, u32[]{:S(2)}) async-start(bf16[32,2,128,128]{3,2,1,0:T(8,128)(2,1)} %bitcast.65), calls=%async_computation | async-start | bytes 4194304 | tf_op jit(solution)/shard_map/all_to_all | solution.py:61
  42.0 4.7 %pad_maximum_fusion = bf16[64,2,128,128]{3,2,1,0:T(8,128)(2,1)} fusion(bf16[64,1,128,128]{3,2,1,0:T(8,128)(2,1)} %get-tuple-element.53, bf16[64,1,128,128]{3,2,1,0:T(8,128)(2,1)} %get-tuple-element.52), kind=kLoop, calls=%fused_computation.11 | loop fusion | flops 2097152 | bytes 8388608 | tf_op jit(solution)/shard_map/stack | solution.py:79
  48.2 20.8 %all-to-all-done = bf16[32,2,128,128]{3,2,1,0:T(8,128)(2,1)} async-done(((bf16[32,2,128,128]{3,2,1,0:T(8,128)(2,1)}), bf16[32,2,128,128]{3,2,1,0:T(8,128)(2,1)}, u32[]{:S(2)}, u32[]{:S(2)}) %all-to-all-start) | async-done | bytes 2097184 | tf_op jit(solution)/shard_map/all_to_all | solution.py:61
  69.0 4.1 %bitcast_convert_fusion = f32[64,128,128]{2,1,0:T(8,128)} fusion(bf16[32,2,128,128]{3,2,1,0:T(8,128)(2,1)} %all-to-all-done), kind=kLoop, calls=%fused_computation.22 | loop fusion | flops 1048576 | bytes 6291456 | tf_op jit(solution)/shard_map/reshape | solution.py:73
  77.6 12.2 %all_gather.11 = bf16[1024,384]{0,1:T(8,128)(2,1)S(1)} all-gather(bf16[256,384]{0,1:T(8,128)(2,1)S(1)} %bitcast.66), channel_id=1, replica_groups=mesh['gx'=8,'gy'=8,'gz'=4] {'gz'}, dimensions={0}, use_global_device_ids=true | all-gather | bytes 983040 | tf_op jit(solution)/shard_map/all_gather | solution.py:101
  89.8 7.2 %fusion = bf16[1024,3072]{0,1:T(8,128)(2,1)} fusion(bf16[384,3072]{1,0:T(8,128)(2,1)} %all-gather.3.cloned.1.call-done, bf16[1024,384]{0,1:T(8,128)(2,1)S(1)} %all_gather.11), kind=kOutput, calls=%fused_computation.7 | convolution fusion | flops 2422210560 | bytes 9437184 | tf_op jit(solution)/shard_map/dot_general | solution.py:113
  96.9 8.6 %copy.53 = bf16[1024,3072]{1,0:T(8,128)(2,1)} copy(bf16[1024,3072]{0,1:T(8,128)(2,1)} %fusion) | data formatting | bytes 12582912
  108.2 58.0 %all_to_all.19 = bf16[32,2,2,128,128]{4,3,1,2,0:T(8,128)(2,1)} all-to-all(bf16[32,2,2,128,128]{4,3,1,2,0:T(8,128)(2,1)S(1)} %copy.43), channel_id=1, replica_groups=mesh['gx'=8,'gy'=8,'gz'=4] {'gx','gz'}, dimensions={0} | all-to-all | bytes 8388608 | tf_op jit(solution)/shard_map/all_to_all | solution.py:84
  166.2 7.1 %multiply_convert_fusion.2 = bf16[384,1024]{1,0:T(8,128)(2,1)} fusion(bf16[384,3072]{1,0:T(8,128)(2,1)} %all-gather.3.cloned.1.call-done, bf16[1024,3072]{0,1:T(8,128)(2,1)} %all-gather.5.cloned.1.call-done), kind=kOutput, calls=%fused_computation.37 | convolution fusion | flops 2416705536 | bytes 9437184 | tf_op jit(solution)/shard_map/dot_general | solution.py:97
  173.6 7.7 %fusion.4 = bf16[384,3072]{0,1:T(8,128)(2,1)} fusion(bf16[1024,3072]{0,1:T(8,128)(2,1)} %all-gather.5.cloned.1.call-done, bf16[1024,384]{0,1:T(8,128)(2,1)S(1)} %all_gather.11), kind=kOutput, calls=%fused_computation.18 | convolution fusion | flops 2418278400 | bytes 9437184 | tf_op jit(solution)/shard_map/dot_general | solution.py:103
  181.3 4.3 %copy.51 = bf16[384,3072]{1,0:T(8,128)(2,1)} copy(bf16[384,3072]{0,1:T(8,128)(2,1)} %fusion.4) | data formatting | bytes 4718592
  186.3 3.2 %copy.44 = f32[32,2,2,128,128]{4,3,1,0,2:T(8,128)S(1)} copy(bf16[32,2,2,128,128]{4,3,1,2,0:T(8,128)(2,1)} %all_to_all.19) | data formatting | bytes 12582912 | tf_op jit(solution)/shard_map/reshape | solution.py:93
  189.5 4.0 %slice_bitcast_fusion = (f32[64,128,128]{2,1,0:T(8,128)}, f32[64,128,128]{2,1,0:T(8,128)}) fusion(f32[64,2,128,128]{3,2,0,1:T(8,128)S(1)} %bitcast.63), kind=kLoop, calls=%fused_computation.9 | loop fusion | bytes 16777216 | tf_op jit(solution)/shard_map/squeeze | solution.py:95
  193.5 4.0 %gather_fusion.5 = f32[24,128,128]{2,1,0:T(8,128)} fusion(f32[64,128,128]{2,1,0:T(8,128)} %get-tuple-element.50, s32[1024]{0:T(1024)S(1)} %pad_clamp_fusion), kind=kCustom, calls=%fused_computation.5.clone | custom fusion | bytes 3145824 | tf_op jit(solution)/shard_map/jit(_take)/gather | solution.py:73
  197.6 4.0 %gather_fusion.4 = f32[24,128,128]{2,1,0:T(8,128)} fusion(f32[64,128,128]{2,1,0:T(8,128)} %get-tuple-element.51, s32[1024]{0:T(1024)S(1)} %pad_clamp_fusion), kind=kCustom, calls=%fused_computation.4.clone | custom fusion | bytes 3145824 | tf_op jit(solution)/shard_map/jit(_take)/gather | solution.py:73
  201.6 3.6 %fusion.11 = (f32[1,128,24,128]{3,1,2,0:T(8,128)S(1)}, f32[1,128,24,128]{3,1,2,0:T(8,128)}) fusion(f32[24,128,128]{2,1,0:T(8,128)} %gather_fusion.5, pred[24]{0:T(512)(128)(4,1)S(1)} %compare_and_fusion, f32[24,128,128]{2,1,0:T(8,128)} %gather_fusion.4), kind=kLoop, calls=%fused_computation.32 | loop fusion | flops 1572864 | bytes 6291480 | tf_op jit(solution)/shard_map/mul | solution.py:122
  205.3 3.0 copy.45
  209.9 24.6 %reduce-scatter.12.cloned.1.call-done = bf16[128,3072]{1,0:T(8,128)(2,1)} async-done(((bf16[1024,3072]{1,0:T(8,128)(2,1)}), bf16[128,3072]{1,0:T(8,128)(2,1)}) %reduce-scatter.12.cloned.1.call-update) | async-done | bytes 786448
  236.8 7.6 %multiply_add_fusion = (f32[128,3072]{0,1:T(8,128)}, f32[128,3072]{0,1:T(8,128)}, f32[128,3072]{0,1:T(8,128)}) fusion(f32[1,128,24,128]{1,3,2,0:T(8,128)S(1)} %copy.42, s32[3072]{0:T(1024)S(1)} %get-tuple-element.59, s32[3072]{0:T(1024)S(1)} %get-tuple-element.60, s32[128]{0:T(128)S(1)} %get-tuple-element.61, s32[128]{0:T(128)S(1)} %get-tuple-element.62, ...), kind=kLoop, calls=%fused_computation.36 | loop fusion | flops 15335424 | bytes 10264704 | tf_op jit(solution)/shard_map/add | solution.py:132
  244.4 3.1 %copy.48 = f32[128,3072]{1,0:T(8,128)} copy(f32[128,3072]{0,1:T(8,128)} %get-tuple-element.47) | data formatting | bytes 3145728
  250.8 8.5 %reduce-scatter.8.cloned.1.call-done = bf16[384,256]{1,0:T(8,128)(2,1)} async-done(((bf16[384,1024]{1,0:T(8,128)(2,1)}), bf16[384,256]{1,0:T(8,128)(2,1)}) %reduce-scatter.8.cloned.1.call-update) | async-done | bytes 196624 | tf_op jit(solution)/shard_map/reduce_scatter | solution.py:98
  259.3 39.4 %reduce-scatter.10.cloned.1.call-done = bf16[48,3072]{1,0:T(8,128)(2,1)} async-done(((bf16[384,3072]{1,0:T(8,128)(2,1)}), bf16[48,3072]{1,0:T(8,128)(2,1)}) %reduce-scatter.10.cloned.1.call-update) | async-done | bytes 294928
  (65 shorter events, 27.5 us)
Async XLA Ops:
  7.2 11.1 %copy-start = (f32[24,128,128]{2,1,0:T(8,128)S(1)}, f32[24,128,128]{2,1,0:T(8,128)}, u32[]{:S(2)}) copy-start(f32[24,128,128]{2,1,0:T(8,128)} %param.12) | copy-start | bytes 4718596
  7.2 61.8 %all-gather.3.cloned.1.call-start = ((), (), s32[]{:S(2)}) async-start(), calls=%async_computation.6 | async-start | bytes 2654208 | tf_op jit(solution)/shard_map/all_gather | solution.py:64
  9.6 24.7 %all-to-all-start.1 = ((s32[32,1,2]{2,1,0:T(1,128)}), s32[32,1,2]{2,1,0:T(1,128)S(1)}, u32[]{:S(2)}, u32[]{:S(2)}) async-start(s32[32,1,2]{2,1,0:T(1,128)} %bitcast.4), calls=%async_computation.1 | async-start | bytes 32768 | tf_op jit(solution)/shard_map/all_to_all | solution.py:58
  18.2 2.8 copy-start.2
  21.0 2.8 copy-start.3
  34.3 34.7 %all-to-all-start = ((bf16[32,2,128,128]{3,2,1,0:T(8,128)(2,1)}), bf16[32,2,128,128]{3,2,1,0:T(8,128)(2,1)}, u32[]{:S(2)}, u32[]{:S(2)}) async-start(bf16[32,2,128,128]{3,2,1,0:T(8,128)(2,1)} %bitcast.65), calls=%async_computation | async-start | bytes 4194304 | tf_op jit(solution)/shard_map/all_to_all | solution.py:61
  41.9 124.3 %all-gather.5.cloned.1.call-start = ((), (), s32[]{:S(2)}) async-start(), calls=%async_computation.7 | async-start | bytes 7077888 | tf_op jit(solution)/shard_map/all_gather | solution.py:91
  76.6 1.0 copy-start.7
  77.6 157.0 %reduce-scatter.12.cloned.1.call-start = ((), (), s32[]{:S(2)}) async-start(), calls=%async_computation.10 | async-start | bytes 7077888
  105.6 153.7 %reduce-scatter.8.cloned.1.call-start = ((), (), s32[]{:S(2)}) async-start(), calls=%async_computation.8 | async-start | bytes 983040 | tf_op jit(solution)/shard_map/reduce_scatter | solution.py:98
  173.4 125.3 %reduce-scatter.10.cloned.1.call-start = ((), (), s32[]{:S(2)}) async-start(), calls=%async_computation.9 | async-start | bytes 2654208
  185.5 0.7 copy-start.8
  209.9 26.9 %copy-start.4 = (f32[1,128,24,128]{1,3,2,0:T(8,128)S(1)}, f32[1,128,24,128]{1,3,2,0:T(8,128)}, u32[]{:S(2)}) copy-start(f32[1,128,24,128]{1,3,2,0:T(8,128)} %copy.45) | copy-start | bytes 4718596
  244.4 3.1 %copy-start.6 = (f32[128,3072]{0,1:T(8,128)S(1)}, f32[128,3072]{0,1:T(8,128)}, u32[]{:S(2)}) copy-start(f32[128,3072]{0,1:T(8,128)} %get-tuple-element.48) | copy-start | bytes 4718596
  247.5 1.6 copy-start.5
  249.1 49.5 %copy-start.1 = (f32[24,128,128]{2,1,0:T(8,128)S(1)}, f32[24,128,128]{2,1,0:T(8,128)}, u32[]{:S(2)}) copy-start(f32[24,128,128]{2,1,0:T(8,128)} %param.12) | copy-start | bytes 4718596
Sparse Core Ops, SparseCore 0:
  9.8 32.2 all-gather.2
  77.7 78.1 all-gather.4
  158.4 76.0 reduce-scatter.11
  237.5 21.6 reduce-scatter.7
  262.3 36.3 reduce-scatter.9

commit v3 on v2

--- a/solution.py
+++ b/solution.py
@@ -62,7 +62,8 @@
         send_weight.reshape(grid_shape), ("gx", "gz"), split_axis=0, concat_axis=0, tiled=True
     )
     token_band = lax.all_gather(tokens, "gx", axis=0, tiled=True)
-    got_weight, token_band = lax.optimization_barrier((got_weight, token_band))
+    grad_band = lax.all_gather(grad_out.T, "gz", axis=0, tiled=True)
+    got_weight, token_band, grad_band = lax.optimization_barrier((got_weight, token_band, grad_band))
     got_weight = got_weight.astype(jnp.float32)
     got_labels = got_labels.reshape(total_slots)
     wanted = jnp.arange(1, tiles_own + 1, dtype=jnp.int32)
@@ -98,22 +99,24 @@
     outputs = lax.psum_scatter(
         partial_out.astype(jnp.bfloat16), "gz", scatter_dimension=1, tiled=True
     )
-    grad_band = lax.all_gather(grad_out.T, "gz", axis=0, tiled=True).T
-    input_grad = lax.psum_scatter(
-        (factor * jnp.dot(grad_band, weight_band, preferred_element_type=jnp.float32)).astype(
+    input_part = (
+        factor
+        * lax.dot_general(
+            grad_band, weight_band, (((0,), (0,)), ((), ())), preferred_element_type=jnp.float32
+        )
+    ).astype(jnp.bfloat16)
+    input_parts = lax.all_to_all(
+        input_part.reshape(size_gx, input_part.shape[0] // size_gx, input_part.shape[1]),
+        "gx",
+        split_axis=0,
+        concat_axis=0,
+        tiled=True,
+    )
+    input_grad = jnp.sum(input_parts.astype(jnp.float32), axis=0).astype(jnp.bfloat16)
+    gradient = lax.psum_scatter(
+        (factor * jnp.dot(grad_band, token_band, preferred_element_type=jnp.float32)).astype(
             jnp.bfloat16
         ),
-        "gx",
-        scatter_dimension=0,
-        tiled=True,
-    )
-    gradient = lax.psum_scatter(
-        (
-            factor
-            * lax.dot_general(
-                grad_band, token_band, (((0,), (0,)), ((), ())), preferred_element_type=jnp.float32
-            )
-        ).astype(jnp.bfloat16),
         "gy",
         scatter_dimension=0,
         tiled=True,

time: 308 us -> 274 us (0.89)
  blocking collectives: 70.2 us -> 30.8 us
  starting transfers between devices: 16.6 us -> 28.4 us
  local copies, waits for them, and re-layouts: 57.8 us -> 46.2 us
  waiting for transfers between devices: 94.1 us -> 102 us
    unnamed x7 -> x4, waiting for transfers between devices: 64.8 us -> 0.73 us
    all_to_all x1 -> x0, blocking collectives: 58 us -> none  [body(): lax.all_to_all(send_moments.reshape(group_size, capacity, 2, tile_side, t...]
    all_to_all x0 -> x2, waiting for transfers between devices: none -> 50.4 us  [the longest x1 50.4 us: body(): lax.all_to_all(send_moments.reshape(group_size, capacity, 2, tile_side, t...]
    reduce_scatter x0 -> x1, waiting for transfers between devices: none -> 27.8 us  [body(): lax.psum_scatter((factor * jnp.dot(grad_band, token_band, preferred_eleme...]
    unnamed x24 -> x15, local copies, waits for them, and re-layouts: 22.2 us -> 1.23 us
    all_to_all x1, waiting for transfers between devices: 20.8 us -> 0.01 us  [body(): lax.all_to_all(send_weight.reshape(grid_shape), ('gx', 'gz'), split_axis=...]
    all_gather x1, blocking collectives: 12.2 us -> 30.8 us  [body(): grad_band = lax.all_gather(grad_out.T, 'gz', axis=0, tiled=True)]
    all_to_all x0 -> x2, starting transfers between devices: none -> 12.1 us  [the longest x1 7.01 us: body(): lax.all_to_all(send_moments.reshape(group_size, capacity, 2, tile_side, t...]
  transfers between devices with their start and end apart: 7 -> 8, of which waited for: 4 -> 4; matrix products, arithmetic and copies ran while one was open for 33% -> 32% of each run, Pallas kernels for 0% -> 0%
where the time goes in v3:
time: 274 us; the launch traced here: 272 us
  waiting for transfers between devices  102 us (37%)
  local copies, waits for them, and re-layouts  46.2 us (17%)
  blocking collectives  30.8 us (11%)
  other arithmetic  29.3 us (11%)
  starting transfers between devices  28.4 us (10%)
  matrix products  21.4 us (8%)
  between operations  14 us (5%)
    all_to_all x1, waiting for transfers between devices, body(): lax.all_to_all(send_moments.reshape(group_size, capacity, 2, tile_side, t...  50.4 us
    all_gather x1, blocking collectives, body(): grad_band = lax.all_gather(grad_out.T, 'gz', axis=0, tiled=True)  30.8 us
    reduce_scatter x1, waiting for transfers between devices, body(): lax.psum_scatter((factor * jnp.dot(grad_band, token_band, preferred_eleme...  27.8 us
    reduce_scatter x1, waiting for transfers between devices, body(): lax.psum_scatter(partial_out.astype(jnp.bfloat16), 'gz', scatter_dimensio...  16.3 us
    another operation x2, other arithmetic, body(): jnp.stack([jnp.take(flat_first, source, axis=0) * filled, jnp.take(flat_s...  12.3 us
    gather x3, local copies, waits for them, and re-layouts, place(): jnp.take(received.reshape(total_slots, tile_side, tile_side), picked, axi...  10.9 us
    all_to_all x1, starting transfers between devices, body(): lax.all_to_all(labels.reshape(group_size, capacity), ('gx', 'gz'), split_...  8.58 us
    squeeze x1, local copies, waits for them, and re-layouts, body(): second_moment = place(got_moments[:, 1])  8.01 us
  transfers between devices with their start and end apart: 8, of which 4 were waited for; matrix products, arithmetic and copies ran while one was open for 32% of the time, Pallas kernels for 0%

profile of v3, /device:TPU:1, one launch (start us, length us, event | category | flops | bytes accessed | tf_op | source)
XLA Modules:
  0.0 272.4 jit_solution(1943363617888783762)
XLA Ops:
  9.6 8.6 %all-to-all-start.1 = ((s32[32,1,2]{2,1,0:T(1,128)}), s32[32,1,2]{2,1,0:T(1,128)S(1)}, u32[]{:S(2)}, u32[]{:S(2)}) async-start(s32[32,1,2]{2,1,0:T(1,128)} %bitcast.5), calls=%async_computation.1 | async-start | bytes 32768 | tf_op jit(solution)/shard_map/all_to_all | solution.py:58
  21.0 2.8 %gather_fusion.2 = f32[64,128,128]{2,1,0:T(8,128)} fusion(f32[24,128,128]{2,1,0:T(8,128)S(1)} %copy-done.2, s32[1024]{0:T(1024)S(1)} %pad_clamp_fusion.1), kind=kCustom, calls=%fused_computation.3.clone | custom fusion | bytes 8388864 | tf_op jit(solution)/shard_map/jit(_take)/gather | solution.py:81
  26.6 7.7 %fusion.3 = (bf16[64,1,128,128]{3,2,1,0:T(8,128)(2,1)}, bf16[64,1,128,128]{3,2,1,0:T(8,128)(2,1)}, bf16[64,128,128]{2,1,0:T(8,128)(2,1)}) fusion(f32[64,128,128]{2,1,0:T(8,128)} %gather_fusion.1, f32[64]{0:T(128)S(1)} %convert_element_type.42, pred[64]{0:T(512)(128)(4,1)S(1)} %compare_and_fusion.1, f32[64,128,128]{2,1,0:T(8,128)} %gather_fusion.2, ...), kind=kLoop, calls=%fused_computation.18 | loop fusion | flops 9437184 | bytes 18874688 | tf_op jit(solution)/shard_map/stack | solution.py:80
  34.2 7.6 %all-to-all-start = ((bf16[32,2,128,128]{3,2,1,0:T(8,128)(2,1)}), bf16[32,2,128,128]{3,2,1,0:T(8,128)(2,1)}, u32[]{:S(2)}, u32[]{:S(2)}) async-start(bf16[32,2,128,128]{3,2,1,0:T(8,128)(2,1)} %bitcast.69), calls=%async_computation | async-start | bytes 4194304 | tf_op jit(solution)/shard_map/all_to_all | solution.py:61
  41.9 4.6 %pad_maximum_fusion = bf16[64,2,128,128]{3,2,1,0:T(8,128)(2,1)} fusion(bf16[64,1,128,128]{3,2,1,0:T(8,128)(2,1)} %get-tuple-element.30, bf16[64,1,128,128]{3,2,1,0:T(8,128)(2,1)} %get-tuple-element.29), kind=kLoop, calls=%fused_computation.10 | loop fusion | flops 2097152 | bytes 8388608 | tf_op jit(solution)/shard_map/stack | solution.py:80
  46.5 30.8 %all_gather.10 = bf16[1024,384]{0,1:T(8,128)(2,1)} all-gather(bf16[256,384]{0,1:T(8,128)(2,1)S(1)} %bitcast.74), channel_id=1, replica_groups=mesh['gx'=8,'gy'=8,'gz'=4] {'gz'}, dimensions={0}, use_global_device_ids=true | all-gather | bytes 983040 | tf_op jit(solution)/shard_map/all_gather | solution.py:65
  78.9 4.1 %bitcast_convert_fusion = f32[64,128,128]{2,1,0:T(8,128)} fusion(bf16[32,2,128,128]{3,2,1,0:T(8,128)(2,1)} %all-to-all-done), kind=kLoop, calls=%fused_computation.20 | loop fusion | flops 1048576 | bytes 6291456 | tf_op jit(solution)/shard_map/reshape | solution.py:74
  83.0 2.8 %gather_fusion.3 = f32[24,128,128]{2,1,0:T(8,128)S(1)} fusion(f32[64,128,128]{2,1,0:T(8,128)} %bitcast_convert_fusion, s32[1024]{0:T(1024)S(1)} %pad_clamp_fusion), kind=kCustom, calls=%fused_computation.1.clone | custom fusion | bytes 3145824 | tf_op jit(solution)/shard_map/jit(_take)/gather | solution.py:74
  88.2 7.1 %multiply_convert_fusion = bf16[1024,3072]{1,0:T(8,128)(2,1)} fusion(bf16[1024,384]{0,1:T(8,128)(2,1)S(1)} %copy-done.4, bf16[384,3072]{1,0:T(8,128)(2,1)} %all-gather.3.cloned.1.call-done), kind=kOutput, calls=%fused_computation.6 | convolution fusion | flops 2422210560 | bytes 9437184 | tf_op jit(solution)/shard_map/dot_general | solution.py:117
  95.3 4.8 %copy.30 = bf16[32,2,2,128,128]{4,3,1,2,0:T(8,128)(2,1)} copy(bf16[32,2,2,128,128]{4,3,2,1,0:T(8,128)(2,1)} %bitcast.66) | data formatting | bytes 8388608 | tf_op jit(solution)/shard_map/reshape | solution.py:86
  100.1 7.0 %all-to-all-start.2 = ((bf16[32,2,2,128,128]{4,3,1,2,0:T(8,128)(2,1)}), bf16[32,2,2,128,128]{4,3,1,2,0:T(8,128)(2,1)}, u32[]{:S(2)}, u32[]{:S(2)}) async-start(bf16[32,2,2,128,128]{4,3,1,2,0:T(8,128)(2,1)} %copy.30), calls=%async_computation.2 | async-start | bytes 8388608 | tf_op jit(solution)/shard_map/all_to_all | solution.py:85
  107.3 50.4 %all-to-all-done.2 = bf16[32,2,2,128,128]{4,3,1,2,0:T(8,128)(2,1)} async-done(((bf16[32,2,2,128,128]{4,3,1,2,0:T(8,128)(2,1)}), bf16[32,2,2,128,128]{4,3,1,2,0:T(8,128)(2,1)}, u32[]{:S(2)}, u32[]{:S(2)}) %all-to-all-start.2) | async-done | bytes 4194336 | tf_op jit(solution)/shard_map/all_to_all | solution.py:85
  157.6 7.1 %all-gather.5.cloned.1.call-done = bf16[1024,3072]{1,0:T(8,128)(2,1)} async-done(((bf16[128,3072]{1,0:T(8,128)(2,1)}), bf16[1024,3072]{1,0:T(8,128)(2,1)}) %all-gather.5.cloned.1.call-update) | async-done | bytes 6291472 | tf_op jit(solution)/shard_map/all_gather | solution.py:92
  164.7 6.7 %multiply_convert_fusion.1 = bf16[384,3072]{1,0:T(8,128)(2,1)} fusion(bf16[1024,384]{0,1:T(8,128)(2,1)S(1)} %copy-done.4, bf16[1024,3072]{1,0:T(8,128)(2,1)} %all-gather.5.cloned.1.call-done), kind=kOutput, calls=%fused_computation.7 | convolution fusion | flops 2418278400 | bytes 9437184 | tf_op jit(solution)/shard_map/dot_general | solution.py:104
  171.4 5.1 %all-to-all-start.3 = ((bf16[8,48,3072]{2,1,0:T(8,128)(2,1)}), bf16[8,48,3072]{2,1,0:T(8,128)(2,1)}, u32[]{:S(2)}, u32[]{:S(2)}) async-start(bf16[8,48,3072]{2,1,0:T(8,128)(2,1)} %bitcast.73), calls=%async_computation.4 | async-start | bytes 4718592 | tf_op jit(solution)/shard_map/all_to_all | solution.py:108
  176.5 7.6 %multiply_convert_fusion.2 = bf16[384,1024]{1,0:T(8,128)(2,1)} fusion(bf16[384,3072]{1,0:T(8,128)(2,1)} %all-gather.3.cloned.1.call-done, bf16[1024,3072]{1,0:T(8,128)(2,1)} %all-gather.5.cloned.1.call-done), kind=kOutput, calls=%fused_computation.35 | convolution fusion | flops 2416705536 | bytes 9437184 | tf_op jit(solution)/shard_map/dot_general | solution.py:98
  184.2 6.5 %copy.31 = f32[32,2,2,128,128]{4,3,1,0,2:T(8,128)} copy(bf16[32,2,2,128,128]{4,3,1,2,0:T(8,128)(2,1)} %all-to-all-done.2) | data formatting | bytes 12582912 | tf_op jit(solution)/shard_map/reshape | solution.py:94
  190.7 8.0 %slice_bitcast_fusion = (f32[64,128,128]{2,1,0:T(8,128)}, f32[64,128,128]{2,1,0:T(8,128)}) fusion(f32[64,2,128,128]{3,2,0,1:T(8,128)} %bitcast.65), kind=kLoop, calls=%fused_computation.8 | loop fusion | bytes 16777216 | tf_op jit(solution)/shard_map/squeeze | solution.py:96
  198.7 4.0 %gather_fusion.5 = f32[24,128,128]{2,1,0:T(8,128)} fusion(f32[64,128,128]{2,1,0:T(8,128)} %get-tuple-element.27, s32[1024]{0:T(1024)S(1)} %pad_clamp_fusion), kind=kCustom, calls=%fused_computation.5.clone | custom fusion | bytes 3145824 | tf_op jit(solution)/shard_map/jit(_take)/gather | solution.py:74
  202.7 4.0 %gather_fusion.4 = f32[24,128,128]{2,1,0:T(8,128)} fusion(f32[64,128,128]{2,1,0:T(8,128)} %get-tuple-element.28, s32[1024]{0:T(1024)S(1)} %pad_clamp_fusion), kind=kCustom, calls=%fused_computation.4.clone | custom fusion | bytes 3145824 | tf_op jit(solution)/shard_map/jit(_take)/gather | solution.py:74
  213.3 27.8 %reduce-scatter.5.cloned.1.call-done = bf16[128,3072]{1,0:T(8,128)(2,1)} async-done(((bf16[1024,3072]{1,0:T(8,128)(2,1)}), bf16[128,3072]{1,0:T(8,128)(2,1)}) %reduce-scatter.5.cloned.1.call-update) | async-done | bytes 786448 | tf_op jit(solution)/shard_map/reduce_scatter | solution.py:116
  241.1 5.6 %multiply_add_fusion = (f32[128,3072]{1,0:T(8,128)}, f32[128,3072]{1,0:T(8,128)}, f32[128,3072]{1,0:T(8,128)}) fusion(f32[16,8,24,128]{3,2,1,0:T(8,128)S(1)} %bitcast.68, s32[3072]{0:T(1024)S(1)} %get-tuple-element.36, s32[3072]{0:T(1024)S(1)} %get-tuple-element.37, s32[128]{0:T(128)S(1)} %get-tuple-element.38, s32[128]{0:T(128)S(1)} %get-tuple-element.39, ...), kind=kLoop, calls=%fused_computation.34 | loop fusion | flops 15335424 | bytes 10264704 | tf_op jit(solution)/shard_map/add | solution.py:135
  246.7 2.8 %reduce_sum.62 = bf16[48,3072]{1,0:T(8,128)(2,1)} reduce(bf16[8,48,3072]{2,1,0:T(8,128)(2,1)} %all-to-all-done.3, bf16[]{:T(256)} %constant.140.clone.1), dimensions={0}, to_apply=%region_6.9 | reduce | flops 1032192 | bytes 2654210 | tf_op jit(solution)/shard_map/reduce_sum | solution.py:115
  249.5 16.3 %reduce-scatter.3.cloned.1.call-done = bf16[384,256]{1,0:T(8,128)(2,1)} async-done(((bf16[384,1024]{1,0:T(8,128)(2,1)}), bf16[384,256]{1,0:T(8,128)(2,1)}) %reduce-scatter.3.cloned.1.call-update) | async-done | bytes 196624 | tf_op jit(solution)/shard_map/reduce_scatter | solution.py:99
  (56 shorter events, 18.6 us)
Async XLA Ops:
  7.2 11.1 %copy-start = (f32[24,128,128]{2,1,0:T(8,128)S(1)}, f32[24,128,128]{2,1,0:T(8,128)}, u32[]{:S(2)}) copy-start(f32[24,128,128]{2,1,0:T(8,128)} %param.12) | copy-start | bytes 4718596
  7.2 71.7 %all-gather.3.cloned.1.call-start = ((), (), s32[]{:S(2)}) async-start(), calls=%async_computation.6 | async-start | bytes 2654208 | tf_op jit(solution)/shard_map/all_gather | solution.py:64
  9.6 24.6 %all-to-all-start.1 = ((s32[32,1,2]{2,1,0:T(1,128)}), s32[32,1,2]{2,1,0:T(1,128)S(1)}, u32[]{:S(2)}, u32[]{:S(2)}) async-start(s32[32,1,2]{2,1,0:T(1,128)} %bitcast.5), calls=%async_computation.1 | async-start | bytes 32768 | tf_op jit(solution)/shard_map/all_to_all | solution.py:58
  18.2 2.8 %copy-start.2 = (f32[24,128,128]{2,1,0:T(8,128)S(1)}, f32[24,128,128]{2,1,0:T(8,128)}, u32[]{:S(2)}) copy-start(f32[24,128,128]{2,1,0:T(8,128)} %param.13) | copy-start | bytes 4718596
  21.0 2.8 %copy-start.3 = (f32[24,128,128]{2,1,0:T(8,128)S(1)}, f32[24,128,128]{2,1,0:T(8,128)}, u32[]{:S(2)}) copy-start(f32[24,128,128]{2,1,0:T(8,128)} %param.11) | copy-start | bytes 4718596
  34.2 44.6 %all-to-all-start = ((bf16[32,2,128,128]{3,2,1,0:T(8,128)(2,1)}), bf16[32,2,128,128]{3,2,1,0:T(8,128)(2,1)}, u32[]{:S(2)}, u32[]{:S(2)}) async-start(bf16[32,2,128,128]{3,2,1,0:T(8,128)(2,1)} %bitcast.69), calls=%async_computation | async-start | bytes 4194304 | tf_op jit(solution)/shard_map/all_to_all | solution.py:61
  41.8 122.9 %all-gather.5.cloned.1.call-start = ((), (), s32[]{:S(2)}) async-start(), calls=%async_computation.7 | async-start | bytes 7077888 | tf_op jit(solution)/shard_map/all_gather | solution.py:92
  41.9 4.7 %copy-start.5 = (bf16[384,256]{1,0:T(8,128)(2,1)S(1)}, bf16[384,256]{1,0:T(8,128)(2,1)}, u32[]{:S(2)}) copy-start(bf16[384,256]{1,0:T(8,128)(2,1)} %param.17) | copy-start | bytes 589828
  86.9 1.3 copy-start.4
  88.1 153.0 %reduce-scatter.5.cloned.1.call-start = ((), (), s32[]{:S(2)}) async-start(), calls=%async_computation.9 | async-start | bytes 7077888 | tf_op jit(solution)/shard_map/reduce_scatter | solution.py:116
  100.1 7.1 %copy-start.6 = (s32[1,24]{1,0:T(1,128)S(1)}, s32[1,24]{1,0:T(1,128)}, u32[]{:S(2)}) copy-start(s32[1,24]{1,0:T(1,128)} %param.15) | copy-start | bytes 292
  100.1 57.5 %all-to-all-start.2 = ((bf16[32,2,2,128,128]{4,3,1,2,0:T(8,128)(2,1)}), bf16[32,2,2,128,128]{4,3,1,2,0:T(8,128)(2,1)}, u32[]{:S(2)}, u32[]{:S(2)}) async-start(bf16[32,2,2,128,128]{4,3,1,2,0:T(8,128)(2,1)} %copy.30), calls=%async_computation.2 | async-start | bytes 8388608 | tf_op jit(solution)/shard_map/all_to_all | solution.py:85
  171.4 75.3 %all-to-all-start.3 = ((bf16[8,48,3072]{2,1,0:T(8,128)(2,1)}), bf16[8,48,3072]{2,1,0:T(8,128)(2,1)}, u32[]{:S(2)}, u32[]{:S(2)}) async-start(bf16[8,48,3072]{2,1,0:T(8,128)(2,1)} %bitcast.73), calls=%async_computation.4 | async-start | bytes 4718592 | tf_op jit(solution)/shard_map/all_to_all | solution.py:108
  176.5 89.3 %reduce-scatter.3.cloned.1.call-start = ((), (), s32[]{:S(2)}) async-start(), calls=%async_computation.8 | async-start | bytes 983040 | tf_op jit(solution)/shard_map/reduce_scatter | solution.py:99
  241.1 24.7 %copy-start.1 = (f32[24,128,128]{2,1,0:T(8,128)S(1)}, f32[24,128,128]{2,1,0:T(8,128)}, u32[]{:S(2)}) copy-start(f32[24,128,128]{2,1,0:T(8,128)} %param.12) | copy-start | bytes 4718596
Sparse Core Ops, SparseCore 0:
  9.8 32.2 all-gather.2
  88.2 76.4 all-gather.4
  167.3 73.8 reduce-scatter.4
  244.1 21.6 reduce-scatter.2

commit v4 on v3

--- a/solution.py
+++ b/solution.py
@@ -51,20 +51,19 @@
     slot_ids = jnp.arange(total_slots, dtype=jnp.int32)
     matches = (position[None, :] == slot_ids[:, None]).astype(jnp.int32)
     source = jnp.sum(matches * ordinal[None, :], axis=1)
-    filled = jnp.sum(matches, axis=1).astype(jnp.float32)[:, None, None]
     labels = jnp.sum(matches * (local_tile[None, :] + 1), axis=1)
     grid_shape = (group_size, capacity, tile_side, tile_side)
-    send_weight = (jnp.take(flat_weight, source, axis=0) * filled).astype(jnp.bfloat16)
+
+    def route(flat):
+        send = jnp.take(flat, source, axis=0).astype(jnp.bfloat16).reshape(grid_shape)
+        return lax.all_to_all(send, ("gx", "gz"), split_axis=0, concat_axis=0, tiled=True)
+
     got_labels = lax.all_to_all(
         labels.reshape(group_size, capacity), ("gx", "gz"), split_axis=0, concat_axis=0, tiled=True
     )
-    got_weight = lax.all_to_all(
-        send_weight.reshape(grid_shape), ("gx", "gz"), split_axis=0, concat_axis=0, tiled=True
-    )
+    got_weight = route(flat_weight)
     token_band = lax.all_gather(tokens, "gx", axis=0, tiled=True)
-    grad_band = lax.all_gather(grad_out.T, "gz", axis=0, tiled=True)
-    got_weight, token_band, grad_band = lax.optimization_barrier((got_weight, token_band, grad_band))
-    got_weight = got_weight.astype(jnp.float32)
+    got_weight, token_band = lax.optimization_barrier((got_weight, token_band))
     got_labels = got_labels.reshape(total_slots)
     wanted = jnp.arange(1, tiles_own + 1, dtype=jnp.int32)
     hits = (got_labels[None, :] == wanted[:, None]).astype(jnp.int32)
@@ -75,25 +74,18 @@
         tile_grid = flat_tiles.reshape(row_tiles, col_tiles, tile_side, tile_side)
         return tile_grid.transpose(0, 2, 1, 3).reshape(row_tiles * tile_side, col_tiles * tile_side)
 
-    weight = place(got_weight)
-    weight_low = weight.astype(jnp.bfloat16)
-    send_moments = jnp.stack(
-        [jnp.take(flat_first, source, axis=0) * filled, jnp.take(flat_second, source, axis=0) * filled],
-        axis=1,
-    ).astype(jnp.bfloat16)
-    send_moments, weight_low = lax.optimization_barrier((send_moments, weight_low))
-    got_moments = lax.all_to_all(
-        send_moments.reshape(group_size, capacity, 2, tile_side, tile_side),
-        ("gx", "gz"),
-        split_axis=0,
-        concat_axis=0,
-        tiled=True,
+    weight_low = place(got_weight)
+    weight = weight_low.astype(jnp.float32)
+    flat_first, flat_second, grad_out, weight_low = lax.optimization_barrier(
+        (flat_first, flat_second, grad_out, weight_low)
     )
     weight_band = lax.all_gather(weight_low, "gy", axis=0, tiled=True)
-    got_moments, weight_band = lax.optimization_barrier((got_moments, weight_band))
-    got_moments = got_moments.astype(jnp.float32).reshape(total_slots, 2, tile_side, tile_side)
-    first_moment = place(got_moments[:, 0])
-    second_moment = place(got_moments[:, 1])
+    grad_band = lax.all_gather(grad_out.T, "gz", axis=0, tiled=True)
+    got_first = route(flat_first)
+    got_second = route(flat_second)
+    got_first, got_second, weight_band = lax.optimization_barrier((got_first, got_second, weight_band))
+    first_moment = place(got_first).astype(jnp.float32)
+    second_moment = place(got_second).astype(jnp.float32)
     factor = 1.0 / math.sqrt(D)
     partial_out = factor * jnp.dot(token_band, weight_band.T, preferred_element_type=jnp.float32)
     outputs = lax.psum_scatter(

time: 274 us -> 251 us (0.916)
  local copies, waits for them, and re-layouts: 46.2 us -> 24 us
  blocking collectives: 30.8 us -> 47.5 us
  other arithmetic: 29.3 us -> 20.3 us
  waiting for transfers between devices: 102 us -> 96.3 us
    all_to_all x0 -> x1, blocking collectives: none -> 36.7 us  [route(): lax.all_to_all(send, ('gx', 'gz'), split_axis=0, concat_axis=0, tiled=True)]
    all_gather x1, blocking collectives: 30.8 us -> 10.8 us  [body(): grad_band = lax.all_gather(grad_out.T, 'gz', axis=0, tiled=True)]
    another operation x2 -> x0, other arithmetic: 12.3 us -> none  [body(): jnp.stack([jnp.take(flat_first, source, axis=0) * filled, jnp.take(flat_s...]
    reshape x2 -> x0, local copies, waits for them, and re-layouts: 11.3 us -> none  [the longest x1 6.51 us: body(): got_moments.astype(jnp.float32)]
    convert_element_type x1 -> x2, other arithmetic: 0.01 us -> 8.4 us  [route(): jnp.take(flat, source, axis=0).astype(jnp.bfloat16).reshape(grid_shape)]
    squeeze x1 -> x0, local copies, waits for them, and re-layouts: 8.01 us -> none  [body(): second_moment = place(got_moments[:, 1])]
    reduce_scatter x1, waiting for transfers between devices: 27.8 us -> 20.1 us  [body(): lax.psum_scatter((factor * jnp.dot(grad_band, token_band, preferred_eleme...]
    all_to_all x2, waiting for transfers between devices: 50.4 us -> 57.7 us  [route(): lax.all_to_all(send, ('gx', 'gz'), split_axis=0, concat_axis=0, tiled=True)]
  transfers between devices with their start and end apart: 8 -> 8, of which waited for: 4 -> 5; matrix products, arithmetic and copies ran while one was open for 32% -> 24% of each run, Pallas kernels for 0% -> 0%
where the time goes in v4:
time: 251 us; the launch traced here: 249 us
  waiting for transfers between devices  96.3 us (38%)
  blocking collectives  47.5 us (19%)
  starting transfers between devices  26 us (10%)
  local copies, waits for them, and re-layouts  24 us (10%)
  matrix products  21.1 us (8%)
  other arithmetic  20.3 us (8%)
  between operations  14 us (6%)
    all_to_all x2, waiting for transfers between devices, route(): lax.all_to_all(send, ('gx', 'gz'), split_axis=0, concat_axis=0, tiled=True)  57.7 us
    all_to_all x1, blocking collectives, route(): lax.all_to_all(send, ('gx', 'gz'), split_axis=0, concat_axis=0, tiled=True)  36.7 us
    reduce_scatter x1, waiting for transfers between devices, body(): lax.psum_scatter((factor * jnp.dot(grad_band, token_band, preferred_eleme...  20.1 us
    reduce_scatter x1, waiting for transfers between devices, body(): lax.psum_scatter(partial_out.astype(jnp.bfloat16), 'gz', scatter_dimensio...  16.5 us
    all_to_all x2, starting transfers between devices, route(): lax.all_to_all(send, ('gx', 'gz'), split_axis=0, concat_axis=0, tiled=True)  11.5 us
    all_gather x1, blocking collectives, body(): grad_band = lax.all_gather(grad_out.T, 'gz', axis=0, tiled=True)  10.8 us
    gather x3, local copies, waits for them, and re-layouts, route(): jnp.take(flat, source, axis=0).astype(jnp.bfloat16).reshape(grid_shape)  9.07 us
    all_to_all x1, starting transfers between devices, body(): lax.all_to_all(labels.reshape(group_size, capacity), ('gx', 'gz'), split_...  8.58 us
  transfers between devices with their start and end apart: 8, of which 5 were waited for; matrix products, arithmetic and copies ran while one was open for 24% of the time, Pallas kernels for 0%

profile of v4, /device:TPU:1, one launch (start us, length us, event | category | flops | bytes accessed | tf_op | source)
XLA Modules:
  0.0 249.2 jit_solution(9334479047735488956)
XLA Ops:
  9.6 8.6 %all-to-all-start.1 = ((s32[32,1,2]{2,1,0:T(1,128)}), s32[32,1,2]{2,1,0:T(1,128)S(1)}, u32[]{:S(2)}, u32[]{:S(2)}) async-start(s32[32,1,2]{2,1,0:T(1,128)} %bitcast.1), calls=%async_computation.1 | async-start | bytes 32768 | tf_op jit(solution)/shard_map/all_to_all | solution.py:61
  18.2 2.1 gather_fusion
  20.3 3.4 %select_convert_fusion.2 = bf16[64,128,128]{2,1,0:T(8,128)(2,1)} fusion(bf16[64,128,128]{2,1,0:T(8,128)(2,1)} %gather_fusion, pred[64]{0:T(512)(128)(4,1)S(1)} %compare_and_fusion.1), kind=kLoop, calls=%fused_computation.10 | loop fusion | flops 1048576 | bytes 4194368 | tf_op jit(solution)/shard_map/convert_element_type | solution.py:58
  25.1 6.1 %all-to-all-start = ((bf16[32,2,128,128]{3,2,1,0:T(8,128)(2,1)}), bf16[32,2,128,128]{3,2,1,0:T(8,128)(2,1)}, u32[]{:S(2)}, u32[]{:S(2)}) async-start(bf16[32,2,128,128]{3,2,1,0:T(8,128)(2,1)} %bitcast.47), calls=%async_computation | async-start | bytes 4194304 | tf_op jit(solution)/shard_map/all_to_all | solution.py:59
  32.7 30.5 %all-to-all-done = bf16[32,2,128,128]{3,2,1,0:T(8,128)(2,1)} async-done(((bf16[32,2,128,128]{3,2,1,0:T(8,128)(2,1)}), bf16[32,2,128,128]{3,2,1,0:T(8,128)(2,1)}, u32[]{:S(2)}, u32[]{:S(2)}) %all-to-all-start) | async-done | bytes 2097184 | tf_op jit(solution)/shard_map/all_to_all | solution.py:59
  63.3 2.3 gather_fusion.1
  67.3 10.8 %all_gather.11 = bf16[1024,384]{0,1:T(8,128)(2,1)S(1)} all-gather(bf16[256,384]{0,1:T(8,128)(2,1)S(1)} %bitcast.57), channel_id=1, replica_groups=mesh['gx'=8,'gy'=8,'gz'=4] {'gz'}, dimensions={0}, use_global_device_ids=true | all-gather | bytes 983040 | tf_op jit(solution)/shard_map/all_gather | solution.py:83
  78.2 7.2 %multiply_convert_fusion = bf16[1024,3072]{1,0:T(8,128)(2,1)} fusion(bf16[1024,384]{0,1:T(8,128)(2,1)S(1)} %all_gather.11, bf16[384,3072]{1,0:T(8,128)(2,1)} %all-gather.3.cloned.1.call-done), kind=kOutput, calls=%fused_computation.6 | convolution fusion | flops 2422210560 | bytes 9437184 | tf_op jit(solution)/shard_map/dot_general | solution.py:109
  85.4 3.5 %gather_fusion.2 = bf16[64,128,128]{2,1,0:T(8,128)(2,1)} fusion(f32[24,128,128]{2,1,0:T(8,128)} %param.12, s32[1024]{0:T(1024)S(1)} %pad_clamp_fusion.1), kind=kCustom, calls=%fused_computation.2.clone | custom fusion | bytes 4194560 | tf_op jit(solution)/shard_map/jit(_take)/gather | solution.py:58
  88.9 3.5 %gather_fusion.3 = bf16[64,128,128]{2,1,0:T(8,128)(2,1)} fusion(f32[24,128,128]{2,1,0:T(8,128)} %param.13, s32[1024]{0:T(1024)S(1)} %pad_clamp_fusion.1), kind=kCustom, calls=%fused_computation.3.clone | custom fusion | bytes 4194560 | tf_op jit(solution)/shard_map/jit(_take)/gather | solution.py:58
  92.4 5.0 %select_convert_fusion = (bf16[64,128,128]{2,1,0:T(8,128)(2,1)}, bf16[64,128,128]{2,1,0:T(8,128)(2,1)S(1)}) fusion(bf16[64,128,128]{2,1,0:T(8,128)(2,1)} %gather_fusion.3, pred[64]{0:T(512)(128)(4,1)S(1)} %compare_and_fusion.1, bf16[64,128,128]{2,1,0:T(8,128)(2,1)} %gather_fusion.2), kind=kLoop, calls=%fused_computation.8 | loop fusion | flops 2097152 | bytes 8388672 | tf_op jit(solution)/shard_map/convert_element_type | solution.py:58
  97.5 36.7 %all_to_all.29 = bf16[32,2,128,128]{3,2,1,0:T(8,128)(2,1)} all-to-all(bf16[32,2,128,128]{3,2,1,0:T(8,128)(2,1)S(1)} %bitcast.49), channel_id=1, replica_groups=mesh['gx'=8,'gy'=8,'gz'=4] {'gx','gz'}, dimensions={0} | all-to-all | bytes 4194304 | tf_op jit(solution)/shard_map/all_to_all | solution.py:59
  134.1 5.4 %all-to-all-start.3 = ((bf16[32,2,128,128]{3,2,1,0:T(8,128)(2,1)}), bf16[32,2,128,128]{3,2,1,0:T(8,128)(2,1)}, u32[]{:S(2)}, u32[]{:S(2)}) async-start(bf16[32,2,128,128]{3,2,1,0:T(8,128)(2,1)} %bitcast.48), calls=%async_computation.3 | async-start | bytes 4194304 | tf_op jit(solution)/shard_map/all_to_all | solution.py:59
  139.6 27.1 %all-to-all-done.3 = bf16[32,2,128,128]{3,2,1,0:T(8,128)(2,1)} async-done(((bf16[32,2,128,128]{3,2,1,0:T(8,128)(2,1)}), bf16[32,2,128,128]{3,2,1,0:T(8,128)(2,1)}, u32[]{:S(2)}, u32[]{:S(2)}) %all-to-all-start.3) | async-done | bytes 2097184 | tf_op jit(solution)/shard_map/all_to_all | solution.py:59
  166.7 6.7 %multiply_convert_fusion.1 = bf16[384,3072]{1,0:T(8,128)(2,1)} fusion(bf16[1024,384]{0,1:T(8,128)(2,1)S(1)} %all_gather.11, bf16[1024,3072]{1,0:T(8,128)(2,1)} %all-gather.5.cloned.1.call-done), kind=kOutput, calls=%fused_computation.7 | convolution fusion | flops 2418278400 | bytes 9437184 | tf_op jit(solution)/shard_map/dot_general | solution.py:96
  173.4 5.8 %all-to-all-start.4 = ((bf16[8,48,3072]{2,1,0:T(8,128)(2,1)}), bf16[8,48,3072]{2,1,0:T(8,128)(2,1)}, u32[]{:S(2)}, u32[]{:S(2)}) async-start(bf16[8,48,3072]{2,1,0:T(8,128)(2,1)} %bitcast.56), calls=%async_computation.5 | async-start | bytes 4718592 | tf_op jit(solution)/shard_map/all_to_all | solution.py:100
  179.2 7.2 %multiply_convert_fusion.2 = bf16[384,1024]{1,0:T(8,128)(2,1)} fusion(bf16[384,3072]{1,0:T(8,128)(2,1)} %all-gather.3.cloned.1.call-done, bf16[1024,3072]{1,0:T(8,128)(2,1)} %all-gather.5.cloned.1.call-done), kind=kOutput, calls=%fused_computation.22 | convolution fusion | flops 2416705536 | bytes 9437184 | tf_op jit(solution)/shard_map/dot_general | solution.py:90
  186.5 2.3 gather_fusion.4
  188.8 3.1 %gather_fusion.5 = bf16[24,128,128]{2,1,0:T(8,128)(2,1)} fusion(bf16[64,128,128]{2,1,0:T(8,128)(2,1)} %bitcast.12, s32[1024]{0:T(1024)S(1)} %pad_clamp_fusion), kind=kCustom, calls=%fused_computation.5.clone | custom fusion | bytes 1572960 | tf_op jit(solution)/shard_map/jit(_take)/gather | solution.py:73
  193.7 2.1 copy.22
  197.9 20.1 %reduce-scatter.5.cloned.1.call-done = bf16[128,3072]{1,0:T(8,128)(2,1)} async-done(((bf16[1024,3072]{1,0:T(8,128)(2,1)}), bf16[128,3072]{1,0:T(8,128)(2,1)}) %reduce-scatter.5.cloned.1.call-update) | async-done | bytes 786448 | tf_op jit(solution)/shard_map/reduce_scatter | solution.py:108
  218.0 5.4 %multiply_add_fusion = (f32[128,3072]{1,0:T(8,128)}, f32[128,3072]{1,0:T(8,128)}, f32[128,3072]{1,0:T(8,128)}) fusion(s32[3072]{0:T(1024)S(1)} %get-tuple-element.36, s32[3072]{0:T(1024)S(1)} %get-tuple-element.37, s32[128]{0:T(128)S(1)} %get-tuple-element.38, s32[128]{0:T(128)S(1)} %get-tuple-element.39, s32[3072]{0:T(1024)S(1)} %broadcast_bitcast_fusion, ...), kind=kLoop, calls=%fused_computation.19 | loop fusion | flops 15728640 | bytes 9478272 | tf_op jit(solution)/shard_map/add | solution.py:127
  223.4 2.8 %reduce_sum.52 = bf16[48,3072]{1,0:T(8,128)(2,1)} reduce(bf16[8,48,3072]{2,1,0:T(8,128)(2,1)} %all-to-all-done.4, bf16[]{:T(256)} %constant.140.clone.1), dimensions={0}, to_apply=%region_5.8 | reduce | flops 1032192 | bytes 2654210 | tf_op jit(solution)/shard_map/reduce_sum | solution.py:107
  226.2 16.5 %reduce-scatter.3.cloned.1.call-done = bf16[384,256]{1,0:T(8,128)(2,1)} async-done(((bf16[384,1024]{1,0:T(8,128)(2,1)}), bf16[384,256]{1,0:T(8,128)(2,1)}) %reduce-scatter.3.cloned.1.call-update) | async-done | bytes 196624 | tf_op jit(solution)/shard_map/reduce_scatter | solution.py:91
  (44 shorter events, 10.9 us)
Async XLA Ops:
  7.2 11.0 %copy-start = (f32[24,128,128]{2,1,0:T(8,128)S(1)}, f32[24,128,128]{2,1,0:T(8,128)}, u32[]{:S(2)}) copy-start(f32[24,128,128]{2,1,0:T(8,128)} %param.11) | copy-start | bytes 4718596
  7.2 56.1 %all-gather.3.cloned.1.call-start = ((), (), s32[]{:S(2)}) async-start(), calls=%async_computation.7 | async-start | bytes 2654208 | tf_op jit(solution)/shard_map/all_gather | solution.py:65
  9.6 15.5 %all-to-all-start.1 = ((s32[32,1,2]{2,1,0:T(1,128)}), s32[32,1,2]{2,1,0:T(1,128)S(1)}, u32[]{:S(2)}, u32[]{:S(2)}) async-start(s32[32,1,2]{2,1,0:T(1,128)} %bitcast.1), calls=%async_computation.1 | async-start | bytes 32768 | tf_op jit(solution)/shard_map/all_to_all | solution.py:61
  25.1 38.2 %all-to-all-start = ((bf16[32,2,128,128]{3,2,1,0:T(8,128)(2,1)}), bf16[32,2,128,128]{3,2,1,0:T(8,128)(2,1)}, u32[]{:S(2)}, u32[]{:S(2)}) async-start(bf16[32,2,128,128]{3,2,1,0:T(8,128)(2,1)} %bitcast.47), calls=%async_computation | async-start | bytes 4194304 | tf_op jit(solution)/shard_map/all_to_all | solution.py:59
  31.1 135.6 %all-gather.5.cloned.1.call-start = ((), (), s32[]{:S(2)}) async-start(), calls=%async_computation.8 | async-start | bytes 7077888 | tf_op jit(solution)/shard_map/all_gather | solution.py:82
  66.2 1.1 copy-start.1
  67.3 150.7 %reduce-scatter.5.cloned.1.call-start = ((), (), s32[]{:S(2)}) async-start(), calls=%async_computation.10 | async-start | bytes 7077888 | tf_op jit(solution)/shard_map/reduce_scatter | solution.py:108
  134.1 32.6 %all-to-all-start.3 = ((bf16[32,2,128,128]{3,2,1,0:T(8,128)(2,1)}), bf16[32,2,128,128]{3,2,1,0:T(8,128)(2,1)}, u32[]{:S(2)}, u32[]{:S(2)}) async-start(bf16[32,2,128,128]{3,2,1,0:T(8,128)(2,1)} %bitcast.48), calls=%async_computation.3 | async-start | bytes 4194304 | tf_op jit(solution)/shard_map/all_to_all | solution.py:59
  173.4 50.0 %all-to-all-start.4 = ((bf16[8,48,3072]{2,1,0:T(8,128)(2,1)}), bf16[8,48,3072]{2,1,0:T(8,128)(2,1)}, u32[]{:S(2)}, u32[]{:S(2)}) async-start(bf16[8,48,3072]{2,1,0:T(8,128)(2,1)} %bitcast.56), calls=%async_computation.5 | async-start | bytes 4718592 | tf_op jit(solution)/shard_map/all_to_all | solution.py:100
  179.2 7.3 %copy-start.2 = (s32[1,24]{1,0:T(1,128)S(1)}, s32[1,24]{1,0:T(1,128)}, u32[]{:S(2)}) copy-start(s32[1,24]{1,0:T(1,128)} %param.15) | copy-start | bytes 292
  179.2 63.5 %reduce-scatter.3.cloned.1.call-start = ((), (), s32[]{:S(2)}) async-start(), calls=%async_computation.9 | async-start | bytes 983040 | tf_op jit(solution)/shard_map/reduce_scatter | solution.py:91
Sparse Core Ops, SparseCore 0:
  9.8 38.8 all-gather.2
  67.4 74.0 all-gather.4
  144.1 73.8 reduce-scatter.4
  220.9 21.6 reduce-scatter.2

commit v5 on v4

--- a/solution.py
+++ b/solution.py
@@ -52,10 +52,10 @@
     matches = (position[None, :] == slot_ids[:, None]).astype(jnp.int32)
     source = jnp.sum(matches * ordinal[None, :], axis=1)
     labels = jnp.sum(matches * (local_tile[None, :] + 1), axis=1)
-    grid_shape = (group_size, capacity, tile_side, tile_side)
 
     def route(flat):
-        send = jnp.take(flat, source, axis=0).astype(jnp.bfloat16).reshape(grid_shape)
+        send = jnp.take(flat, source, axis=0).astype(jnp.bfloat16)
+        send = send.reshape(group_size, capacity, *flat.shape[1:])
         return lax.all_to_all(send, ("gx", "gz"), split_axis=0, concat_axis=0, tiled=True)
 
     got_labels = lax.all_to_all(
@@ -81,16 +81,23 @@
     )
     weight_band = lax.all_gather(weight_low, "gy", axis=0, tiled=True)
     grad_band = lax.all_gather(grad_out.T, "gz", axis=0, tiled=True)
-    got_first = route(flat_first)
-    got_second = route(flat_second)
-    got_first, got_second, weight_band = lax.optimization_barrier((got_first, got_second, weight_band))
-    first_moment = place(got_first).astype(jnp.float32)
-    second_moment = place(got_second).astype(jnp.float32)
+    got_moments = route(jnp.concatenate([flat_first, flat_second], axis=1))
+    got_moments, weight_band = lax.optimization_barrier((got_moments, weight_band))
+    got_moments = got_moments.reshape(total_slots, 2 * tile_side, tile_side)
+    first_moment = place(got_moments[:, :tile_side]).astype(jnp.float32)
+    second_moment = place(got_moments[:, tile_side:]).astype(jnp.float32)
     factor = 1.0 / math.sqrt(D)
     partial_out = factor * jnp.dot(token_band, weight_band.T, preferred_element_type=jnp.float32)
-    outputs = lax.psum_scatter(
-        partial_out.astype(jnp.bfloat16), "gz", scatter_dimension=1, tiled=True
+    out_parts = lax.all_to_all(
+        partial_out.astype(jnp.bfloat16).reshape(
+            partial_out.shape[0], size_gz, partial_out.shape[1] // size_gz
+        ),
+        "gz",
+        split_axis=1,
+        concat_axis=1,
+        tiled=True,
     )
+    outputs = jnp.sum(out_parts.astype(jnp.float32), axis=1).astype(jnp.bfloat16)
     input_part = (
         factor
         * lax.dot_general(

time: 251 us -> 234 us (0.932)
  blocking collectives: 47.5 us -> 10.8 us
  starting transfers between devices: 26 us -> 35.8 us
  waiting for transfers between devices: 96.3 us -> 101 us
  other arithmetic: 20.3 us -> 24.2 us
  local copies, waits for them, and re-layouts: 24 us -> 26.9 us
    all_to_all x1 -> x0, blocking collectives: 36.7 us -> none  [route(): lax.all_to_all(send, ('gx', 'gz'), split_axis=0, concat_axis=0, tiled=True)]
    all_to_all x2, waiting for transfers between devices: 57.7 us -> 80.9 us  [route(): lax.all_to_all(send, ('gx', 'gz'), split_axis=0, concat_axis=0, tiled=True)]
    reduce_scatter x1 -> x0, waiting for transfers between devices: 16.5 us -> none  [body(): lax.psum_scatter(partial_out.astype(jnp.bfloat16), 'gz', scatter_dimensio...]
    reduce_scatter x1, waiting for transfers between devices: 20.1 us -> 13.8 us  [body(): lax.psum_scatter((factor * jnp.dot(grad_band, token_band, preferred_eleme...]
    all_to_all x0 -> x1, starting transfers between devices: none -> 5.07 us  [body(): lax.all_to_all(partial_out.astype(jnp.bfloat16).reshape(partial_out.shape...]
    slice x0 -> x1, local copies, waits for them, and re-layouts: none -> 4.99 us  [body(): second_moment = place(got_moments[:, tile_side:]).astype(jnp.float32)]
    all_to_all x0 -> x1, waiting for transfers between devices: none -> 4.43 us  [body(): lax.all_to_all(partial_out.astype(jnp.bfloat16).reshape(partial_out.shape...]
    all_to_all x2, starting transfers between devices: 11.5 us -> 15.7 us  [route(): lax.all_to_all(send, ('gx', 'gz'), split_axis=0, concat_axis=0, tiled=True)]
  transfers between devices with their start and end apart: 8 -> 8, of which waited for: 5 -> 5; matrix products, arithmetic and copies ran while one was open for 24% -> 27% of each run, Pallas kernels for 0% -> 0%
where the time goes in v5:
time: 234 us; the launch traced here: 233 us
  waiting for transfers between devices  101 us (43%)
  starting transfers between devices  35.8 us (15%)
  local copies, waits for them, and re-layouts  26.9 us (11%)
  other arithmetic  24.2 us (10%)
  matrix products  20.2 us (9%)
  between operations  14 us (6%)
  blocking collectives  10.8 us (5%)
    all_to_all x2, waiting for transfers between devices, route(): lax.all_to_all(send, ('gx', 'gz'), split_axis=0, concat_axis=0, tiled=True)  80.9 us
    all_to_all x2, starting transfers between devices, route(): lax.all_to_all(send, ('gx', 'gz'), split_axis=0, concat_axis=0, tiled=True)  15.7 us
    reduce_scatter x1, waiting for transfers between devices, body(): lax.psum_scatter((factor * jnp.dot(grad_band, token_band, preferred_eleme...  13.8 us
    all_gather x1, blocking collectives, body(): grad_band = lax.all_gather(grad_out.T, 'gz', axis=0, tiled=True)  10.8 us
    convert_element_type x2, other arithmetic, route(): send = jnp.take(flat, source, axis=0).astype(jnp.bfloat16)  9.29 us
    all_to_all x1, starting transfers between devices, body(): lax.all_to_all(labels.reshape(group_size, capacity), ('gx', 'gz'), split_...  8.58 us
    gather x3, local copies, waits for them, and re-layouts, place(): jnp.take(received.reshape(total_slots, tile_side, tile_side), picked, axi...  7.81 us
    dot_general x1, matrix products, body(): jnp.dot(grad_band, token_band, preferred_element_type=jnp.float32)  7.28 us
  transfers between devices with their start and end apart: 8, of which 5 were waited for; matrix products, arithmetic and copies ran while one was open for 27% of the time, Pallas kernels for 0%

profile of v5, /device:TPU:1, one launch (start us, length us, event | category | flops | bytes accessed | tf_op | source)
XLA Modules:
  0.0 232.9 jit_solution(18231689409735734618)
XLA Ops:
  9.6 8.6 %all-to-all-start.1 = ((s32[32,1,2]{2,1,0:T(1,128)}), s32[32,1,2]{2,1,0:T(1,128)S(1)}, u32[]{:S(2)}, u32[]{:S(2)}) async-start(s32[32,1,2]{2,1,0:T(1,128)} %bitcast.3), calls=%async_computation.1 | async-start | bytes 32768 | tf_op jit(solution)/shard_map/all_to_all | solution.py:61
  20.4 3.4 %select_convert_fusion.1 = bf16[32,2,128,128]{3,2,1,0:T(8,128)(2,1)} fusion(bf16[32,2,128,128]{3,2,1,0:T(8,128)(2,1)} %bitcast.54, pred[32,2]{1,0:T(8,128)(4,1)S(1)} %compare_and_fusion), kind=kLoop, calls=%fused_computation.8 | loop fusion | flops 1048576 | bytes 4194368 | tf_op jit(solution)/shard_map/convert_element_type | solution.py:57
  25.1 6.2 %all-to-all-start = ((bf16[32,2,128,128]{3,2,1,0:T(8,128)(2,1)}), bf16[32,2,128,128]{3,2,1,0:T(8,128)(2,1)}, u32[]{:S(2)}, u32[]{:S(2)}) async-start(bf16[32,2,128,128]{3,2,1,0:T(8,128)(2,1)} %select_convert_fusion.1), calls=%async_computation | async-start | bytes 4194304 | tf_op jit(solution)/shard_map/all_to_all | solution.py:59
  32.9 30.5 %all-to-all-done = bf16[32,2,128,128]{3,2,1,0:T(8,128)(2,1)} async-done(((bf16[32,2,128,128]{3,2,1,0:T(8,128)(2,1)}), bf16[32,2,128,128]{3,2,1,0:T(8,128)(2,1)}, u32[]{:S(2)}, u32[]{:S(2)}) %all-to-all-start) | async-done | bytes 2097184 | tf_op jit(solution)/shard_map/all_to_all | solution.py:59
  63.3 2.3 gather_fusion.2
  67.4 10.8 %all_gather.11 = bf16[1024,384]{0,1:T(8,128)(2,1)S(1)} all-gather(bf16[256,384]{0,1:T(8,128)(2,1)S(1)} %bitcast.62), channel_id=1, replica_groups=mesh['gx'=8,'gy'=8,'gz'=4] {'gz'}, dimensions={0}, use_global_device_ids=true | all-gather | bytes 983040 | tf_op jit(solution)/shard_map/all_gather | solution.py:83
  78.2 7.3 %multiply_convert_fusion = bf16[1024,3072]{1,0:T(8,128)(2,1)} fusion(bf16[1024,384]{0,1:T(8,128)(2,1)S(1)} %all_gather.11, bf16[384,3072]{1,0:T(8,128)(2,1)} %all-gather.3.cloned.1.call-done), kind=kOutput, calls=%fused_computation.5 | convolution fusion | flops 2422210560 | bytes 9437184 | tf_op jit(solution)/shard_map/dot_general | solution.py:116
  85.5 2.2 pad_maximum_fusion
  87.6 3.0 %gather_fusion.1 = bf16[64,256,128]{2,1,0:T(8,128)(2,1)} fusion(bf16[24,256,128]{2,1,0:T(8,128)(2,1)S(1)} %pad_maximum_fusion, s32[1024]{0:T(1024)S(1)} %pad_clamp_fusion.1), kind=kCustom, calls=%fused_computation.4 | custom fusion | bytes 8388864 | tf_op jit(solution)/shard_map/jit(_take)/gather | solution.py:57
  90.7 5.9 %select_convert_fusion = bf16[32,2,256,128]{3,2,1,0:T(8,128)(2,1)} fusion(bf16[32,2,256,128]{3,2,1,0:T(8,128)(2,1)} %bitcast.53, pred[32,2]{1,0:T(8,128)(4,1)S(1)} %compare_and_fusion), kind=kLoop, calls=%fused_computation.6 | loop fusion | flops 2097152 | bytes 8388672 | tf_op jit(solution)/shard_map/convert_element_type | solution.py:57
  96.5 9.5 %all-to-all-start.2 = ((bf16[32,2,256,128]{3,2,1,0:T(8,128)(2,1)}), bf16[32,2,256,128]{3,2,1,0:T(8,128)(2,1)}, u32[]{:S(2)}, u32[]{:S(2)}) async-start(bf16[32,2,256,128]{3,2,1,0:T(8,128)(2,1)} %select_convert_fusion), calls=%async_computation.2 | async-start | bytes 8388608 | tf_op jit(solution)/shard_map/all_to_all | solution.py:59
  106.1 50.5 %all-to-all-done.2 = bf16[32,2,256,128]{3,2,1,0:T(8,128)(2,1)} async-done(((bf16[32,2,256,128]{3,2,1,0:T(8,128)(2,1)}), bf16[32,2,256,128]{3,2,1,0:T(8,128)(2,1)}, u32[]{:S(2)}, u32[]{:S(2)}) %all-to-all-start.2) | async-done | bytes 4194336 | tf_op jit(solution)/shard_map/all_to_all | solution.py:59
  156.6 6.1 %multiply_convert_fusion.2 = bf16[384,1024]{1,0:T(8,128)(2,1)S(1)} fusion(bf16[384,3072]{1,0:T(8,128)(2,1)} %all-gather.3.cloned.1.call-done, bf16[1024,3072]{1,0:T(8,128)(2,1)} %all-gather.5.cloned.1.call-done), kind=kOutput, calls=%fused_computation.21 | convolution fusion | flops 2416705536 | bytes 9437184 | tf_op jit(solution)/shard_map/dot_general | solution.py:90
  163.6 5.1 %all-to-all-start.3 = ((bf16[384,4,256]{2,0,1:T(8,128)(2,1)}), bf16[384,4,256]{2,0,1:T(8,128)(2,1)S(1)}, u32[]{:S(2)}, u32[]{:S(2)}) async-start(bf16[384,4,256]{2,0,1:T(8,128)(2,1)} %bitcast.52), calls=%async_computation.3 | async-start | bytes 1572864 | tf_op jit(solution)/shard_map/all_to_all | solution.py:91
  168.7 6.7 %multiply_convert_fusion.1 = bf16[384,3072]{1,0:T(8,128)(2,1)} fusion(bf16[1024,384]{0,1:T(8,128)(2,1)S(1)} %all_gather.11, bf16[1024,3072]{1,0:T(8,128)(2,1)} %all-gather.5.cloned.1.call-done), kind=kOutput, calls=%fused_computation.7 | convolution fusion | flops 2418278400 | bytes 9437184 | tf_op jit(solution)/shard_map/dot_general | solution.py:103
  175.4 4.4 %all-to-all-done.3 = bf16[384,4,256]{2,0,1:T(8,128)(2,1)S(1)} async-done(((bf16[384,4,256]{2,0,1:T(8,128)(2,1)}), bf16[384,4,256]{2,0,1:T(8,128)(2,1)S(1)}, u32[]{:S(2)}, u32[]{:S(2)}) %all-to-all-start.3) | async-done | bytes 786464 | tf_op jit(solution)/shard_map/all_to_all | solution.py:91
  180.7 6.3 %all-to-all-start.4 = ((bf16[8,48,3072]{2,1,0:T(8,128)(2,1)}), bf16[8,48,3072]{2,1,0:T(8,128)(2,1)}, u32[]{:S(2)}, u32[]{:S(2)}) async-start(bf16[8,48,3072]{2,1,0:T(8,128)(2,1)} %bitcast.60), calls=%async_computation.4 | async-start | bytes 4718592 | tf_op jit(solution)/shard_map/all_to_all | solution.py:107
  187.2 5.0 %fusion.14 = (bf16[64,128,128]{2,1,0:T(8,128)(2,1)}, bf16[64,128,128]{2,1,0:T(8,128)(2,1)}) fusion(bf16[64,256,128]{2,1,0:T(8,128)(2,1)} %bitcast.10), kind=kLoop, calls=%fused_computation.61 | loop fusion | bytes 8388608 | tf_op jit(solution)/shard_map/slice | solution.py:88
  192.1 2.3 %gather_fusion.4 = bf16[24,128,128]{2,1,0:T(8,128)(2,1)S(1)} fusion(bf16[64,128,128]{2,1,0:T(8,128)(2,1)} %get-tuple-element.27, s32[1024]{0:T(1024)S(1)} %pad_clamp_fusion), kind=kCustom, calls=%fused_computation.2.clone | custom fusion | bytes 1572960 | tf_op jit(solution)/shard_map/jit(_take)/gather | solution.py:73
  194.5 3.2 %gather_fusion.3 = bf16[24,128,128]{2,1,0:T(8,128)(2,1)} fusion(bf16[64,128,128]{2,1,0:T(8,128)(2,1)} %get-tuple-element.28, s32[1024]{0:T(1024)S(1)} %pad_clamp_fusion), kind=kCustom, calls=%fused_computation.1.clone | custom fusion | bytes 1572960 | tf_op jit(solution)/shard_map/jit(_take)/gather | solution.py:73
  199.3 2.1 copy.23
  204.2 13.8 %reduce-scatter.2.cloned.1.call-done = bf16[128,3072]{1,0:T(8,128)(2,1)} async-done(((bf16[1024,3072]{1,0:T(8,128)(2,1)}), bf16[128,3072]{1,0:T(8,128)(2,1)}) %reduce-scatter.2.cloned.1.call-update) | async-done | bytes 786448 | tf_op jit(solution)/shard_map/reduce_scatter | solution.py:115
  218.1 5.6 %multiply_add_fusion = (f32[128,3072]{1,0:T(8,128)}, f32[128,3072]{1,0:T(8,128)}, f32[128,3072]{1,0:T(8,128)}) fusion(s32[3072]{0:T(1024)S(1)} %get-tuple-element.33, s32[3072]{0:T(1024)S(1)} %get-tuple-element.34, s32[128]{0:T(128)S(1)} %get-tuple-element.35, s32[128]{0:T(128)S(1)} %get-tuple-element.36, s32[3072]{0:T(1024)S(1)} %broadcast_bitcast_fusion, ...), kind=kLoop, calls=%fused_computation.18 | loop fusion | flops 15728640 | bytes 9478272 | tf_op jit(solution)/shard_map/add | solution.py:134
  223.6 2.8 %reduce_sum.71 = bf16[48,3072]{1,0:T(8,128)(2,1)} reduce(bf16[8,48,3072]{2,1,0:T(8,128)(2,1)} %all-to-all-done.4, bf16[]{:T(256)} %constant.157.clone.1), dimensions={0}, to_apply=%region_5.7 | reduce | flops 1032192 | bytes 2654210 | tf_op jit(solution)/shard_map/reduce_sum | solution.py:114
  (52 shorter events, 15.5 us)
Async XLA Ops:
  7.2 11.2 %copy-start = (f32[24,128,128]{2,1,0:T(8,128)S(1)}, f32[24,128,128]{2,1,0:T(8,128)}, u32[]{:S(2)}) copy-start(f32[24,128,128]{2,1,0:T(8,128)} %param.9) | copy-start | bytes 4718596
  7.2 56.1 %all-gather.3.cloned.1.call-start = ((), (), s32[]{:S(2)}) async-start(), calls=%async_computation.6 | async-start | bytes 2654208 | tf_op jit(solution)/shard_map/all_gather | solution.py:65
  9.6 15.5 %all-to-all-start.1 = ((s32[32,1,2]{2,1,0:T(1,128)}), s32[32,1,2]{2,1,0:T(1,128)S(1)}, u32[]{:S(2)}, u32[]{:S(2)}) async-start(s32[32,1,2]{2,1,0:T(1,128)} %bitcast.3), calls=%async_computation.1 | async-start | bytes 32768 | tf_op jit(solution)/shard_map/all_to_all | solution.py:61
  25.1 38.3 %all-to-all-start = ((bf16[32,2,128,128]{3,2,1,0:T(8,128)(2,1)}), bf16[32,2,128,128]{3,2,1,0:T(8,128)(2,1)}, u32[]{:S(2)}, u32[]{:S(2)}) async-start(bf16[32,2,128,128]{3,2,1,0:T(8,128)(2,1)} %select_convert_fusion.1), calls=%async_computation | async-start | bytes 4194304 | tf_op jit(solution)/shard_map/all_to_all | solution.py:59
  31.3 125.3 %all-gather.5.cloned.1.call-start = ((), (), s32[]{:S(2)}) async-start(), calls=%async_computation.7 | async-start | bytes 7077888 | tf_op jit(solution)/shard_map/all_gather | solution.py:82
  66.3 1.1 copy-start.4
  67.3 150.7 %reduce-scatter.2.cloned.1.call-start = ((), (), s32[]{:S(2)}) async-start(), calls=%async_computation.8 | async-start | bytes 7077888 | tf_op jit(solution)/shard_map/reduce_scatter | solution.py:115
  96.5 60.0 %all-to-all-start.2 = ((bf16[32,2,256,128]{3,2,1,0:T(8,128)(2,1)}), bf16[32,2,256,128]{3,2,1,0:T(8,128)(2,1)}, u32[]{:S(2)}, u32[]{:S(2)}) async-start(bf16[32,2,256,128]{3,2,1,0:T(8,128)(2,1)} %select_convert_fusion), calls=%async_computation.2 | async-start | bytes 8388608 | tf_op jit(solution)/shard_map/all_to_all | solution.py:59
  163.6 16.2 %all-to-all-start.3 = ((bf16[384,4,256]{2,0,1:T(8,128)(2,1)}), bf16[384,4,256]{2,0,1:T(8,128)(2,1)S(1)}, u32[]{:S(2)}, u32[]{:S(2)}) async-start(bf16[384,4,256]{2,0,1:T(8,128)(2,1)} %bitcast.52), calls=%async_computation.3 | async-start | bytes 1572864 | tf_op jit(solution)/shard_map/all_to_all | solution.py:91
  179.9 0.9 copy-start.2
  179.9 7.2 %copy-start.5 = (s32[1,24]{1,0:T(1,128)S(1)}, s32[1,24]{1,0:T(1,128)}, u32[]{:S(2)}) copy-start(s32[1,24]{1,0:T(1,128)} %param.13) | copy-start | bytes 292
  180.7 42.9 %all-to-all-start.4 = ((bf16[8,48,3072]{2,1,0:T(8,128)(2,1)}), bf16[8,48,3072]{2,1,0:T(8,128)(2,1)}, u32[]{:S(2)}, u32[]{:S(2)}) async-start(bf16[8,48,3072]{2,1,0:T(8,128)(2,1)} %bitcast.60), calls=%async_computation.4 | async-start | bytes 4718592 | tf_op jit(solution)/shard_map/all_to_all | solution.py:107
  201.4 2.1 copy-start.3
  218.1 8.4 %copy-start.1 = (f32[24,128,128]{2,1,0:T(8,128)S(1)}, f32[24,128,128]{2,1,0:T(8,128)}, u32[]{:S(2)}) copy-start(f32[24,128,128]{2,1,0:T(8,128)} %param.9) | copy-start | bytes 4718596
Sparse Core Ops, SparseCore 0:
  9.8 38.3 all-gather.2
  67.5 74.1 all-gather.4
  144.2 73.8 reduce-scatter.1

commit v6 on v5

--- a/solution.py
+++ b/solution.py
@@ -58,12 +58,23 @@
         send = send.reshape(group_size, capacity, *flat.shape[1:])
         return lax.all_to_all(send, ("gx", "gz"), split_axis=0, concat_axis=0, tiled=True)
 
-    got_labels = lax.all_to_all(
-        labels.reshape(group_size, capacity), ("gx", "gz"), split_axis=0, concat_axis=0, tiled=True
+    label_rows = jnp.broadcast_to(
+        labels.astype(jnp.bfloat16)[:, None, None], (total_slots, 16, tile_side)
     )
-    got_weight = route(flat_weight)
+    send_weight = jnp.concatenate(
+        [jnp.take(flat_weight, source, axis=0).astype(jnp.bfloat16), label_rows], axis=1
+    )
+    got_weight = lax.all_to_all(
+        send_weight.reshape(group_size, capacity, tile_side + 16, tile_side),
+        ("gx", "gz"),
+        split_axis=0,
+        concat_axis=0,
+        tiled=True,
+    ).reshape(total_slots, tile_side + 16, tile_side)
     token_band = lax.all_gather(tokens, "gx", axis=0, tiled=True)
     got_weight, token_band = lax.optimization_barrier((got_weight, token_band))
+    got_labels = got_weight[:, tile_side, 0].astype(jnp.int32)
+    got_weight = got_weight[:, :tile_side]
     got_labels = got_labels.reshape(total_slots)
     wanted = jnp.arange(1, tiles_own + 1, dtype=jnp.int32)
     hits = (got_labels[None, :] == wanted[:, None]).astype(jnp.int32)

time: 234 us -> 240 us (1.026)
  waiting for transfers between devices: 101 us -> 110 us
  starting transfers between devices: 35.8 us -> 27.5 us
    all_to_all x1, waiting for transfers between devices: 1.24 us -> 38.5 us  [body(): lax.all_to_all(send_weight.reshape(group_size, capacity, tile_side + 16,...]
    all_to_all x2 -> x1, waiting for transfers between devices: 80.9 us -> 50.5 us  [route(): lax.all_to_all(send, ('gx', 'gz'), split_axis=0, concat_axis=0, tiled=True)]
    all_to_all x2 -> x1, starting transfers between devices: 15.7 us -> 7.49 us  [route(): lax.all_to_all(send, ('gx', 'gz'), split_axis=0, concat_axis=0, tiled=True)]
    convert_element_type x0 -> x3, other arithmetic: none -> 4.21 us  [the longest x1 2.13 us: body(): got_labels = got_weight[:, tile_side, 0].astype(jnp.int32)]
    convert_element_type x2 -> x1, other arithmetic: 9.29 us -> 5.87 us  [route(): send = jnp.take(flat, source, axis=0).astype(jnp.bfloat16)]
    slice x0 -> x1, local copies, waits for them, and re-layouts: none -> 3.14 us  [body(): got_weight = got_weight[:, :tile_side]]
    gather x2 -> x1, local copies, waits for them, and re-layouts: 5.09 us -> 3.03 us  [route(): send = jnp.take(flat, source, axis=0).astype(jnp.bfloat16)]
  transfers between devices with their start and end apart: 8 -> 7, of which waited for: 5 -> 4; matrix products, arithmetic and copies ran while one was open for 27% -> 26% of each run, Pallas kernels for 0% -> 0%
where the time goes in v6:
time: 240 us; the launch traced here: 239 us
  waiting for transfers between devices  110 us (46%)
  local copies, waits for them, and re-layouts  29 us (12%)
  starting transfers between devices  27.5 us (11%)
  other arithmetic  25.9 us (11%)
  matrix products  20.2 us (8%)
  between operations  14 us (6%)
  blocking collectives  12.6 us (5%)
    all_to_all x1, waiting for transfers between devices, route(): lax.all_to_all(send, ('gx', 'gz'), split_axis=0, concat_axis=0, tiled=True)  50.5 us
    all_to_all x1, waiting for transfers between devices, body(): lax.all_to_all(send_weight.reshape(group_size, capacity, tile_side + 16,...  38.5 us
    reduce_scatter x1, waiting for transfers between devices, body(): lax.psum_scatter((factor * jnp.dot(grad_band, token_band, preferred_eleme...  15.8 us
    all_gather x1, blocking collectives, body(): grad_band = lax.all_gather(grad_out.T, 'gz', axis=0, tiled=True)  12.6 us
    all_to_all x1, starting transfers between devices, body(): lax.all_to_all(send_weight.reshape(group_size, capacity, tile_side + 16,...  8.63 us
    gather x3, local copies, waits for them, and re-layouts, place(): jnp.take(received.reshape(total_slots, tile_side, tile_side), picked, axi...  7.8 us
    all_to_all x1, starting transfers between devices, route(): lax.all_to_all(send, ('gx', 'gz'), split_axis=0, concat_axis=0, tiled=True)  7.49 us
    dot_general x1, matrix products, body(): jnp.dot(grad_band, token_band, preferred_element_type=jnp.float32)  7.26 us
  transfers between devices with their start and end apart: 7, of which 4 were waited for; matrix products, arithmetic and copies ran while one was open for 26% of the time, Pallas kernels for 0%

profile of v6, /device:TPU:1, one launch (start us, length us, event | category | flops | bytes accessed | tf_op | source)
XLA Modules:
  0.0 239.2 jit_solution(5350248835543948490)
XLA Ops:
  9.2 2.1 gather_fusion
  15.1 8.6 %all-to-all-start = ((bf16[32,2,144,128]{3,2,1,0:T(8,128)(2,1)}), bf16[32,2,144,128]{3,2,1,0:T(8,128)(2,1)}, u32[]{:S(2)}, u32[]{:S(2)}) async-start(bf16[32,2,144,128]{3,2,1,0:T(8,128)(2,1)} %pad_maximum_fusion.1), calls=%async_computation | async-start | bytes 4718592 | tf_op jit(solution)/shard_map/all_to_all | solution.py:67
  23.8 38.5 %all-to-all-done = bf16[32,2,144,128]{3,2,1,0:T(8,128)(2,1)} async-done(((bf16[32,2,144,128]{3,2,1,0:T(8,128)(2,1)}), bf16[32,2,144,128]{3,2,1,0:T(8,128)(2,1)}, u32[]{:S(2)}, u32[]{:S(2)}) %all-to-all-start) | async-done | bytes 2359328 | tf_op jit(solution)/shard_map/all_to_all | solution.py:67
  62.3 3.1 %slice.12 = bf16[64,128,128]{2,1,0:T(8,128)(2,1)} slice(bf16[64,144,128]{2,1,0:T(8,128)(2,1)} %bitcast.3), slice={[0:64], [0:128], [0:128]} | slice | bytes 4194304 | tf_op jit(solution)/shard_map/slice | solution.py:77
  65.4 2.1 convert_reduce_fusion
  67.8 2.3 gather_fusion.2
  71.9 12.6 %all_gather.11 = bf16[1024,384]{0,1:T(8,128)(2,1)S(1)} all-gather(bf16[256,384]{0,1:T(8,128)(2,1)S(1)} %bitcast.61), channel_id=1, replica_groups=mesh['gx'=8,'gy'=8,'gz'=4] {'gz'}, dimensions={0}, use_global_device_ids=true | all-gather | bytes 983040 | tf_op jit(solution)/shard_map/all_gather | solution.py:94
  84.4 7.3 %multiply_convert_fusion = bf16[1024,3072]{1,0:T(8,128)(2,1)} fusion(bf16[1024,384]{0,1:T(8,128)(2,1)S(1)} %all_gather.11, bf16[384,3072]{1,0:T(8,128)(2,1)} %all-gather.3.cloned.1.call-done), kind=kOutput, calls=%fused_computation.5 | convolution fusion | flops 2422210560 | bytes 9437184 | tf_op jit(solution)/shard_map/dot_general | solution.py:127
  91.7 2.2 pad_maximum_fusion
  93.9 3.0 %gather_fusion.1 = bf16[64,256,128]{2,1,0:T(8,128)(2,1)} fusion(bf16[24,256,128]{2,1,0:T(8,128)(2,1)S(1)} %pad_maximum_fusion, s32[1024]{0:T(1024)S(1)} %pad_clamp_fusion.1), kind=kCustom, calls=%fused_computation.4 | custom fusion | bytes 8388864 | tf_op jit(solution)/shard_map/jit(_take)/gather | solution.py:57
  96.9 5.9 %select_convert_fusion = bf16[32,2,256,128]{3,2,1,0:T(8,128)(2,1)} fusion(bf16[32,2,256,128]{3,2,1,0:T(8,128)(2,1)} %bitcast.52, pred[32,2]{1,0:T(8,128)(4,1)S(1)} %compare_and_fusion), kind=kLoop, calls=%fused_computation.6 | loop fusion | flops 2097152 | bytes 8388672 | tf_op jit(solution)/shard_map/convert_element_type | solution.py:57
  102.8 7.5 %all-to-all-start.1 = ((bf16[32,2,256,128]{3,2,1,0:T(8,128)(2,1)}), bf16[32,2,256,128]{3,2,1,0:T(8,128)(2,1)}, u32[]{:S(2)}, u32[]{:S(2)}) async-start(bf16[32,2,256,128]{3,2,1,0:T(8,128)(2,1)} %select_convert_fusion), calls=%async_computation.1 | async-start | bytes 8388608 | tf_op jit(solution)/shard_map/all_to_all | solution.py:59
  110.3 50.5 %all-to-all-done.1 = bf16[32,2,256,128]{3,2,1,0:T(8,128)(2,1)} async-done(((bf16[32,2,256,128]{3,2,1,0:T(8,128)(2,1)}), bf16[32,2,256,128]{3,2,1,0:T(8,128)(2,1)}, u32[]{:S(2)}, u32[]{:S(2)}) %all-to-all-start.1) | async-done | bytes 4194336 | tf_op jit(solution)/shard_map/all_to_all | solution.py:59
  160.8 6.2 %multiply_convert_fusion.2 = bf16[384,1024]{1,0:T(8,128)(2,1)S(1)} fusion(bf16[384,3072]{1,0:T(8,128)(2,1)} %all-gather.3.cloned.1.call-done, bf16[1024,3072]{1,0:T(8,128)(2,1)} %all-gather.5.cloned.1.call-done), kind=kOutput, calls=%fused_computation.22 | convolution fusion | flops 2416705536 | bytes 9437184 | tf_op jit(solution)/shard_map/dot_general | solution.py:101
  168.0 4.9 %all-to-all-start.2 = ((bf16[384,4,256]{2,0,1:T(8,128)(2,1)}), bf16[384,4,256]{2,0,1:T(8,128)(2,1)S(1)}, u32[]{:S(2)}, u32[]{:S(2)}) async-start(bf16[384,4,256]{2,0,1:T(8,128)(2,1)} %bitcast.51), calls=%async_computation.2 | async-start | bytes 1572864 | tf_op jit(solution)/shard_map/all_to_all | solution.py:102
  172.9 6.7 %multiply_convert_fusion.1 = bf16[384,3072]{1,0:T(8,128)(2,1)} fusion(bf16[1024,384]{0,1:T(8,128)(2,1)S(1)} %all_gather.11, bf16[1024,3072]{1,0:T(8,128)(2,1)} %all-gather.5.cloned.1.call-done), kind=kOutput, calls=%fused_computation.7 | convolution fusion | flops 2418278400 | bytes 9437184 | tf_op jit(solution)/shard_map/dot_general | solution.py:114
  179.6 4.4 %all-to-all-done.2 = bf16[384,4,256]{2,0,1:T(8,128)(2,1)S(1)} async-done(((bf16[384,4,256]{2,0,1:T(8,128)(2,1)}), bf16[384,4,256]{2,0,1:T(8,128)(2,1)S(1)}, u32[]{:S(2)}, u32[]{:S(2)}) %all-to-all-start.2) | async-done | bytes 786464 | tf_op jit(solution)/shard_map/all_to_all | solution.py:102
  185.0 6.3 %all-to-all-start.3 = ((bf16[8,48,3072]{2,1,0:T(8,128)(2,1)}), bf16[8,48,3072]{2,1,0:T(8,128)(2,1)}, u32[]{:S(2)}, u32[]{:S(2)}) async-start(bf16[8,48,3072]{2,1,0:T(8,128)(2,1)} %bitcast.59), calls=%async_computation.3 | async-start | bytes 4718592 | tf_op jit(solution)/shard_map/all_to_all | solution.py:118
  191.4 5.0 %fusion.14 = (bf16[64,128,128]{2,1,0:T(8,128)(2,1)}, bf16[64,128,128]{2,1,0:T(8,128)(2,1)}) fusion(bf16[64,256,128]{2,1,0:T(8,128)(2,1)} %bitcast.9), kind=kLoop, calls=%fused_computation.63 | loop fusion | bytes 8388608 | tf_op jit(solution)/shard_map/slice | solution.py:99
  196.4 2.3 gather_fusion.4
  198.7 3.2 %gather_fusion.3 = bf16[24,128,128]{2,1,0:T(8,128)(2,1)} fusion(bf16[64,128,128]{2,1,0:T(8,128)(2,1)} %get-tuple-element.28, s32[1024]{0:T(1024)S(1)} %pad_clamp_fusion), kind=kCustom, calls=%fused_computation.1.clone | custom fusion | bytes 1572960 | tf_op jit(solution)/shard_map/jit(_take)/gather | solution.py:84
  208.4 15.8 %reduce-scatter.2.cloned.1.call-done = bf16[128,3072]{1,0:T(8,128)(2,1)} async-done(((bf16[1024,3072]{1,0:T(8,128)(2,1)}), bf16[128,3072]{1,0:T(8,128)(2,1)}) %reduce-scatter.2.cloned.1.call-update) | async-done | bytes 786448 | tf_op jit(solution)/shard_map/reduce_scatter | solution.py:126
  224.3 5.6 %multiply_add_fusion = (f32[128,3072]{1,0:T(8,128)}, f32[128,3072]{1,0:T(8,128)}, f32[128,3072]{1,0:T(8,128)}) fusion(s32[3072]{0:T(1024)S(1)} %get-tuple-element.33, s32[3072]{0:T(1024)S(1)} %get-tuple-element.34, s32[128]{0:T(128)S(1)} %get-tuple-element.35, s32[128]{0:T(128)S(1)} %get-tuple-element.36, s32[3072]{0:T(1024)S(1)} %broadcast_bitcast_fusion, ...), kind=kLoop, calls=%fused_computation.19 | loop fusion | flops 15728640 | bytes 9478272 | tf_op jit(solution)/shard_map/add | solution.py:145
  229.8 2.8 %reduce_sum.71 = bf16[48,3072]{1,0:T(8,128)(2,1)} reduce(bf16[8,48,3072]{2,1,0:T(8,128)(2,1)} %all-to-all-done.3, bf16[]{:T(256)} %constant.157.clone.1), dimensions={0}, to_apply=%region_5.7 | reduce | flops 1032192 | bytes 2654210 | tf_op jit(solution)/shard_map/reduce_sum | solution.py:125
  (52 shorter events, 16.2 us)
Async XLA Ops:
  7.2 2.0 copy-start
  7.2 55.1 %all-gather.3.cloned.1.call-start = ((), (), s32[]{:S(2)}) async-start(), calls=%async_computation.5 | async-start | bytes 2654208 | tf_op jit(solution)/shard_map/all_gather | solution.py:74
  15.1 47.2 %all-to-all-start = ((bf16[32,2,144,128]{3,2,1,0:T(8,128)(2,1)}), bf16[32,2,144,128]{3,2,1,0:T(8,128)(2,1)}, u32[]{:S(2)}, u32[]{:S(2)}) async-start(bf16[32,2,144,128]{3,2,1,0:T(8,128)(2,1)} %pad_maximum_fusion.1), calls=%async_computation | async-start | bytes 4718592 | tf_op jit(solution)/shard_map/all_to_all | solution.py:67
  23.7 137.1 %all-gather.5.cloned.1.call-start = ((), (), s32[]{:S(2)}) async-start(), calls=%async_computation.6 | async-start | bytes 7077888 | tf_op jit(solution)/shard_map/all_gather | solution.py:93
  70.7 1.1 copy-start.4
  71.8 152.5 %reduce-scatter.2.cloned.1.call-start = ((), (), s32[]{:S(2)}) async-start(), calls=%async_computation.7 | async-start | bytes 7077888 | tf_op jit(solution)/shard_map/reduce_scatter | solution.py:126
  102.8 58.0 %all-to-all-start.1 = ((bf16[32,2,256,128]{3,2,1,0:T(8,128)(2,1)}), bf16[32,2,256,128]{3,2,1,0:T(8,128)(2,1)}, u32[]{:S(2)}, u32[]{:S(2)}) async-start(bf16[32,2,256,128]{3,2,1,0:T(8,128)(2,1)} %select_convert_fusion), calls=%async_computation.1 | async-start | bytes 8388608 | tf_op jit(solution)/shard_map/all_to_all | solution.py:59
  168.0 16.1 %all-to-all-start.2 = ((bf16[384,4,256]{2,0,1:T(8,128)(2,1)}), bf16[384,4,256]{2,0,1:T(8,128)(2,1)S(1)}, u32[]{:S(2)}, u32[]{:S(2)}) async-start(bf16[384,4,256]{2,0,1:T(8,128)(2,1)} %bitcast.51), calls=%async_computation.2 | async-start | bytes 1572864 | tf_op jit(solution)/shard_map/all_to_all | solution.py:102
  184.1 0.9 copy-start.2
  184.1 7.2 %copy-start.5 = (s32[1,24]{1,0:T(1,128)S(1)}, s32[1,24]{1,0:T(1,128)}, u32[]{:S(2)}) copy-start(s32[1,24]{1,0:T(1,128)} %param.13) | copy-start | bytes 292
  185.0 44.9 %all-to-all-start.3 = ((bf16[8,48,3072]{2,1,0:T(8,128)(2,1)}), bf16[8,48,3072]{2,1,0:T(8,128)(2,1)}, u32[]{:S(2)}, u32[]{:S(2)}) async-start(bf16[8,48,3072]{2,1,0:T(8,128)(2,1)} %bitcast.59), calls=%async_computation.3 | async-start | bytes 4718592 | tf_op jit(solution)/shard_map/all_to_all | solution.py:118
  205.6 2.1 copy-start.3
  224.3 8.4 %copy-start.1 = (f32[24,128,128]{2,1,0:T(8,128)S(1)}, f32[24,128,128]{2,1,0:T(8,128)}, u32[]{:S(2)}) copy-start(f32[24,128,128]{2,1,0:T(8,128)} %param.9) | copy-start | bytes 4718596
Sparse Core Ops, SparseCore 0:
  9.8 50.9 all-gather.2
  71.9 75.8 all-gather.4
  150.4 73.8 reduce-scatter.1

commit v7 on v5

--- a/solution.py
+++ b/solution.py
@@ -120,17 +120,20 @@
         scatter_dimension=0,
         tiled=True,
     ).astype(jnp.float32)
+    block_shape = weight.shape
+    row_ids = lax.broadcasted_iota(jnp.int32, block_shape, 0)
+    col_ids = lax.broadcasted_iota(jnp.int32, block_shape, 1)
+    seed_full = jnp.repeat(jnp.repeat(tile_seeds, tile_side, axis=0), tile_side, axis=1)
+    noise = dither(seed_full, row_ids % tile_side * tile_side + col_ids % tile_side)
+    noise, input_grad, first_moment, second_moment, weight = lax.optimization_barrier(
+        (noise, input_grad, first_moment, second_moment, weight)
+    )
     first_new = BETA_ONE * first_moment + (1.0 - BETA_ONE) * gradient
     second_new = BETA_TWO * second_moment + (1.0 - BETA_TWO) * gradient * gradient
     direction = (
         first_new / BIAS_ONE / (jnp.sqrt(second_new / BIAS_TWO) + EPSILON) + WEIGHT_DECAY * weight
     )
     moved = weight - LEARN_RATE * direction
-    block_shape = weight.shape
-    row_ids = lax.broadcasted_iota(jnp.int32, block_shape, 0)
-    col_ids = lax.broadcasted_iota(jnp.int32, block_shape, 1)
-    seed_full = jnp.repeat(jnp.repeat(tile_seeds, tile_side, axis=0), tile_side, axis=1)
-    noise = dither(seed_full, row_ids % tile_side * tile_side + col_ids % tile_side)
     weight_new = moved + jnp.abs(moved) * DITHER_SCALE * noise
     return (outputs, input_grad, weight_new, first_new, second_new)
 

time: 234 us -> 233 us (level)
  waiting for transfers between devices: 101 us -> 96.5 us
  other arithmetic: 24.2 us -> 27.8 us
    reduce_scatter x1, waiting for transfers between devices: 13.8 us -> 0.01 us  [body(): lax.psum_scatter((factor * jnp.dot(grad_band, token_band, preferred_eleme...]
    all_to_all x1, waiting for transfers between devices: 0.01 us -> 9.26 us  [body(): lax.all_to_all(input_part.reshape(size_gx, input_part.shape[0] // size_gx...]
    mul x2 -> x0, local copies, waits for them, and re-layouts: 4.17 us -> none  [the longest x1 2.11 us: body(): first_new = BETA_ONE * first_moment + (1.0 - BETA_ONE) * gradient]
    convert_element_type x0 -> x3, local copies, waits for them, and re-layouts: none -> 4.05 us  [the longest x2 3.13 us: body(): second_moment = place(got_moments[:, tile_side:]).astype(jnp.float32)]
    convert_element_type x0 -> x2, other arithmetic: none -> 2.8 us  [the longest x1 1.68 us: body(): second_moment = place(got_moments[:, tile_side:]).astype(jnp.float32)]
where the time goes in v7:
time: 233 us; the launch traced here: 232 us
  waiting for transfers between devices  96.5 us (41%)
  starting transfers between devices  36 us (15%)
  other arithmetic  27.8 us (12%)
  local copies, waits for them, and re-layouts  26.6 us (11%)
  matrix products  20.3 us (9%)
  between operations  14 us (6%)
  blocking collectives  10.8 us (5%)
    all_to_all x2, waiting for transfers between devices, route(): lax.all_to_all(send, ('gx', 'gz'), split_axis=0, concat_axis=0, tiled=True)  80.8 us
    all_to_all x2, starting transfers between devices, route(): lax.all_to_all(send, ('gx', 'gz'), split_axis=0, concat_axis=0, tiled=True)  15.9 us
    all_gather x1, blocking collectives, body(): grad_band = lax.all_gather(grad_out.T, 'gz', axis=0, tiled=True)  10.8 us
    convert_element_type x2, other arithmetic, route(): send = jnp.take(flat, source, axis=0).astype(jnp.bfloat16)  9.28 us
    all_to_all x1, waiting for transfers between devices, body(): lax.all_to_all(input_part.reshape(size_gx, input_part.shape[0] // size_gx...  9.26 us
    gather x3, local copies, waits for them, and re-layouts, place(): jnp.take(received.reshape(total_slots, tile_side, tile_side), picked, axi...  8.61 us
    all_to_all x1, starting transfers between devices, body(): lax.all_to_all(labels.reshape(group_size, capacity), ('gx', 'gz'), split_...  8.58 us
    dot_general x1, matrix products, body(): jnp.dot(grad_band, token_band, preferred_element_type=jnp.float32)  7.46 us
  transfers between devices with their start and end apart: 8, of which 5 were waited for; matrix products, arithmetic and copies ran while one was open for 27% of the time, Pallas kernels for 0%

profile of v7, /device:TPU:1, one launch (start us, length us, event | category | flops | bytes accessed | tf_op | source)
XLA Modules:
  0.0 232.0 jit_solution(17146917710728522818)
XLA Ops:
  9.6 8.6 %all-to-all-start.1 = ((s32[32,1,2]{2,1,0:T(1,128)}), s32[32,1,2]{2,1,0:T(1,128)S(1)}, u32[]{:S(2)}, u32[]{:S(2)}) async-start(s32[32,1,2]{2,1,0:T(1,128)} %bitcast.3), calls=%async_computation.1 | async-start | bytes 32768 | tf_op jit(solution)/shard_map/all_to_all | solution.py:61
  20.4 3.4 %select_convert_fusion.1 = bf16[32,2,128,128]{3,2,1,0:T(8,128)(2,1)} fusion(bf16[32,2,128,128]{3,2,1,0:T(8,128)(2,1)} %bitcast.53, pred[32,2]{1,0:T(8,128)(4,1)S(1)} %compare_and_fusion), kind=kLoop, calls=%fused_computation.8 | loop fusion | flops 1048576 | bytes 4194368 | tf_op jit(solution)/shard_map/convert_element_type | solution.py:57
  25.1 6.2 %all-to-all-start = ((bf16[32,2,128,128]{3,2,1,0:T(8,128)(2,1)}), bf16[32,2,128,128]{3,2,1,0:T(8,128)(2,1)}, u32[]{:S(2)}, u32[]{:S(2)}) async-start(bf16[32,2,128,128]{3,2,1,0:T(8,128)(2,1)} %select_convert_fusion.1), calls=%async_computation | async-start | bytes 4194304 | tf_op jit(solution)/shard_map/all_to_all | solution.py:59
  32.9 30.5 %all-to-all-done = bf16[32,2,128,128]{3,2,1,0:T(8,128)(2,1)} async-done(((bf16[32,2,128,128]{3,2,1,0:T(8,128)(2,1)}), bf16[32,2,128,128]{3,2,1,0:T(8,128)(2,1)}, u32[]{:S(2)}, u32[]{:S(2)}) %all-to-all-start) | async-done | bytes 2097184 | tf_op jit(solution)/shard_map/all_to_all | solution.py:59
  63.3 2.3 gather_fusion.2
  67.5 10.8 %all_gather.11 = bf16[1024,384]{0,1:T(8,128)(2,1)S(1)} all-gather(bf16[256,384]{0,1:T(8,128)(2,1)S(1)} %bitcast.59), channel_id=1, replica_groups=mesh['gx'=8,'gy'=8,'gz'=4] {'gz'}, dimensions={0}, use_global_device_ids=true | all-gather | bytes 983040 | tf_op jit(solution)/shard_map/all_gather | solution.py:83
  78.3 7.5 %multiply_convert_fusion = bf16[1024,3072]{1,0:T(8,128)(2,1)} fusion(bf16[1024,384]{0,1:T(8,128)(2,1)S(1)} %all_gather.11, bf16[384,3072]{1,0:T(8,128)(2,1)} %all-gather.3.cloned.1.call-done), kind=kOutput, calls=%fused_computation.5 | convolution fusion | flops 2422210560 | bytes 9437184 | tf_op jit(solution)/shard_map/dot_general | solution.py:116
  85.7 2.2 pad_maximum_fusion
  87.9 3.0 %gather_fusion.1 = bf16[64,256,128]{2,1,0:T(8,128)(2,1)} fusion(bf16[24,256,128]{2,1,0:T(8,128)(2,1)S(1)} %pad_maximum_fusion, s32[1024]{0:T(1024)S(1)} %pad_clamp_fusion.1), kind=kCustom, calls=%fused_computation.4 | custom fusion | bytes 8388864 | tf_op jit(solution)/shard_map/jit(_take)/gather | solution.py:57
  90.9 5.9 %select_convert_fusion = bf16[32,2,256,128]{3,2,1,0:T(8,128)(2,1)} fusion(bf16[32,2,256,128]{3,2,1,0:T(8,128)(2,1)} %bitcast.52, pred[32,2]{1,0:T(8,128)(4,1)S(1)} %compare_and_fusion), kind=kLoop, calls=%fused_computation.6 | loop fusion | flops 2097152 | bytes 8388672 | tf_op jit(solution)/shard_map/convert_element_type | solution.py:57
  96.8 9.7 %all-to-all-start.2 = ((bf16[32,2,256,128]{3,2,1,0:T(8,128)(2,1)}), bf16[32,2,256,128]{3,2,1,0:T(8,128)(2,1)}, u32[]{:S(2)}, u32[]{:S(2)}) async-start(bf16[32,2,256,128]{3,2,1,0:T(8,128)(2,1)} %select_convert_fusion), calls=%async_computation.2 | async-start | bytes 8388608 | tf_op jit(solution)/shard_map/all_to_all | solution.py:59
  106.7 50.4 %all-to-all-done.2 = bf16[32,2,256,128]{3,2,1,0:T(8,128)(2,1)} async-done(((bf16[32,2,256,128]{3,2,1,0:T(8,128)(2,1)}), bf16[32,2,256,128]{3,2,1,0:T(8,128)(2,1)}, u32[]{:S(2)}, u32[]{:S(2)}) %all-to-all-start.2) | async-done | bytes 4194336 | tf_op jit(solution)/shard_map/all_to_all | solution.py:59
  157.0 6.1 %multiply_convert_fusion.2 = bf16[384,1024]{1,0:T(8,128)(2,1)S(1)} fusion(bf16[384,3072]{1,0:T(8,128)(2,1)} %all-gather.3.cloned.1.call-done, bf16[1024,3072]{1,0:T(8,128)(2,1)} %all-gather.5.cloned.1.call-done), kind=kOutput, calls=%fused_computation.20 | convolution fusion | flops 2416705536 | bytes 9437184 | tf_op jit(solution)/shard_map/dot_general | solution.py:90
  164.1 5.1 %all-to-all-start.3 = ((bf16[384,4,256]{2,0,1:T(8,128)(2,1)}), bf16[384,4,256]{2,0,1:T(8,128)(2,1)S(1)}, u32[]{:S(2)}, u32[]{:S(2)}) async-start(bf16[384,4,256]{2,0,1:T(8,128)(2,1)} %bitcast.51), calls=%async_computation.3 | async-start | bytes 1572864 | tf_op jit(solution)/shard_map/all_to_all | solution.py:91
  169.2 6.7 %multiply_convert_fusion.1 = bf16[384,3072]{1,0:T(8,128)(2,1)} fusion(bf16[1024,384]{0,1:T(8,128)(2,1)S(1)} %copy-done.5, bf16[1024,3072]{1,0:T(8,128)(2,1)} %all-gather.5.cloned.1.call-done), kind=kOutput, calls=%fused_computation.7 | convolution fusion | flops 2418278400 | bytes 9437184 | tf_op jit(solution)/shard_map/dot_general | solution.py:103
  175.9 4.5 %all-to-all-done.3 = bf16[384,4,256]{2,0,1:T(8,128)(2,1)S(1)} async-done(((bf16[384,4,256]{2,0,1:T(8,128)(2,1)}), bf16[384,4,256]{2,0,1:T(8,128)(2,1)S(1)}, u32[]{:S(2)}, u32[]{:S(2)}) %all-to-all-start.3) | async-done | bytes 786464 | tf_op jit(solution)/shard_map/all_to_all | solution.py:91
  181.3 6.3 %all-to-all-start.4 = ((bf16[8,48,3072]{2,1,0:T(8,128)(2,1)}), bf16[8,48,3072]{2,1,0:T(8,128)(2,1)}, u32[]{:S(2)}, u32[]{:S(2)}) async-start(bf16[8,48,3072]{2,1,0:T(8,128)(2,1)} %bitcast.57), calls=%async_computation.4 | async-start | bytes 4718592 | tf_op jit(solution)/shard_map/all_to_all | solution.py:107
  189.6 5.0 %fusion.13 = (bf16[64,128,128]{2,1,0:T(8,128)(2,1)}, bf16[64,128,128]{2,1,0:T(8,128)(2,1)}) fusion(bf16[64,256,128]{2,1,0:T(8,128)(2,1)} %bitcast.12), kind=kLoop, calls=%fused_computation.61 | loop fusion | bytes 8388608 | tf_op jit(solution)/shard_map/slice | solution.py:88
  194.6 3.2 %gather_fusion.4 = bf16[24,128,128]{2,1,0:T(8,128)(2,1)} fusion(bf16[64,128,128]{2,1,0:T(8,128)(2,1)} %get-tuple-element.37, s32[1024]{0:T(1024)S(1)} %pad_clamp_fusion), kind=kCustom, calls=%fused_computation.2.clone | custom fusion | bytes 1572960 | tf_op jit(solution)/shard_map/jit(_take)/gather | solution.py:73
  197.8 3.1 %gather_fusion.3 = bf16[24,128,128]{2,1,0:T(8,128)(2,1)} fusion(bf16[64,128,128]{2,1,0:T(8,128)(2,1)} %get-tuple-element.38, s32[1024]{0:T(1024)S(1)} %pad_clamp_fusion), kind=kCustom, calls=%fused_computation.1.clone | custom fusion | bytes 1572960 | tf_op jit(solution)/shard_map/jit(_take)/gather | solution.py:73
  204.4 2.2 copy_bitcast_fusion
  207.5 9.3 %all-to-all-done.4 = bf16[8,48,3072]{2,1,0:T(8,128)(2,1)} async-done(((bf16[8,48,3072]{2,1,0:T(8,128)(2,1)}), bf16[8,48,3072]{2,1,0:T(8,128)(2,1)}, u32[]{:S(2)}, u32[]{:S(2)}) %all-to-all-start.4) | async-done | bytes 2359328 | tf_op jit(solution)/shard_map/all_to_all | solution.py:107
  216.7 2.8 %reduce_sum.71 = bf16[48,3072]{1,0:T(8,128)(2,1)} reduce(bf16[8,48,3072]{2,1,0:T(8,128)(2,1)} %all-to-all-done.4, bf16[]{:T(256)} %constant.157.clone.1), dimensions={0}, to_apply=%region_5.7 | reduce | flops 1032192 | bytes 2654210 | tf_op jit(solution)/shard_map/reduce_sum | solution.py:114
  219.6 5.9 %multiply_add_fusion = (f32[128,3072]{1,0:T(8,128)}, f32[128,3072]{1,0:T(8,128)}, f32[128,3072]{1,0:T(8,128)}) fusion(f32[128,3072]{1,0:T(8,128)} %multiply_add_fusion.1, f32[128,3072]{1,0:T(8,128)S(1)} %get-tuple-element.28, bf16[128,3072]{1,0:T(8,128)(2,1)} %reduce-scatter.2.cloned.1.call-done, f32[128,3072]{1,0:T(8,128)} %get-tuple-element.29, ...), kind=kLoop, calls=%fused_computation.18 | loop fusion | flops 7864320 | bytes 11796480 | tf_op jit(solution)/shard_map/add | solution.py:137
  (58 shorter events, 17.5 us)
Async XLA Ops:
  7.2 11.1 %copy-start = (f32[24,128,128]{2,1,0:T(8,128)S(1)}, f32[24,128,128]{2,1,0:T(8,128)}, u32[]{:S(2)}) copy-start(f32[24,128,128]{2,1,0:T(8,128)} %param.9) | copy-start | bytes 4718596
  7.2 56.1 %all-gather.3.cloned.1.call-start = ((), (), s32[]{:S(2)}) async-start(), calls=%async_computation.6 | async-start | bytes 2654208 | tf_op jit(solution)/shard_map/all_gather | solution.py:65
  9.6 15.5 %all-to-all-start.1 = ((s32[32,1,2]{2,1,0:T(1,128)}), s32[32,1,2]{2,1,0:T(1,128)S(1)}, u32[]{:S(2)}, u32[]{:S(2)}) async-start(s32[32,1,2]{2,1,0:T(1,128)} %bitcast.3), calls=%async_computation.1 | async-start | bytes 32768 | tf_op jit(solution)/shard_map/all_to_all | solution.py:61
  25.1 38.3 %all-to-all-start = ((bf16[32,2,128,128]{3,2,1,0:T(8,128)(2,1)}), bf16[32,2,128,128]{3,2,1,0:T(8,128)(2,1)}, u32[]{:S(2)}, u32[]{:S(2)}) async-start(bf16[32,2,128,128]{3,2,1,0:T(8,128)(2,1)} %select_convert_fusion.1), calls=%async_computation | async-start | bytes 4194304 | tf_op jit(solution)/shard_map/all_to_all | solution.py:59
  31.3 125.8 %all-gather.5.cloned.1.call-start = ((), (), s32[]{:S(2)}) async-start(), calls=%async_computation.7 | async-start | bytes 7077888 | tf_op jit(solution)/shard_map/all_gather | solution.py:82
  66.3 1.2 copy-start.6
  67.4 152.1 %reduce-scatter.2.cloned.1.call-start = ((), (), s32[]{:S(2)}) async-start(), calls=%async_computation.8 | async-start | bytes 7077888 | tf_op jit(solution)/shard_map/reduce_scatter | solution.py:115
  78.3 7.5 %copy-start.4 = (bf16[1024,384]{0,1:T(8,128)(2,1)}, bf16[1024,384]{0,1:T(8,128)(2,1)S(1)}, u32[]{:S(2)}) copy-start(bf16[1024,384]{0,1:T(8,128)(2,1)S(1)} %all_gather.11) | copy-start | bytes 2359300
  96.8 9.8 %copy-start.7 = (s32[1,24]{1,0:T(1,128)S(1)}, s32[1,24]{1,0:T(1,128)}, u32[]{:S(2)}) copy-start(s32[1,24]{1,0:T(1,128)} %param.13) | copy-start | bytes 292
  96.8 60.2 %all-to-all-start.2 = ((bf16[32,2,256,128]{3,2,1,0:T(8,128)(2,1)}), bf16[32,2,256,128]{3,2,1,0:T(8,128)(2,1)}, u32[]{:S(2)}, u32[]{:S(2)}) async-start(bf16[32,2,256,128]{3,2,1,0:T(8,128)(2,1)} %select_convert_fusion), calls=%async_computation.2 | async-start | bytes 8388608 | tf_op jit(solution)/shard_map/all_to_all | solution.py:59
  163.1 6.0 %copy-start.5 = (bf16[1024,384]{0,1:T(8,128)(2,1)S(1)}, bf16[1024,384]{0,1:T(8,128)(2,1)}, u32[]{:S(2)}) copy-start(bf16[1024,384]{0,1:T(8,128)(2,1)} %copy-done.4) | copy-start | bytes 2359300
  164.1 16.3 %all-to-all-start.3 = ((bf16[384,4,256]{2,0,1:T(8,128)(2,1)}), bf16[384,4,256]{2,0,1:T(8,128)(2,1)S(1)}, u32[]{:S(2)}, u32[]{:S(2)}) async-start(bf16[384,4,256]{2,0,1:T(8,128)(2,1)} %bitcast.51), calls=%async_computation.3 | async-start | bytes 1572864 | tf_op jit(solution)/shard_map/all_to_all | solution.py:91
  180.4 0.9 copy-start.2
  181.3 35.5 %all-to-all-start.4 = ((bf16[8,48,3072]{2,1,0:T(8,128)(2,1)}), bf16[8,48,3072]{2,1,0:T(8,128)(2,1)}, u32[]{:S(2)}, u32[]{:S(2)}) async-start(bf16[8,48,3072]{2,1,0:T(8,128)(2,1)} %bitcast.57), calls=%async_computation.4 | async-start | bytes 4718592 | tf_op jit(solution)/shard_map/all_to_all | solution.py:107
  204.4 2.2 copy-start.3
  219.6 5.9 %copy-start.1 = (f32[24,128,128]{2,1,0:T(8,128)S(1)}, f32[24,128,128]{2,1,0:T(8,128)}, u32[]{:S(2)}) copy-start(f32[24,128,128]{2,1,0:T(8,128)} %param.9) | copy-start | bytes 4718596
Sparse Core Ops, SparseCore 0:
  9.8 38.3 all-gather.2
  67.6 74.1 all-gather.4
  144.3 73.8 reduce-scatter.1

commit v8 on v7

--- a/solution.py
+++ b/solution.py
@@ -76,11 +76,14 @@
 
     weight_low = place(got_weight)
     weight = weight_low.astype(jnp.float32)
-    flat_first, flat_second, grad_out, weight_low = lax.optimization_barrier(
-        (flat_first, flat_second, grad_out, weight_low)
+    flat_first, flat_second, weight_low = lax.optimization_barrier(
+        (flat_first, flat_second, weight_low)
     )
     weight_band = lax.all_gather(weight_low, "gy", axis=0, tiled=True)
-    grad_band = lax.all_gather(grad_out.T, "gz", axis=0, tiled=True)
+    own_gz = lax.axis_index("gz")
+    grad_band = lax.psum(
+        jnp.zeros((size_gz,) + grad_out.T.shape, grad_out.dtype).at[own_gz].set(grad_out.T), "gz"
+    ).reshape(size_gz * grad_out.shape[1], grad_out.shape[0])
     got_moments = route(jnp.concatenate([flat_first, flat_second], axis=1))
     got_moments, weight_band = lax.optimization_barrier((got_moments, weight_band))
     got_moments = got_moments.reshape(total_slots, 2 * tile_side, tile_side)

time: 233 us -> 247 us (1.060)
  waiting for transfers between devices: 96.5 us -> 118 us
  blocking collectives: 10.8 us -> 0 us
    psum x0 -> x1, waiting for transfers between devices: none -> 24.6 us  [body(): lax.psum(jnp.zeros((size_gz,) + grad_out.T.shape, grad_out.dtype).at[own_...]
    all_gather x1 -> x0, blocking collectives: 10.8 us -> none  [body(): grad_band = lax.all_gather(grad_out.T, 'gz', axis=0, tiled=True)]
    all_to_all x2, waiting for transfers between devices: 80.8 us -> 78.1 us  [route(): lax.all_to_all(send, ('gx', 'gz'), split_axis=0, concat_axis=0, tiled=True)]
  transfers between devices with their start and end apart: 8 -> 9, of which waited for: 5 -> 6; matrix products, arithmetic and copies ran while one was open for 27% -> 28% of each run, Pallas kernels for 0% -> 0%
where the time goes in v8:
time: 247 us; the launch traced here: 246 us
  waiting for transfers between devices  118 us (48%)
  starting transfers between devices  34.6 us (14%)
  other arithmetic  29.2 us (12%)
  local copies, waits for them, and re-layouts  27.7 us (11%)
  matrix products  21.4 us (9%)
  between operations  15.5 us (6%)
    all_to_all x2, waiting for transfers between devices, route(): lax.all_to_all(send, ('gx', 'gz'), split_axis=0, concat_axis=0, tiled=True)  78.1 us
    psum x1, waiting for transfers between devices, body(): lax.psum(jnp.zeros((size_gz,) + grad_out.T.shape, grad_out.dtype).at[own_...  24.6 us
    all_to_all x2, starting transfers between devices, route(): lax.all_to_all(send, ('gx', 'gz'), split_axis=0, concat_axis=0, tiled=True)  14.5 us
    convert_element_type x2, other arithmetic, route(): send = jnp.take(flat, source, axis=0).astype(jnp.bfloat16)  9.28 us
    all_to_all x1, waiting for transfers between devices, body(): lax.all_to_all(input_part.reshape(size_gx, input_part.shape[0] // size_gx...  9.27 us
    gather x3, local copies, waits for them, and re-layouts, place(): jnp.take(received.reshape(total_slots, tile_side, tile_side), picked, axi...  8.62 us
    all_to_all x1, starting transfers between devices, body(): lax.all_to_all(labels.reshape(group_size, capacity), ('gx', 'gz'), split_...  8.58 us
    dot_general x1, matrix products, body(): jnp.dot(grad_band, token_band, preferred_element_type=jnp.float32)  8.01 us
  transfers between devices with their start and end apart: 9, of which 6 were waited for; matrix products, arithmetic and copies ran while one was open for 28% of the time, Pallas kernels for 0%

profile of v8, /device:TPU:1, one launch (start us, length us, event | category | flops | bytes accessed | tf_op | source)
XLA Modules:
  0.0 246.4 jit_solution(11709548990675144225)
XLA Ops:
  10.4 8.6 %all-to-all-start.1 = ((s32[32,1,2]{2,1,0:T(1,128)}), s32[32,1,2]{2,1,0:T(1,128)S(1)}, u32[]{:S(2)}, u32[]{:S(2)}) async-start(s32[32,1,2]{2,1,0:T(1,128)} %bitcast.3), calls=%async_computation.1 | async-start | bytes 32768 | tf_op jit(solution)/shard_map/all_to_all | solution.py:61
  21.3 3.4 %select_convert_fusion.1 = bf16[32,2,128,128]{3,2,1,0:T(8,128)(2,1)} fusion(bf16[32,2,128,128]{3,2,1,0:T(8,128)(2,1)} %bitcast.58, pred[32,2]{1,0:T(8,128)(4,1)S(1)} %compare_and_fusion), kind=kLoop, calls=%fused_computation.8 | loop fusion | flops 1048576 | bytes 4194368 | tf_op jit(solution)/shard_map/convert_element_type | solution.py:57
  25.9 6.3 %all-to-all-start = ((bf16[32,2,128,128]{3,2,1,0:T(8,128)(2,1)}), bf16[32,2,128,128]{3,2,1,0:T(8,128)(2,1)}, u32[]{:S(2)}, u32[]{:S(2)}) async-start(bf16[32,2,128,128]{3,2,1,0:T(8,128)(2,1)} %select_convert_fusion.1), calls=%async_computation | async-start | bytes 4194304 | tf_op jit(solution)/shard_map/all_to_all | solution.py:59
  36.5 27.8 %all-to-all-done = bf16[32,2,128,128]{3,2,1,0:T(8,128)(2,1)} async-done(((bf16[32,2,128,128]{3,2,1,0:T(8,128)(2,1)}), bf16[32,2,128,128]{3,2,1,0:T(8,128)(2,1)}, u32[]{:S(2)}, u32[]{:S(2)}) %all-to-all-start) | async-done | bytes 2097184 | tf_op jit(solution)/shard_map/all_to_all | solution.py:59
  64.3 2.3 gather_fusion.2
  68.4 24.6 %all-reduce.2.cloned.1.call-done = bf16[1024,384]{1,0:T(8,128)(2,1)} async-done(((bf16[1024,384]{1,0:T(8,128)(2,1)}), bf16[1024,384]{1,0:T(8,128)(2,1)}) %all-reduce.2.cloned.1.call-update) | async-done | bytes 786448 | tf_op jit(solution)/shard_map/psum | solution.py:84
  93.1 8.0 %multiply_convert_fusion = bf16[1024,3072]{1,0:T(8,128)(2,1)} fusion(bf16[1024,384]{1,0:T(8,128)(2,1)} %all-reduce.2.cloned.1.call-done, bf16[384,3072]{1,0:T(8,128)(2,1)} %all-gather.3.cloned.1.call-done), kind=kOutput, calls=%fused_computation.5 | convolution fusion | flops 2422210560 | bytes 9437184 | tf_op jit(solution)/shard_map/dot_general | solution.py:119
  101.1 2.2 pad_maximum_fusion
  103.3 3.0 %gather_fusion.1 = bf16[64,256,128]{2,1,0:T(8,128)(2,1)} fusion(bf16[24,256,128]{2,1,0:T(8,128)(2,1)S(1)} %pad_maximum_fusion, s32[1024]{0:T(1024)S(1)} %pad_clamp_fusion.1), kind=kCustom, calls=%fused_computation.4 | custom fusion | bytes 8388864 | tf_op jit(solution)/shard_map/jit(_take)/gather | solution.py:57
  106.3 5.9 %select_convert_fusion = bf16[32,2,256,128]{3,2,1,0:T(8,128)(2,1)} fusion(bf16[32,2,256,128]{3,2,1,0:T(8,128)(2,1)} %bitcast.57, pred[32,2]{1,0:T(8,128)(4,1)S(1)} %compare_and_fusion), kind=kLoop, calls=%fused_computation.6 | loop fusion | flops 2097152 | bytes 8388672 | tf_op jit(solution)/shard_map/convert_element_type | solution.py:57
  112.2 8.1 %all-to-all-start.2 = ((bf16[32,2,256,128]{3,2,1,0:T(8,128)(2,1)}), bf16[32,2,256,128]{3,2,1,0:T(8,128)(2,1)}, u32[]{:S(2)}, u32[]{:S(2)}) async-start(bf16[32,2,256,128]{3,2,1,0:T(8,128)(2,1)} %select_convert_fusion), calls=%async_computation.2 | async-start | bytes 8388608 | tf_op jit(solution)/shard_map/all_to_all | solution.py:59
  120.4 50.4 %all-to-all-done.2 = bf16[32,2,256,128]{3,2,1,0:T(8,128)(2,1)} async-done(((bf16[32,2,256,128]{3,2,1,0:T(8,128)(2,1)}), bf16[32,2,256,128]{3,2,1,0:T(8,128)(2,1)}, u32[]{:S(2)}, u32[]{:S(2)}) %all-to-all-start.2) | async-done | bytes 4194336 | tf_op jit(solution)/shard_map/all_to_all | solution.py:59
  170.8 6.2 %multiply_convert_fusion.2 = bf16[384,1024]{1,0:T(8,128)(2,1)S(1)} fusion(bf16[384,3072]{1,0:T(8,128)(2,1)} %all-gather.3.cloned.1.call-done, bf16[1024,3072]{1,0:T(8,128)(2,1)} %all-gather.5.cloned.1.call-done), kind=kOutput, calls=%fused_computation.20 | convolution fusion | flops 2416705536 | bytes 9437184 | tf_op jit(solution)/shard_map/dot_general | solution.py:93
  177.9 5.1 %all-to-all-start.3 = ((bf16[384,4,256]{2,0,1:T(8,128)(2,1)}), bf16[384,4,256]{2,0,1:T(8,128)(2,1)S(1)}, u32[]{:S(2)}, u32[]{:S(2)}) async-start(bf16[384,4,256]{2,0,1:T(8,128)(2,1)} %bitcast.56), calls=%async_computation.3 | async-start | bytes 1572864 | tf_op jit(solution)/shard_map/all_to_all | solution.py:94
  183.0 7.2 %multiply_convert_fusion.1 = bf16[384,3072]{1,0:T(8,128)(2,1)} fusion(bf16[1024,384]{1,0:T(8,128)(2,1)} %all-reduce.2.cloned.1.call-done, bf16[1024,3072]{1,0:T(8,128)(2,1)} %all-gather.5.cloned.1.call-done), kind=kOutput, calls=%fused_computation.7 | convolution fusion | flops 2418278400 | bytes 9437184 | tf_op jit(solution)/shard_map/dot_general | solution.py:106
  190.2 4.0 %all-to-all-done.3 = bf16[384,4,256]{2,0,1:T(8,128)(2,1)S(1)} async-done(((bf16[384,4,256]{2,0,1:T(8,128)(2,1)}), bf16[384,4,256]{2,0,1:T(8,128)(2,1)S(1)}, u32[]{:S(2)}, u32[]{:S(2)}) %all-to-all-start.3) | async-done | bytes 786464 | tf_op jit(solution)/shard_map/all_to_all | solution.py:94
  195.1 6.3 %all-to-all-start.4 = ((bf16[8,48,3072]{2,1,0:T(8,128)(2,1)}), bf16[8,48,3072]{2,1,0:T(8,128)(2,1)}, u32[]{:S(2)}, u32[]{:S(2)}) async-start(bf16[8,48,3072]{2,1,0:T(8,128)(2,1)} %bitcast.63), calls=%async_computation.4 | async-start | bytes 4718592 | tf_op jit(solution)/shard_map/all_to_all | solution.py:110
  203.4 5.0 %fusion.13 = (bf16[64,128,128]{2,1,0:T(8,128)(2,1)}, bf16[64,128,128]{2,1,0:T(8,128)(2,1)}) fusion(bf16[64,256,128]{2,1,0:T(8,128)(2,1)} %bitcast.15), kind=kLoop, calls=%fused_computation.63 | loop fusion | bytes 8388608 | tf_op jit(solution)/shard_map/slice | solution.py:91
  208.4 3.2 %gather_fusion.4 = bf16[24,128,128]{2,1,0:T(8,128)(2,1)} fusion(bf16[64,128,128]{2,1,0:T(8,128)(2,1)} %get-tuple-element.47, s32[1024]{0:T(1024)S(1)} %pad_clamp_fusion), kind=kCustom, calls=%fused_computation.2.clone | custom fusion | bytes 1572960 | tf_op jit(solution)/shard_map/jit(_take)/gather | solution.py:73
  211.6 3.2 %gather_fusion.3 = bf16[24,128,128]{2,1,0:T(8,128)(2,1)} fusion(bf16[64,128,128]{2,1,0:T(8,128)(2,1)} %get-tuple-element.48, s32[1024]{0:T(1024)S(1)} %pad_clamp_fusion), kind=kCustom, calls=%fused_computation.1.clone | custom fusion | bytes 1572960 | tf_op jit(solution)/shard_map/jit(_take)/gather | solution.py:73
  218.3 2.2 copy_bitcast_fusion
  221.3 9.3 %all-to-all-done.4 = bf16[8,48,3072]{2,1,0:T(8,128)(2,1)} async-done(((bf16[8,48,3072]{2,1,0:T(8,128)(2,1)}), bf16[8,48,3072]{2,1,0:T(8,128)(2,1)}, u32[]{:S(2)}, u32[]{:S(2)}) %all-to-all-start.4) | async-done | bytes 2359328 | tf_op jit(solution)/shard_map/all_to_all | solution.py:110
  230.6 2.8 %reduce_sum.71 = bf16[48,3072]{1,0:T(8,128)(2,1)} reduce(bf16[8,48,3072]{2,1,0:T(8,128)(2,1)} %all-to-all-done.4, bf16[]{:T(256)} %constant.181.clone.1), dimensions={0}, to_apply=%region_7.9 | reduce | flops 1032192 | bytes 2654210 | tf_op jit(solution)/shard_map/reduce_sum | solution.py:117
  233.4 5.9 %multiply_add_fusion = (f32[128,3072]{1,0:T(8,128)}, f32[128,3072]{1,0:T(8,128)}, f32[128,3072]{1,0:T(8,128)}) fusion(f32[128,3072]{1,0:T(8,128)} %multiply_add_fusion.1, f32[128,3072]{1,0:T(8,128)S(1)} %get-tuple-element.38, bf16[128,3072]{1,0:T(8,128)(2,1)} %reduce-scatter.2.cloned.1.call-done, f32[128,3072]{1,0:T(8,128)} %get-tuple-element.39, ...), kind=kLoop, calls=%fused_computation.18 | loop fusion | flops 7864320 | bytes 11796480 | tf_op jit(solution)/shard_map/add | solution.py:140
  (64 shorter events, 20.0 us)
Async XLA Ops:
  8.0 11.1 %copy-start = (f32[24,128,128]{2,1,0:T(8,128)S(1)}, f32[24,128,128]{2,1,0:T(8,128)}, u32[]{:S(2)}) copy-start(f32[24,128,128]{2,1,0:T(8,128)} %param.11) | copy-start | bytes 4718596
  8.0 56.2 %all-gather.3.cloned.1.call-start = ((), (), s32[]{:S(2)}) async-start(), calls=%async_computation.6 | async-start | bytes 2654208 | tf_op jit(solution)/shard_map/all_gather | solution.py:65
  10.4 15.5 %all-to-all-start.1 = ((s32[32,1,2]{2,1,0:T(1,128)}), s32[32,1,2]{2,1,0:T(1,128)S(1)}, u32[]{:S(2)}, u32[]{:S(2)}) async-start(s32[32,1,2]{2,1,0:T(1,128)} %bitcast.3), calls=%async_computation.1 | async-start | bytes 32768 | tf_op jit(solution)/shard_map/all_to_all | solution.py:61
  24.7 7.6 %copy-start.5 = (bf16[384,256]{1,0:T(8,128)(2,1)S(1)}, bf16[384,256]{1,0:T(8,128)(2,1)}, u32[]{:S(2)}) copy-start(bf16[384,256]{1,0:T(8,128)(2,1)} %param.17) | copy-start | bytes 589828
  24.7 7.8 %copy-start.7 = (s32[3]{0:T(128)S(1)}, s32[3]{0:T(128)}, u32[]{:S(2)}) copy-start(s32[3]{0:T(128)} %constant.196.clone.1) | copy-start | bytes 40
  25.9 38.4 %all-to-all-start = ((bf16[32,2,128,128]{3,2,1,0:T(8,128)(2,1)}), bf16[32,2,128,128]{3,2,1,0:T(8,128)(2,1)}, u32[]{:S(2)}, u32[]{:S(2)}) async-start(bf16[32,2,128,128]{3,2,1,0:T(8,128)(2,1)} %select_convert_fusion.1), calls=%async_computation | async-start | bytes 4194304 | tf_op jit(solution)/shard_map/all_to_all | solution.py:59
  32.2 60.8 %all-reduce.2.cloned.1.call-start = ((), (), s32[]{:S(2)}) async-start(), calls=%async_computation.8 | async-start | bytes 1572864 | tf_op jit(solution)/shard_map/psum | solution.py:84
  34.0 0.9 copy-start.4
  34.9 135.9 %all-gather.5.cloned.1.call-start = ((), (), s32[]{:S(2)}) async-start(), calls=%async_computation.7 | async-start | bytes 7077888 | tf_op jit(solution)/shard_map/all_gather | solution.py:82
  68.4 165.0 %reduce-scatter.2.cloned.1.call-start = ((), (), s32[]{:S(2)}) async-start(), calls=%async_computation.9 | async-start | bytes 7077888 | tf_op jit(solution)/shard_map/reduce_scatter | solution.py:118
  112.2 8.2 %copy-start.6 = (s32[1,24]{1,0:T(1,128)S(1)}, s32[1,24]{1,0:T(1,128)}, u32[]{:S(2)}) copy-start(s32[1,24]{1,0:T(1,128)} %param.15) | copy-start | bytes 292
  112.2 58.6 %all-to-all-start.2 = ((bf16[32,2,256,128]{3,2,1,0:T(8,128)(2,1)}), bf16[32,2,256,128]{3,2,1,0:T(8,128)(2,1)}, u32[]{:S(2)}, u32[]{:S(2)}) async-start(bf16[32,2,256,128]{3,2,1,0:T(8,128)(2,1)} %select_convert_fusion), calls=%async_computation.2 | async-start | bytes 8388608 | tf_op jit(solution)/shard_map/all_to_all | solution.py:59
  177.9 16.2 %all-to-all-start.3 = ((bf16[384,4,256]{2,0,1:T(8,128)(2,1)}), bf16[384,4,256]{2,0,1:T(8,128)(2,1)S(1)}, u32[]{:S(2)}, u32[]{:S(2)}) async-start(bf16[384,4,256]{2,0,1:T(8,128)(2,1)} %bitcast.56), calls=%async_computation.3 | async-start | bytes 1572864 | tf_op jit(solution)/shard_map/all_to_all | solution.py:94
  194.2 0.9 copy-start.2
  195.1 35.5 %all-to-all-start.4 = ((bf16[8,48,3072]{2,1,0:T(8,128)(2,1)}), bf16[8,48,3072]{2,1,0:T(8,128)(2,1)}, u32[]{:S(2)}, u32[]{:S(2)}) async-start(bf16[8,48,3072]{2,1,0:T(8,128)(2,1)} %bitcast.63), calls=%async_computation.4 | async-start | bytes 4718592 | tf_op jit(solution)/shard_map/all_to_all | solution.py:110
  218.2 2.2 copy-start.3
  233.4 5.9 %copy-start.1 = (f32[24,128,128]{2,1,0:T(8,128)S(1)}, f32[24,128,128]{2,1,0:T(8,128)}, u32[]{:S(2)}) copy-start(f32[24,128,128]{2,1,0:T(8,128)} %param.11) | copy-start | bytes 4718596
Sparse Core Ops, SparseCore 0:
  10.7 38.2 all-gather.2
  68.5 74.1 all-gather.4
  145.2 73.8 reduce-scatter.1
Sparse Core Ops, SparseCore 1:
  35.7 57.3 all-reduce.1

commit v9 on v7

--- a/solution.py
+++ b/solution.py
@@ -53,17 +53,25 @@
     source = jnp.sum(matches * ordinal[None, :], axis=1)
     labels = jnp.sum(matches * (local_tile[None, :] + 1), axis=1)
 
-    def route(flat):
-        send = jnp.take(flat, source, axis=0).astype(jnp.bfloat16)
-        send = send.reshape(group_size, capacity, *flat.shape[1:])
+    def exchange(send):
+        send = send.reshape(group_size, capacity, *send.shape[1:])
         return lax.all_to_all(send, ("gx", "gz"), split_axis=0, concat_axis=0, tiled=True)
 
     got_labels = lax.all_to_all(
         labels.reshape(group_size, capacity), ("gx", "gz"), split_axis=0, concat_axis=0, tiled=True
     )
-    got_weight = route(flat_weight)
+    send_weight = jnp.take(flat_weight, source, axis=0).astype(jnp.bfloat16)
+    send_weight, flat_first, flat_second = lax.optimization_barrier(
+        (send_weight, flat_first, flat_second)
+    )
+    got_weight = exchange(send_weight)
+    send_moments = jnp.take(
+        jnp.concatenate([flat_first, flat_second], axis=1), source, axis=0
+    ).astype(jnp.bfloat16)
     token_band = lax.all_gather(tokens, "gx", axis=0, tiled=True)
-    got_weight, token_band = lax.optimization_barrier((got_weight, token_band))
+    got_weight, token_band, send_moments = lax.optimization_barrier(
+        (got_weight, token_band, send_moments)
+    )
     got_labels = got_labels.reshape(total_slots)
     wanted = jnp.arange(1, tiles_own + 1, dtype=jnp.int32)
     hits = (got_labels[None, :] == wanted[:, None]).astype(jnp.int32)
@@ -76,12 +84,12 @@
 
     weight_low = place(got_weight)
     weight = weight_low.astype(jnp.float32)
-    flat_first, flat_second, grad_out, weight_low = lax.optimization_barrier(
-        (flat_first, flat_second, grad_out, weight_low)
+    send_moments, grad_out, weight_low = lax.optimization_barrier(
+        (send_moments, grad_out, weight_low)
     )
     weight_band = lax.all_gather(weight_low, "gy", axis=0, tiled=True)
     grad_band = lax.all_gather(grad_out.T, "gz", axis=0, tiled=True)
-    got_moments = route(jnp.concatenate([flat_first, flat_second], axis=1))
+    got_moments = exchange(send_moments)
     got_moments, weight_band = lax.optimization_barrier((got_moments, weight_band))
     got_moments = got_moments.reshape(total_slots, 2 * tile_side, tile_side)
     first_moment = place(got_moments[:, :tile_side]).astype(jnp.float32)

time: 233 us -> 231 us (level)
    reduce_scatter x1, waiting for transfers between devices: 0.01 us -> 10.9 us  [body(): lax.psum_scatter((factor * jnp.dot(grad_band, token_band, preferred_eleme...]
    all_to_all x2, waiting for transfers between devices: 80.8 us -> 70.1 us  [exchange(): lax.all_to_all(send, ('gx', 'gz'), split_axis=0, concat_axis=0, tiled=True)]
  transfers between devices with their start and end apart: 8 -> 8, of which waited for: 5 -> 6; matrix products, arithmetic and copies ran while one was open for 27% -> 27% of each run, Pallas kernels for 0% -> 0%
where the time goes in v9:
time: 231 us
  waiting for transfers between devices  96.9 us (42%)
  starting transfers between devices  35 us (15%)
  other arithmetic  27.4 us (12%)
  local copies, waits for them, and re-layouts  26.5 us (11%)
  matrix products  20 us (9%)
  between operations  14 us (6%)
  blocking collectives  10.7 us (5%)
    all_to_all x2, waiting for transfers between devices, exchange(): lax.all_to_all(send, ('gx', 'gz'), split_axis=0, concat_axis=0, tiled=True)  70.1 us
    all_to_all x2, starting transfers between devices, exchange(): lax.all_to_all(send, ('gx', 'gz'), split_axis=0, concat_axis=0, tiled=True)  14.9 us
    reduce_scatter x1, waiting for transfers between devices, body(): lax.psum_scatter((factor * jnp.dot(grad_band, token_band, preferred_eleme...  10.9 us
    all_gather x1, blocking collectives, body(): grad_band = lax.all_gather(grad_out.T, 'gz', axis=0, tiled=True)  10.7 us
    all_to_all x1, waiting for transfers between devices, body(): lax.all_to_all(input_part.reshape(size_gx, input_part.shape[0] // size_gx...  9.29 us
    gather x3, local copies, waits for them, and re-layouts, place(): jnp.take(received.reshape(total_slots, tile_side, tile_side), picked, axi...  8.61 us
    all_to_all x1, starting transfers between devices, body(): lax.all_to_all(labels.reshape(group_size, capacity), ('gx', 'gz'), split_...  8.58 us
    dot_general x1, matrix products, body(): jnp.dot(grad_band, token_band, preferred_element_type=jnp.float32)  7.26 us
  transfers between devices with their start and end apart: 8, of which 6 were waited for; matrix products, arithmetic and copies ran while one was open for 27% of the time, Pallas kernels for 0%

profile of v9, /device:TPU:1, one launch (start us, length us, event | category | flops | bytes accessed | tf_op | source)
XLA Modules:
  0.0 230.6 jit_solution(17916592344385656348)
XLA Ops:
  9.6 8.6 %all-to-all-start.1 = ((s32[32,1,2]{2,1,0:T(1,128)}), s32[32,1,2]{2,1,0:T(1,128)S(1)}, u32[]{:S(2)}, u32[]{:S(2)}) async-start(s32[32,1,2]{2,1,0:T(1,128)} %bitcast.3), calls=%async_computation.1 | async-start | bytes 32768 | tf_op jit(solution)/shard_map/all_to_all | solution.py:60
  20.3 3.4 %select_convert_fusion.1 = bf16[64,128,128]{2,1,0:T(8,128)(2,1)} fusion(bf16[64,128,128]{2,1,0:T(8,128)(2,1)} %gather_fusion, pred[64]{0:T(512)(128)(4,1)S(1)} %compare_and_fusion.2), kind=kLoop, calls=%fused_computation.8 | loop fusion | flops 1048576 | bytes 4194368 | tf_op jit(solution)/shard_map/convert_element_type | solution.py:63
  25.1 6.2 %all-to-all-start = ((bf16[32,2,128,128]{3,2,1,0:T(8,128)(2,1)}), bf16[32,2,128,128]{3,2,1,0:T(8,128)(2,1)}, u32[]{:S(2)}, u32[]{:S(2)}) async-start(bf16[32,2,128,128]{3,2,1,0:T(8,128)(2,1)} %bitcast.53), calls=%async_computation | async-start | bytes 4194304 | tf_op jit(solution)/shard_map/all_to_all | solution.py:58
  33.1 3.0 %gather_fusion.1 = bf16[64,256,128]{2,1,0:T(8,128)(2,1)} fusion(bf16[24,256,128]{2,1,0:T(8,128)(2,1)S(1)} %pad_maximum_fusion, s32[1024]{0:T(1024)S(1)} %pad_clamp_fusion.1), kind=kCustom, calls=%fused_computation.4 | custom fusion | bytes 8388864 | tf_op jit(solution)/shard_map/jit(_take)/gather | solution.py:68
  36.1 5.9 %select_convert_fusion = bf16[64,256,128]{2,1,0:T(8,128)(2,1)} fusion(bf16[64,256,128]{2,1,0:T(8,128)(2,1)} %gather_fusion.1, pred[64]{0:T(512)(128)(4,1)S(1)} %compare_and_fusion.2), kind=kLoop, calls=%fused_computation.6 | loop fusion | flops 2097152 | bytes 8388672 | tf_op jit(solution)/shard_map/convert_element_type | solution.py:70
  43.5 19.8 %all-to-all-done = bf16[32,2,128,128]{3,2,1,0:T(8,128)(2,1)} async-done(((bf16[32,2,128,128]{3,2,1,0:T(8,128)(2,1)}), bf16[32,2,128,128]{3,2,1,0:T(8,128)(2,1)}, u32[]{:S(2)}, u32[]{:S(2)}) %all-to-all-start) | async-done | bytes 2097184 | tf_op jit(solution)/shard_map/all_to_all | solution.py:58
  63.3 2.3 gather_fusion.2
  67.5 10.7 %all_gather.11 = bf16[1024,384]{0,1:T(8,128)(2,1)S(1)} all-gather(bf16[256,384]{0,1:T(8,128)(2,1)S(1)} %bitcast.59), channel_id=1, replica_groups=mesh['gx'=8,'gy'=8,'gz'=4] {'gz'}, dimensions={0}, use_global_device_ids=true | all-gather | bytes 983040 | tf_op jit(solution)/shard_map/all_gather | solution.py:91
  78.3 7.3 %multiply_convert_fusion = bf16[1024,3072]{1,0:T(8,128)(2,1)} fusion(bf16[1024,384]{0,1:T(8,128)(2,1)S(1)} %all_gather.11, bf16[384,3072]{1,0:T(8,128)(2,1)} %all-gather.3.cloned.1.call-done), kind=kOutput, calls=%fused_computation.5 | convolution fusion | flops 2422210560 | bytes 9437184 | tf_op jit(solution)/shard_map/dot_general | solution.py:124
  85.6 8.7 %all-to-all-start.2 = ((bf16[32,2,256,128]{3,2,1,0:T(8,128)(2,1)}), bf16[32,2,256,128]{3,2,1,0:T(8,128)(2,1)}, u32[]{:S(2)}, u32[]{:S(2)}) async-start(bf16[32,2,256,128]{3,2,1,0:T(8,128)(2,1)} %bitcast.52), calls=%async_computation.2 | async-start | bytes 8388608 | tf_op jit(solution)/shard_map/all_to_all | solution.py:58
  94.4 50.4 %all-to-all-done.2 = bf16[32,2,256,128]{3,2,1,0:T(8,128)(2,1)} async-done(((bf16[32,2,256,128]{3,2,1,0:T(8,128)(2,1)}), bf16[32,2,256,128]{3,2,1,0:T(8,128)(2,1)}, u32[]{:S(2)}, u32[]{:S(2)}) %all-to-all-start.2) | async-done | bytes 4194336 | tf_op jit(solution)/shard_map/all_to_all | solution.py:58
  144.8 6.1 %multiply_convert_fusion.2 = bf16[384,1024]{1,0:T(8,128)(2,1)S(1)} fusion(bf16[384,3072]{1,0:T(8,128)(2,1)} %all-gather.3.cloned.1.call-done, bf16[1024,3072]{1,0:T(8,128)(2,1)} %all-gather.5.cloned.1.call-done), kind=kOutput, calls=%fused_computation.20 | convolution fusion | flops 2416705536 | bytes 9437184 | tf_op jit(solution)/shard_map/dot_general | solution.py:98
  151.8 5.1 %all-to-all-start.3 = ((bf16[384,4,256]{2,0,1:T(8,128)(2,1)}), bf16[384,4,256]{2,0,1:T(8,128)(2,1)S(1)}, u32[]{:S(2)}, u32[]{:S(2)}) async-start(bf16[384,4,256]{2,0,1:T(8,128)(2,1)} %bitcast.51), calls=%async_computation.3 | async-start | bytes 1572864 | tf_op jit(solution)/shard_map/all_to_all | solution.py:99
  156.9 6.6 %multiply_convert_fusion.1 = bf16[384,3072]{1,0:T(8,128)(2,1)} fusion(bf16[1024,384]{0,1:T(8,128)(2,1)S(1)} %all_gather.11, bf16[1024,3072]{1,0:T(8,128)(2,1)} %all-gather.5.cloned.1.call-done), kind=kOutput, calls=%fused_computation.7 | convolution fusion | flops 2418278400 | bytes 9437184 | tf_op jit(solution)/shard_map/dot_general | solution.py:111
  163.5 4.5 %all-to-all-done.3 = bf16[384,4,256]{2,0,1:T(8,128)(2,1)S(1)} async-done(((bf16[384,4,256]{2,0,1:T(8,128)(2,1)}), bf16[384,4,256]{2,0,1:T(8,128)(2,1)S(1)}, u32[]{:S(2)}, u32[]{:S(2)}) %all-to-all-start.3) | async-done | bytes 786464 | tf_op jit(solution)/shard_map/all_to_all | solution.py:99
  168.9 6.3 %all-to-all-start.4 = ((bf16[8,48,3072]{2,1,0:T(8,128)(2,1)}), bf16[8,48,3072]{2,1,0:T(8,128)(2,1)}, u32[]{:S(2)}, u32[]{:S(2)}) async-start(bf16[8,48,3072]{2,1,0:T(8,128)(2,1)} %bitcast.57), calls=%async_computation.4 | async-start | bytes 4718592 | tf_op jit(solution)/shard_map/all_to_all | solution.py:115
  177.3 5.0 %fusion.13 = (bf16[64,128,128]{2,1,0:T(8,128)(2,1)}, bf16[64,128,128]{2,1,0:T(8,128)(2,1)}) fusion(bf16[64,256,128]{2,1,0:T(8,128)(2,1)} %bitcast.12), kind=kLoop, calls=%fused_computation.61 | loop fusion | bytes 8388608 | tf_op jit(solution)/shard_map/slice | solution.py:96
  182.2 3.2 %gather_fusion.4 = bf16[24,128,128]{2,1,0:T(8,128)(2,1)} fusion(bf16[64,128,128]{2,1,0:T(8,128)(2,1)} %get-tuple-element.43, s32[1024]{0:T(1024)S(1)} %pad_clamp_fusion), kind=kCustom, calls=%fused_computation.2.clone | custom fusion | bytes 1572960 | tf_op jit(solution)/shard_map/jit(_take)/gather | solution.py:81
  185.4 3.2 %gather_fusion.3 = bf16[24,128,128]{2,1,0:T(8,128)(2,1)} fusion(bf16[64,128,128]{2,1,0:T(8,128)(2,1)} %get-tuple-element.44, s32[1024]{0:T(1024)S(1)} %pad_clamp_fusion), kind=kCustom, calls=%fused_computation.1.clone | custom fusion | bytes 1572960 | tf_op jit(solution)/shard_map/jit(_take)/gather | solution.py:81
  192.1 2.2 copy_bitcast_fusion
  195.1 9.3 %all-to-all-done.4 = bf16[8,48,3072]{2,1,0:T(8,128)(2,1)} async-done(((bf16[8,48,3072]{2,1,0:T(8,128)(2,1)}), bf16[8,48,3072]{2,1,0:T(8,128)(2,1)}, u32[]{:S(2)}, u32[]{:S(2)}) %all-to-all-start.4) | async-done | bytes 2359328 | tf_op jit(solution)/shard_map/all_to_all | solution.py:115
  204.4 2.8 %reduce_sum.68 = bf16[48,3072]{1,0:T(8,128)(2,1)} reduce(bf16[8,48,3072]{2,1,0:T(8,128)(2,1)} %all-to-all-done.4, bf16[]{:T(256)} %constant.157.clone.1), dimensions={0}, to_apply=%region_5.7 | reduce | flops 1032192 | bytes 2654210 | tf_op jit(solution)/shard_map/reduce_sum | solution.py:122
  207.2 10.9 %reduce-scatter.2.cloned.1.call-done = bf16[128,3072]{1,0:T(8,128)(2,1)} async-done(((bf16[1024,3072]{1,0:T(8,128)(2,1)}), bf16[128,3072]{1,0:T(8,128)(2,1)}) %reduce-scatter.2.cloned.1.call-update) | async-done | bytes 786448 | tf_op jit(solution)/shard_map/reduce_scatter | solution.py:123
  218.2 5.9 %multiply_add_fusion = (f32[128,3072]{1,0:T(8,128)}, f32[128,3072]{1,0:T(8,128)}, f32[128,3072]{1,0:T(8,128)}) fusion(f32[128,3072]{1,0:T(8,128)} %multiply_add_fusion.1, f32[128,3072]{1,0:T(8,128)S(1)} %get-tuple-element.34, bf16[128,3072]{1,0:T(8,128)(2,1)} %reduce-scatter.2.cloned.1.call-done, f32[128,3072]{1,0:T(8,128)} %get-tuple-element.35, ...), kind=kLoop, calls=%fused_computation.18 | loop fusion | flops 7864320 | bytes 11796480 | tf_op jit(solution)/shard_map/add | solution.py:145
  (55 shorter events, 19.2 us)
Async XLA Ops:
  7.2 11.0 %copy-start = (f32[24,128,128]{2,1,0:T(8,128)S(1)}, f32[24,128,128]{2,1,0:T(8,128)}, u32[]{:S(2)}) copy-start(f32[24,128,128]{2,1,0:T(8,128)} %param.9) | copy-start | bytes 4718596
  7.2 56.1 %all-gather.3.cloned.1.call-start = ((), (), s32[]{:S(2)}) async-start(), calls=%async_computation.6 | async-start | bytes 2654208 | tf_op jit(solution)/shard_map/all_gather | solution.py:71
  9.6 15.5 %all-to-all-start.1 = ((s32[32,1,2]{2,1,0:T(1,128)}), s32[32,1,2]{2,1,0:T(1,128)S(1)}, u32[]{:S(2)}, u32[]{:S(2)}) async-start(s32[32,1,2]{2,1,0:T(1,128)} %bitcast.3), calls=%async_computation.1 | async-start | bytes 32768 | tf_op jit(solution)/shard_map/all_to_all | solution.py:60
  25.1 6.3 %copy-start.4 = (f32[24,128,128]{2,1,0:T(8,128)S(1)}, f32[24,128,128]{2,1,0:T(8,128)}, u32[]{:S(2)}) copy-start(f32[24,128,128]{2,1,0:T(8,128)} %param.11) | copy-start | bytes 4718596
  25.1 38.3 %all-to-all-start = ((bf16[32,2,128,128]{3,2,1,0:T(8,128)(2,1)}), bf16[32,2,128,128]{3,2,1,0:T(8,128)(2,1)}, u32[]{:S(2)}, u32[]{:S(2)}) async-start(bf16[32,2,128,128]{3,2,1,0:T(8,128)(2,1)} %bitcast.53), calls=%async_computation | async-start | bytes 4194304 | tf_op jit(solution)/shard_map/all_to_all | solution.py:58
  31.3 113.5 %all-gather.5.cloned.1.call-start = ((), (), s32[]{:S(2)}) async-start(), calls=%async_computation.7 | async-start | bytes 7077888 | tf_op jit(solution)/shard_map/all_gather | solution.py:90
  66.3 1.2 copy-start.5
  67.4 150.7 %reduce-scatter.2.cloned.1.call-start = ((), (), s32[]{:S(2)}) async-start(), calls=%async_computation.8 | async-start | bytes 7077888 | tf_op jit(solution)/shard_map/reduce_scatter | solution.py:123
  85.5 8.8 %copy-start.6 = (s32[1,24]{1,0:T(1,128)S(1)}, s32[1,24]{1,0:T(1,128)}, u32[]{:S(2)}) copy-start(s32[1,24]{1,0:T(1,128)} %param.13) | copy-start | bytes 292
  85.6 59.2 %all-to-all-start.2 = ((bf16[32,2,256,128]{3,2,1,0:T(8,128)(2,1)}), bf16[32,2,256,128]{3,2,1,0:T(8,128)(2,1)}, u32[]{:S(2)}, u32[]{:S(2)}) async-start(bf16[32,2,256,128]{3,2,1,0:T(8,128)(2,1)} %bitcast.52), calls=%async_computation.2 | async-start | bytes 8388608 | tf_op jit(solution)/shard_map/all_to_all | solution.py:58
  151.8 16.2 %all-to-all-start.3 = ((bf16[384,4,256]{2,0,1:T(8,128)(2,1)}), bf16[384,4,256]{2,0,1:T(8,128)(2,1)S(1)}, u32[]{:S(2)}, u32[]{:S(2)}) async-start(bf16[384,4,256]{2,0,1:T(8,128)(2,1)} %bitcast.51), calls=%async_computation.3 | async-start | bytes 1572864 | tf_op jit(solution)/shard_map/all_to_all | solution.py:99
  168.0 0.9 copy-start.2
  168.9 35.5 %all-to-all-start.4 = ((bf16[8,48,3072]{2,1,0:T(8,128)(2,1)}), bf16[8,48,3072]{2,1,0:T(8,128)(2,1)}, u32[]{:S(2)}, u32[]{:S(2)}) async-start(bf16[8,48,3072]{2,1,0:T(8,128)(2,1)} %bitcast.57), calls=%async_computation.4 | async-start | bytes 4718592 | tf_op jit(solution)/shard_map/all_to_all | solution.py:115
  192.1 2.2 copy-start.3
  218.2 5.9 %copy-start.1 = (f32[24,128,128]{2,1,0:T(8,128)S(1)}, f32[24,128,128]{2,1,0:T(8,128)}, u32[]{:S(2)}) copy-start(f32[24,128,128]{2,1,0:T(8,128)} %param.9) | copy-start | bytes 4718596
Sparse Core Ops, SparseCore 0:
  9.8 38.3 all-gather.2
  67.6 74.1 all-gather.4
  144.3 73.8 reduce-scatter.1

commit v10 on v9

--- a/solution.py
+++ b/solution.py
@@ -92,8 +92,8 @@
     got_moments = exchange(send_moments)
     got_moments, weight_band = lax.optimization_barrier((got_moments, weight_band))
     got_moments = got_moments.reshape(total_slots, 2 * tile_side, tile_side)
-    first_moment = place(got_moments[:, :tile_side]).astype(jnp.float32)
-    second_moment = place(got_moments[:, tile_side:]).astype(jnp.float32)
+    first_low = place(got_moments[:, :tile_side])
+    second_low = place(got_moments[:, tile_side:])
     factor = 1.0 / math.sqrt(D)
     partial_out = factor * jnp.dot(token_band, weight_band.T, preferred_element_type=jnp.float32)
     out_parts = lax.all_to_all(
@@ -132,10 +132,13 @@
     row_ids = lax.broadcasted_iota(jnp.int32, block_shape, 0)
     col_ids = lax.broadcasted_iota(jnp.int32, block_shape, 1)
     seed_full = jnp.repeat(jnp.repeat(tile_seeds, tile_side, axis=0), tile_side, axis=1)
+    input_grad, first_low, second_low, weight_low = lax.optimization_barrier(
+        (input_grad, first_low, second_low, weight_low)
+    )
+    first_moment = first_low.astype(jnp.float32)
+    second_moment = second_low.astype(jnp.float32)
+    weight = weight_low.astype(jnp.float32)
     noise = dither(seed_full, row_ids % tile_side * tile_side + col_ids % tile_side)
-    noise, input_grad, first_moment, second_moment, weight = lax.optimization_barrier(
-        (noise, input_grad, first_moment, second_moment, weight)
-    )
     first_new = BETA_ONE * first_moment + (1.0 - BETA_ONE) * gradient
     second_new = BETA_TWO * second_moment + (1.0 - BETA_TWO) * gradient * gradient
     direction = (

time: 231 us -> 230 us (level)
  blocking collectives: 10.7 us -> 70.3 us
  waiting for transfers between devices: 96.9 us -> 55.7 us
  starting transfers between devices: 35 us -> 24.7 us
  other arithmetic: 27.4 us -> 21.8 us
  local copies, waits for them, and re-layouts: 26.5 us -> 23 us
    all_to_all x0 -> x1, blocking collectives: none -> 59.5 us  [exchange(): lax.all_to_all(send, ('gx', 'gz'), split_axis=0, concat_axis=0, tiled=True)]
    all_to_all x2 -> x1, waiting for transfers between devices: 70.1 us -> 19.8 us  [exchange(): lax.all_to_all(send, ('gx', 'gz'), split_axis=0, concat_axis=0, tiled=True)]
    all_to_all x2 -> x1, starting transfers between devices: 14.9 us -> 6.19 us  [exchange(): lax.all_to_all(send, ('gx', 'gz'), split_axis=0, concat_axis=0, tiled=True)]
    all_to_all x1, waiting for transfers between devices: 9.29 us -> 16.3 us  [body(): lax.all_to_all(input_part.reshape(size_gx, input_part.shape[0] // size_gx...]
    convert_element_type x3 -> x0, local copies, waits for them, and re-layouts: 4.05 us -> none  [the longest x2 3.13 us: body(): second_moment = place(got_moments[:, tile_side:]).astype(jnp.float32)]
    convert_element_type x2 -> x0, other arithmetic: 2.78 us -> none  [the longest x1 1.66 us: body(): second_moment = place(got_moments[:, tile_side:]).astype(jnp.float32)]
  transfers between devices with their start and end apart: 8 -> 7, of which waited for: 6 -> 5; matrix products, arithmetic and copies ran while one was open for 27% -> 24% of each run, Pallas kernels for 0% -> 0%
where the time goes in v10:
time: 230 us
  blocking collectives  70.3 us (31%)
  waiting for transfers between devices  55.7 us (24%)
  starting transfers between devices  24.7 us (11%)
  local copies, waits for them, and re-layouts  23 us (10%)
  other arithmetic  21.8 us (9%)
  matrix products  20.1 us (9%)
  between operations  14 us (6%)
    all_to_all x1, blocking collectives, exchange(): lax.all_to_all(send, ('gx', 'gz'), split_axis=0, concat_axis=0, tiled=True)  59.5 us
    all_to_all x1, waiting for transfers between devices, exchange(): lax.all_to_all(send, ('gx', 'gz'), split_axis=0, concat_axis=0, tiled=True)  19.8 us
    all_to_all x1, waiting for transfers between devices, body(): lax.all_to_all(input_part.reshape(size_gx, input_part.shape[0] // size_gx...  16.3 us
    reduce_scatter x1, waiting for transfers between devices, body(): lax.psum_scatter((factor * jnp.dot(grad_band, token_band, preferred_eleme...  12.9 us
    all_gather x1, blocking collectives, body(): grad_band = lax.all_gather(grad_out.T, 'gz', axis=0, tiled=True)  10.8 us
    all_to_all x1, starting transfers between devices, body(): lax.all_to_all(labels.reshape(group_size, capacity), ('gx', 'gz'), split_...  8.58 us
    dot_general x1, matrix products, body(): jnp.dot(grad_band, token_band, preferred_element_type=jnp.float32)  7.27 us
    gather x3, local copies, waits for them, and re-layouts, place(): jnp.take(received.reshape(total_slots, tile_side, tile_side), picked, axi...  6.86 us
  transfers between devices with their start and end apart: 7, of which 5 were waited for; matrix products, arithmetic and copies ran while one was open for 24% of the time, Pallas kernels for 0%

profile of v10, /device:TPU:1, one launch (start us, length us, event | category | flops | bytes accessed | tf_op | source)
XLA Modules:
  0.0 229.5 jit_solution(9249391063092930942)
XLA Ops:
  9.6 8.6 %all-to-all-start.1 = ((s32[32,1,2]{2,1,0:T(1,128)}), s32[32,1,2]{2,1,0:T(1,128)S(1)}, u32[]{:S(2)}, u32[]{:S(2)}) async-start(s32[32,1,2]{2,1,0:T(1,128)} %bitcast.3), calls=%async_computation.1 | async-start | bytes 32768 | tf_op jit(solution)/shard_map/all_to_all | solution.py:60
  18.2 2.1 gather_fusion
  20.3 3.4 %select_convert_fusion.1 = bf16[64,128,128]{2,1,0:T(8,128)(2,1)} fusion(bf16[64,128,128]{2,1,0:T(8,128)(2,1)} %gather_fusion, pred[64]{0:T(512)(128)(4,1)S(1)} %compare_and_fusion.2), kind=kLoop, calls=%fused_computation.8 | loop fusion | flops 1048576 | bytes 4194368 | tf_op jit(solution)/shard_map/convert_element_type | solution.py:63
  25.1 6.2 %all-to-all-start = ((bf16[32,2,128,128]{3,2,1,0:T(8,128)(2,1)}), bf16[32,2,128,128]{3,2,1,0:T(8,128)(2,1)}, u32[]{:S(2)}, u32[]{:S(2)}) async-start(bf16[32,2,128,128]{3,2,1,0:T(8,128)(2,1)} %bitcast.51), calls=%async_computation | async-start | bytes 4194304 | tf_op jit(solution)/shard_map/all_to_all | solution.py:58
  31.3 1.7 pad_maximum_fusion
  33.1 3.0 %gather_fusion.1 = bf16[64,256,128]{2,1,0:T(8,128)(2,1)} fusion(bf16[24,256,128]{2,1,0:T(8,128)(2,1)S(1)} %pad_maximum_fusion, s32[1024]{0:T(1024)S(1)} %pad_clamp_fusion.1), kind=kCustom, calls=%fused_computation.4 | custom fusion | bytes 8388864 | tf_op jit(solution)/shard_map/jit(_take)/gather | solution.py:68
  36.1 5.9 %select_convert_fusion = bf16[64,256,128]{2,1,0:T(8,128)(2,1)} fusion(bf16[64,256,128]{2,1,0:T(8,128)(2,1)} %gather_fusion.1, pred[64]{0:T(512)(128)(4,1)S(1)} %compare_and_fusion.2), kind=kLoop, calls=%fused_computation.6 | loop fusion | flops 2097152 | bytes 8388672 | tf_op jit(solution)/shard_map/convert_element_type | solution.py:70
  43.5 19.8 %all-to-all-done = bf16[32,2,128,128]{3,2,1,0:T(8,128)(2,1)} async-done(((bf16[32,2,128,128]{3,2,1,0:T(8,128)(2,1)}), bf16[32,2,128,128]{3,2,1,0:T(8,128)(2,1)}, u32[]{:S(2)}, u32[]{:S(2)}) %all-to-all-start) | async-done | bytes 2097184 | tf_op jit(solution)/shard_map/all_to_all | solution.py:58
  63.3 2.3 gather_fusion.2
  67.4 10.8 %all_gather.11 = bf16[1024,384]{0,1:T(8,128)(2,1)S(1)} all-gather(bf16[256,384]{0,1:T(8,128)(2,1)S(1)} %bitcast.59), channel_id=1, replica_groups=mesh['gx'=8,'gy'=8,'gz'=4] {'gz'}, dimensions={0}, use_global_device_ids=true | all-gather | bytes 983040 | tf_op jit(solution)/shard_map/all_gather | solution.py:91
  78.2 7.3 %multiply_convert_fusion = bf16[1024,3072]{1,0:T(8,128)(2,1)} fusion(bf16[1024,384]{0,1:T(8,128)(2,1)S(1)} %all_gather.11, bf16[384,3072]{1,0:T(8,128)(2,1)} %all-gather.3.cloned.1.call-done), kind=kOutput, calls=%fused_computation.5 | convolution fusion | flops 2422210560 | bytes 9437184 | tf_op jit(solution)/shard_map/dot_general | solution.py:124
  85.4 59.5 %all_to_all.29 = bf16[32,2,256,128]{3,2,1,0:T(8,128)(2,1)} all-to-all(bf16[32,2,256,128]{3,2,1,0:T(8,128)(2,1)} %bitcast.49), channel_id=1, replica_groups=mesh['gx'=8,'gy'=8,'gz'=4] {'gx','gz'}, dimensions={0} | all-to-all | bytes 8388608 | tf_op jit(solution)/shard_map/all_to_all | solution.py:58
  145.0 6.1 %multiply_convert_fusion.2 = bf16[384,1024]{1,0:T(8,128)(2,1)S(1)} fusion(bf16[384,3072]{1,0:T(8,128)(2,1)} %all-gather.3.cloned.1.call-done, bf16[1024,3072]{1,0:T(8,128)(2,1)} %all-gather.5.cloned.1.call-done), kind=kOutput, calls=%fused_computation.19 | convolution fusion | flops 2416705536 | bytes 9437184 | tf_op jit(solution)/shard_map/dot_general | solution.py:98
  152.0 3.6 %all-to-all-start.3 = ((bf16[384,4,256]{2,0,1:T(8,128)(2,1)}), bf16[384,4,256]{2,0,1:T(8,128)(2,1)S(1)}, u32[]{:S(2)}, u32[]{:S(2)}) async-start(bf16[384,4,256]{2,0,1:T(8,128)(2,1)} %bitcast.48), calls=%async_computation.3 | async-start | bytes 1572864 | tf_op jit(solution)/shard_map/all_to_all | solution.py:99
  155.6 6.7 %multiply_convert_fusion.1 = bf16[384,3072]{1,0:T(8,128)(2,1)} fusion(bf16[1024,384]{0,1:T(8,128)(2,1)S(1)} %all_gather.11, bf16[1024,3072]{1,0:T(8,128)(2,1)} %all-gather.5.cloned.1.call-done), kind=kOutput, calls=%fused_computation.7 | convolution fusion | flops 2418278400 | bytes 9437184 | tf_op jit(solution)/shard_map/dot_general | solution.py:111
  162.3 4.6 %all-to-all-done.3 = bf16[384,4,256]{2,0,1:T(8,128)(2,1)S(1)} async-done(((bf16[384,4,256]{2,0,1:T(8,128)(2,1)}), bf16[384,4,256]{2,0,1:T(8,128)(2,1)S(1)}, u32[]{:S(2)}, u32[]{:S(2)}) %all-to-all-start.3) | async-done | bytes 786464 | tf_op jit(solution)/shard_map/all_to_all | solution.py:99
  166.9 6.3 %all-to-all-start.4 = ((bf16[8,48,3072]{2,1,0:T(8,128)(2,1)}), bf16[8,48,3072]{2,1,0:T(8,128)(2,1)}, u32[]{:S(2)}, u32[]{:S(2)}) async-start(bf16[8,48,3072]{2,1,0:T(8,128)(2,1)} %bitcast.57), calls=%async_computation.4 | async-start | bytes 4718592 | tf_op jit(solution)/shard_map/all_to_all | solution.py:115
  173.3 5.0 %fusion.14 = (bf16[64,128,128]{2,1,0:T(8,128)(2,1)}, bf16[64,128,128]{2,1,0:T(8,128)(2,1)}) fusion(bf16[64,256,128]{2,1,0:T(8,128)(2,1)} %bitcast.50), kind=kLoop, calls=%fused_computation.63 | loop fusion | bytes 8388608 | tf_op jit(solution)/shard_map/slice | solution.py:96
  178.3 2.3 gather_fusion.4
  180.6 2.3 gather_fusion.3
  186.1 16.3 %all-to-all-done.4 = bf16[8,48,3072]{2,1,0:T(8,128)(2,1)} async-done(((bf16[8,48,3072]{2,1,0:T(8,128)(2,1)}), bf16[8,48,3072]{2,1,0:T(8,128)(2,1)}, u32[]{:S(2)}, u32[]{:S(2)}) %all-to-all-start.4) | async-done | bytes 2359328 | tf_op jit(solution)/shard_map/all_to_all | solution.py:115
  202.3 2.9 %reduce_sum.68 = bf16[48,3072]{1,0:T(8,128)(2,1)} reduce(bf16[8,48,3072]{2,1,0:T(8,128)(2,1)} %all-to-all-done.4, bf16[]{:T(256)} %constant.157.clone.1), dimensions={0}, to_apply=%region_5.7 | reduce | flops 1032192 | bytes 2654210 | tf_op jit(solution)/shard_map/reduce_sum | solution.py:122
  205.2 12.9 %reduce-scatter.2.cloned.1.call-done = bf16[128,3072]{1,0:T(8,128)(2,1)} async-done(((bf16[1024,3072]{1,0:T(8,128)(2,1)}), bf16[128,3072]{1,0:T(8,128)(2,1)}) %reduce-scatter.2.cloned.1.call-update) | async-done | bytes 786448 | tf_op jit(solution)/shard_map/reduce_scatter | solution.py:123
  218.1 4.9 %multiply_add_fusion = (f32[128,3072]{1,0:T(8,128)}, f32[128,3072]{1,0:T(8,128)}, f32[128,3072]{1,0:T(8,128)}) fusion(bf16[128,3072]{1,0:T(8,128)(2,1)S(1)} %bitcast.53, s32[3072]{0:T(1024)S(1)} %get-tuple-element.49, s32[3072]{0:T(1024)S(1)} %get-tuple-element.50, s32[128]{0:T(128)S(1)} %get-tuple-element.51, s32[128]{0:T(128)S(1)} %get-tuple-element.52, ...), kind=kLoop, calls=%fused_computation.18 | loop fusion | flops 17301504 | bytes 7905408 | tf_op jit(solution)/shard_map/add | solution.py:148
  (51 shorter events, 11.3 us)
Async XLA Ops:
  7.2 11.0 %copy-start = (f32[24,128,128]{2,1,0:T(8,128)S(1)}, f32[24,128,128]{2,1,0:T(8,128)}, u32[]{:S(2)}) copy-start(f32[24,128,128]{2,1,0:T(8,128)} %param.9) | copy-start | bytes 4718596
  7.2 56.1 %all-gather.3.cloned.1.call-start = ((), (), s32[]{:S(2)}) async-start(), calls=%async_computation.6 | async-start | bytes 2654208 | tf_op jit(solution)/shard_map/all_gather | solution.py:71
  9.6 15.5 %all-to-all-start.1 = ((s32[32,1,2]{2,1,0:T(1,128)}), s32[32,1,2]{2,1,0:T(1,128)S(1)}, u32[]{:S(2)}, u32[]{:S(2)}) async-start(s32[32,1,2]{2,1,0:T(1,128)} %bitcast.3), calls=%async_computation.1 | async-start | bytes 32768 | tf_op jit(solution)/shard_map/all_to_all | solution.py:60
  25.1 6.2 %copy-start.3 = (f32[24,128,128]{2,1,0:T(8,128)S(1)}, f32[24,128,128]{2,1,0:T(8,128)}, u32[]{:S(2)}) copy-start(f32[24,128,128]{2,1,0:T(8,128)} %param.11) | copy-start | bytes 4718596
  25.1 38.3 %all-to-all-start = ((bf16[32,2,128,128]{3,2,1,0:T(8,128)(2,1)}), bf16[32,2,128,128]{3,2,1,0:T(8,128)(2,1)}, u32[]{:S(2)}, u32[]{:S(2)}) async-start(bf16[32,2,128,128]{3,2,1,0:T(8,128)(2,1)} %bitcast.51), calls=%async_computation | async-start | bytes 4194304 | tf_op jit(solution)/shard_map/all_to_all | solution.py:58
  31.3 113.7 %all-gather.5.cloned.1.call-start = ((), (), s32[]{:S(2)}) async-start(), calls=%async_computation.7 | async-start | bytes 7077888 | tf_op jit(solution)/shard_map/all_gather | solution.py:90
  66.3 1.1 copy-start.4
  67.3 150.7 %reduce-scatter.2.cloned.1.call-start = ((), (), s32[]{:S(2)}) async-start(), calls=%async_computation.8 | async-start | bytes 7077888 | tf_op jit(solution)/shard_map/reduce_scatter | solution.py:123
  152.0 14.9 %all-to-all-start.3 = ((bf16[384,4,256]{2,0,1:T(8,128)(2,1)}), bf16[384,4,256]{2,0,1:T(8,128)(2,1)S(1)}, u32[]{:S(2)}, u32[]{:S(2)}) async-start(bf16[384,4,256]{2,0,1:T(8,128)(2,1)} %bitcast.48), calls=%async_computation.3 | async-start | bytes 1572864 | tf_op jit(solution)/shard_map/all_to_all | solution.py:99
  166.9 6.3 %copy-start.5 = (s32[1,24]{1,0:T(1,128)S(1)}, s32[1,24]{1,0:T(1,128)}, u32[]{:S(2)}) copy-start(s32[1,24]{1,0:T(1,128)} %param.13) | copy-start | bytes 292
  166.9 35.4 %all-to-all-start.4 = ((bf16[8,48,3072]{2,1,0:T(8,128)(2,1)}), bf16[8,48,3072]{2,1,0:T(8,128)(2,1)}, u32[]{:S(2)}, u32[]{:S(2)}) async-start(bf16[8,48,3072]{2,1,0:T(8,128)(2,1)} %bitcast.57), calls=%async_computation.4 | async-start | bytes 4718592 | tf_op jit(solution)/shard_map/all_to_all | solution.py:115
  186.1 32.0 %copy-start.2 = (bf16[16,8,24,128]{3,1,2,0:T(8,128)(2,1)S(1)}, bf16[16,8,24,128]{3,1,2,0:T(8,128)(2,1)}, u32[]{:S(2)}) copy-start(bf16[16,8,24,128]{3,1,2,0:T(8,128)(2,1)} %copy.33) | copy-start | bytes 2359300
  218.1 4.9 %copy-start.1 = (f32[24,128,128]{2,1,0:T(8,128)S(1)}, f32[24,128,128]{2,1,0:T(8,128)}, u32[]{:S(2)}) copy-start(f32[24,128,128]{2,1,0:T(8,128)} %param.9) | copy-start | bytes 4718596
Sparse Core Ops, SparseCore 0:
  9.8 38.4 all-gather.2
  67.5 74.1 all-gather.4
  144.2 73.8 reduce-scatter.1

commit v11 on v10

--- a/solution.py
+++ b/solution.py
@@ -57,14 +57,15 @@
         send = send.reshape(group_size, capacity, *send.shape[1:])
         return lax.all_to_all(send, ("gx", "gz"), split_axis=0, concat_axis=0, tiled=True)
 
-    got_labels = lax.all_to_all(
-        labels.reshape(group_size, capacity), ("gx", "gz"), split_axis=0, concat_axis=0, tiled=True
-    )
     send_weight = jnp.take(flat_weight, source, axis=0).astype(jnp.bfloat16)
     send_weight, flat_first, flat_second = lax.optimization_barrier(
         (send_weight, flat_first, flat_second)
     )
     got_weight = exchange(send_weight)
+    labels, _ = lax.optimization_barrier((labels, send_weight))
+    got_labels = lax.all_to_all(
+        labels.reshape(group_size, capacity), ("gx", "gz"), split_axis=0, concat_axis=0, tiled=True
+    )
     send_moments = jnp.take(
         jnp.concatenate([flat_first, flat_second], axis=1), source, axis=0
     ).astype(jnp.bfloat16)

time: 230 us -> 231 us (level)
  blocking collectives: 70.3 us -> 85.5 us
  starting transfers between devices: 24.7 us -> 15.1 us
  waiting for transfers between devices: 55.7 us -> 51.3 us
    all_to_all x0 -> x1, blocking collectives: none -> 15.3 us  [body(): lax.all_to_all(labels.reshape(group_size, capacity), ('gx', 'gz'), split_...]
    all_to_all x1 -> x0, starting transfers between devices: 8.58 us -> none  [body(): lax.all_to_all(labels.reshape(group_size, capacity), ('gx', 'gz'), split_...]
    all_to_all x1, waiting for transfers between devices: 19.8 us -> 16.9 us  [exchange(): lax.all_to_all(send, ('gx', 'gz'), split_axis=0, concat_axis=0, tiled=True)]
  transfers between devices with their start and end apart: 7 -> 6, of which waited for: 5 -> 4; matrix products, arithmetic and copies ran while one was open for 24% -> 24% of each run, Pallas kernels for 0% -> 0%
where the time goes in v11:
time: 231 us; the launch traced here: 230 us
  blocking collectives  85.5 us (37%)
  waiting for transfers between devices  51.3 us (22%)
  local copies, waits for them, and re-layouts  22.4 us (10%)
  other arithmetic  21.7 us (9%)
  matrix products  20 us (9%)
  starting transfers between devices  15.1 us (7%)
  between operations  14 us (6%)
    all_to_all x1, blocking collectives, exchange(): lax.all_to_all(send, ('gx', 'gz'), split_axis=0, concat_axis=0, tiled=True)  59.4 us
    all_to_all x1, waiting for transfers between devices, exchange(): lax.all_to_all(send, ('gx', 'gz'), split_axis=0, concat_axis=0, tiled=True)  16.9 us
    all_to_all x1, waiting for transfers between devices, body(): lax.all_to_all(input_part.reshape(size_gx, input_part.shape[0] // size_gx...  16.3 us
    all_to_all x1, blocking collectives, body(): lax.all_to_all(labels.reshape(group_size, capacity), ('gx', 'gz'), split_...  15.3 us
    reduce_scatter x1, waiting for transfers between devices, body(): lax.psum_scatter((factor * jnp.dot(grad_band, token_band, preferred_eleme...  12.9 us
    all_gather x1, blocking collectives, body(): grad_band = lax.all_gather(grad_out.T, 'gz', axis=0, tiled=True)  10.8 us
    dot_general x1, matrix products, body(): jnp.dot(grad_band, token_band, preferred_element_type=jnp.float32)  7.23 us
    gather x3, local copies, waits for them, and re-layouts, place(): jnp.take(received.reshape(total_slots, tile_side, tile_side), picked, axi...  6.86 us
  transfers between devices with their start and end apart: 6, of which 4 were waited for; matrix products, arithmetic and copies ran while one was open for 24% of the time, Pallas kernels for 0%

profile of v11, /device:TPU:1, one launch (start us, length us, event | category | flops | bytes accessed | tf_op | source)
XLA Modules:
  0.0 230.0 jit_solution(13866421206314142745)
XLA Ops:
  8.9 2.1 gather_fusion
  11.0 3.4 %select_convert_fusion.1 = bf16[64,128,128]{2,1,0:T(8,128)(2,1)} fusion(bf16[64,128,128]{2,1,0:T(8,128)(2,1)} %gather_fusion, pred[64]{0:T(512)(128)(4,1)S(1)} %compare_and_fusion.2), kind=kLoop, calls=%fused_computation.8 | loop fusion | flops 1048576 | bytes 4194368 | tf_op jit(solution)/shard_map/convert_element_type | solution.py:60
  14.5 15.3 %all_to_all.29 = s32[32,1,2]{2,1,0:T(1,128)S(1)} all-to-all(s32[32,1,2]{2,1,0:T(1,128)S(1)} %bitcast.60), channel_id=1, replica_groups=mesh['gx'=8,'gy'=8,'gz'=4] {'gx','gz'}, dimensions={0} | all-to-all | bytes 512 | tf_op jit(solution)/shard_map/all_to_all | solution.py:66
  29.8 5.1 %all-to-all-start = ((bf16[32,2,128,128]{3,2,1,0:T(8,128)(2,1)}), bf16[32,2,128,128]{3,2,1,0:T(8,128)(2,1)}, u32[]{:S(2)}, u32[]{:S(2)}) async-start(bf16[32,2,128,128]{3,2,1,0:T(8,128)(2,1)} %bitcast.51), calls=%async_computation | async-start | bytes 4194304 | tf_op jit(solution)/shard_map/all_to_all | solution.py:58
  35.0 1.7 pad_maximum_fusion
  36.7 3.0 %gather_fusion.1 = bf16[64,256,128]{2,1,0:T(8,128)(2,1)} fusion(bf16[24,256,128]{2,1,0:T(8,128)(2,1)S(1)} %pad_maximum_fusion, s32[1024]{0:T(1024)S(1)} %pad_clamp_fusion.1), kind=kCustom, calls=%fused_computation.4 | custom fusion | bytes 8388864 | tf_op jit(solution)/shard_map/jit(_take)/gather | solution.py:69
  39.8 5.8 %select_convert_fusion = bf16[64,256,128]{2,1,0:T(8,128)(2,1)} fusion(bf16[64,256,128]{2,1,0:T(8,128)(2,1)} %gather_fusion.1, pred[64]{0:T(512)(128)(4,1)S(1)} %compare_and_fusion.2), kind=kLoop, calls=%fused_computation.6 | loop fusion | flops 2097152 | bytes 8388672 | tf_op jit(solution)/shard_map/convert_element_type | solution.py:71
  47.1 16.9 %all-to-all-done = bf16[32,2,128,128]{3,2,1,0:T(8,128)(2,1)} async-done(((bf16[32,2,128,128]{3,2,1,0:T(8,128)(2,1)}), bf16[32,2,128,128]{3,2,1,0:T(8,128)(2,1)}, u32[]{:S(2)}, u32[]{:S(2)}) %all-to-all-start) | async-done | bytes 2097184 | tf_op jit(solution)/shard_map/all_to_all | solution.py:58
  64.0 2.3 gather_fusion.2
  68.1 10.8 %all_gather.11 = bf16[1024,384]{0,1:T(8,128)(2,1)S(1)} all-gather(bf16[256,384]{0,1:T(8,128)(2,1)S(1)} %bitcast.59), channel_id=1, replica_groups=mesh['gx'=8,'gy'=8,'gz'=4] {'gz'}, dimensions={0}, use_global_device_ids=true | all-gather | bytes 983040 | tf_op jit(solution)/shard_map/all_gather | solution.py:92
  78.8 7.2 %multiply_convert_fusion = bf16[1024,3072]{1,0:T(8,128)(2,1)} fusion(bf16[1024,384]{0,1:T(8,128)(2,1)S(1)} %all_gather.11, bf16[384,3072]{1,0:T(8,128)(2,1)} %all-gather.3.cloned.1.call-done), kind=kOutput, calls=%fused_computation.5 | convolution fusion | flops 2422210560 | bytes 9437184 | tf_op jit(solution)/shard_map/dot_general | solution.py:125
  86.1 59.4 %all_to_all.30 = bf16[32,2,256,128]{3,2,1,0:T(8,128)(2,1)} all-to-all(bf16[32,2,256,128]{3,2,1,0:T(8,128)(2,1)} %bitcast.49), channel_id=1, replica_groups=mesh['gx'=8,'gy'=8,'gz'=4] {'gx','gz'}, dimensions={0} | all-to-all | bytes 8388608 | tf_op jit(solution)/shard_map/all_to_all | solution.py:58
  145.5 6.1 %multiply_convert_fusion.2 = bf16[384,1024]{1,0:T(8,128)(2,1)S(1)} fusion(bf16[384,3072]{1,0:T(8,128)(2,1)} %all-gather.3.cloned.1.call-done, bf16[1024,3072]{1,0:T(8,128)(2,1)} %all-gather.5.cloned.1.call-done), kind=kOutput, calls=%fused_computation.19 | convolution fusion | flops 2416705536 | bytes 9437184 | tf_op jit(solution)/shard_map/dot_general | solution.py:99
  152.6 3.6 %all-to-all-start.3 = ((bf16[384,4,256]{2,0,1:T(8,128)(2,1)}), bf16[384,4,256]{2,0,1:T(8,128)(2,1)S(1)}, u32[]{:S(2)}, u32[]{:S(2)}) async-start(bf16[384,4,256]{2,0,1:T(8,128)(2,1)} %bitcast.48), calls=%async_computation.3 | async-start | bytes 1572864 | tf_op jit(solution)/shard_map/all_to_all | solution.py:100
  156.2 6.7 %multiply_convert_fusion.1 = bf16[384,3072]{1,0:T(8,128)(2,1)} fusion(bf16[1024,384]{0,1:T(8,128)(2,1)S(1)} %all_gather.11, bf16[1024,3072]{1,0:T(8,128)(2,1)} %all-gather.5.cloned.1.call-done), kind=kOutput, calls=%fused_computation.7 | convolution fusion | flops 2418278400 | bytes 9437184 | tf_op jit(solution)/shard_map/dot_general | solution.py:112
  162.8 4.7 %all-to-all-done.3 = bf16[384,4,256]{2,0,1:T(8,128)(2,1)S(1)} async-done(((bf16[384,4,256]{2,0,1:T(8,128)(2,1)}), bf16[384,4,256]{2,0,1:T(8,128)(2,1)S(1)}, u32[]{:S(2)}, u32[]{:S(2)}) %all-to-all-start.3) | async-done | bytes 786464 | tf_op jit(solution)/shard_map/all_to_all | solution.py:100
  167.5 6.3 %all-to-all-start.4 = ((bf16[8,48,3072]{2,1,0:T(8,128)(2,1)}), bf16[8,48,3072]{2,1,0:T(8,128)(2,1)}, u32[]{:S(2)}, u32[]{:S(2)}) async-start(bf16[8,48,3072]{2,1,0:T(8,128)(2,1)} %bitcast.57), calls=%async_computation.4 | async-start | bytes 4718592 | tf_op jit(solution)/shard_map/all_to_all | solution.py:116
  173.9 5.0 %fusion.14 = (bf16[64,128,128]{2,1,0:T(8,128)(2,1)}, bf16[64,128,128]{2,1,0:T(8,128)(2,1)}) fusion(bf16[64,256,128]{2,1,0:T(8,128)(2,1)} %bitcast.50), kind=kLoop, calls=%fused_computation.63 | loop fusion | bytes 8388608 | tf_op jit(solution)/shard_map/slice | solution.py:97
  178.8 2.3 gather_fusion.4
  181.1 2.3 gather_fusion.3
  186.6 16.3 %all-to-all-done.4 = bf16[8,48,3072]{2,1,0:T(8,128)(2,1)} async-done(((bf16[8,48,3072]{2,1,0:T(8,128)(2,1)}), bf16[8,48,3072]{2,1,0:T(8,128)(2,1)}, u32[]{:S(2)}, u32[]{:S(2)}) %all-to-all-start.4) | async-done | bytes 2359328 | tf_op jit(solution)/shard_map/all_to_all | solution.py:116
  202.9 2.9 %reduce_sum.68 = bf16[48,3072]{1,0:T(8,128)(2,1)} reduce(bf16[8,48,3072]{2,1,0:T(8,128)(2,1)} %all-to-all-done.4, bf16[]{:T(256)} %constant.157.clone.1), dimensions={0}, to_apply=%region_5.7 | reduce | flops 1032192 | bytes 2654210 | tf_op jit(solution)/shard_map/reduce_sum | solution.py:123
  205.7 12.9 %reduce-scatter.2.cloned.1.call-done = bf16[128,3072]{1,0:T(8,128)(2,1)} async-done(((bf16[1024,3072]{1,0:T(8,128)(2,1)}), bf16[128,3072]{1,0:T(8,128)(2,1)}) %reduce-scatter.2.cloned.1.call-update) | async-done | bytes 786448 | tf_op jit(solution)/shard_map/reduce_scatter | solution.py:124
  218.6 4.9 %multiply_add_fusion = (f32[128,3072]{1,0:T(8,128)}, f32[128,3072]{1,0:T(8,128)}, f32[128,3072]{1,0:T(8,128)}) fusion(bf16[128,3072]{1,0:T(8,128)(2,1)S(1)} %bitcast.53, s32[3072]{0:T(1024)S(1)} %get-tuple-element.51, s32[3072]{0:T(1024)S(1)} %get-tuple-element.52, s32[128]{0:T(128)S(1)} %get-tuple-element.53, s32[128]{0:T(128)S(1)} %get-tuple-element.54, ...), kind=kLoop, calls=%fused_computation.18 | loop fusion | flops 17301504 | bytes 7905408 | tf_op jit(solution)/shard_map/add | solution.py:149
  (50 shorter events, 9.3 us)
Async XLA Ops:
  7.2 1.7 copy-start
  7.2 56.8 %all-gather.3.cloned.1.call-start = ((), (), s32[]{:S(2)}) async-start(), calls=%async_computation.6 | async-start | bytes 2654208 | tf_op jit(solution)/shard_map/all_gather | solution.py:72
  29.8 5.2 %copy-start.3 = (f32[24,128,128]{2,1,0:T(8,128)S(1)}, f32[24,128,128]{2,1,0:T(8,128)}, u32[]{:S(2)}) copy-start(f32[24,128,128]{2,1,0:T(8,128)} %param.11) | copy-start | bytes 4718596
  29.8 34.2 %all-to-all-start = ((bf16[32,2,128,128]{3,2,1,0:T(8,128)(2,1)}), bf16[32,2,128,128]{3,2,1,0:T(8,128)(2,1)}, u32[]{:S(2)}, u32[]{:S(2)}) async-start(bf16[32,2,128,128]{3,2,1,0:T(8,128)(2,1)} %bitcast.51), calls=%async_computation | async-start | bytes 4194304 | tf_op jit(solution)/shard_map/all_to_all | solution.py:58
  35.0 110.6 %all-gather.5.cloned.1.call-start = ((), (), s32[]{:S(2)}) async-start(), calls=%async_computation.7 | async-start | bytes 7077888 | tf_op jit(solution)/shard_map/all_gather | solution.py:91
  66.9 1.1 copy-start.4
  68.0 150.6 %reduce-scatter.2.cloned.1.call-start = ((), (), s32[]{:S(2)}) async-start(), calls=%async_computation.8 | async-start | bytes 7077888 | tf_op jit(solution)/shard_map/reduce_scatter | solution.py:124
  152.6 14.9 %all-to-all-start.3 = ((bf16[384,4,256]{2,0,1:T(8,128)(2,1)}), bf16[384,4,256]{2,0,1:T(8,128)(2,1)S(1)}, u32[]{:S(2)}, u32[]{:S(2)}) async-start(bf16[384,4,256]{2,0,1:T(8,128)(2,1)} %bitcast.48), calls=%async_computation.3 | async-start | bytes 1572864 | tf_op jit(solution)/shard_map/all_to_all | solution.py:100
  167.5 6.3 %copy-start.5 = (s32[1,24]{1,0:T(1,128)S(1)}, s32[1,24]{1,0:T(1,128)}, u32[]{:S(2)}) copy-start(s32[1,24]{1,0:T(1,128)} %param.13) | copy-start | bytes 292
  167.5 35.4 %all-to-all-start.4 = ((bf16[8,48,3072]{2,1,0:T(8,128)(2,1)}), bf16[8,48,3072]{2,1,0:T(8,128)(2,1)}, u32[]{:S(2)}, u32[]{:S(2)}) async-start(bf16[8,48,3072]{2,1,0:T(8,128)(2,1)} %bitcast.57), calls=%async_computation.4 | async-start | bytes 4718592 | tf_op jit(solution)/shard_map/all_to_all | solution.py:116
  186.6 32.0 %copy-start.2 = (bf16[16,8,24,128]{3,1,2,0:T(8,128)(2,1)S(1)}, bf16[16,8,24,128]{3,1,2,0:T(8,128)(2,1)}, u32[]{:S(2)}) copy-start(bf16[16,8,24,128]{3,1,2,0:T(8,128)(2,1)} %copy.33) | copy-start | bytes 2359300
  218.6 4.9 %copy-start.1 = (f32[24,128,128]{2,1,0:T(8,128)S(1)}, f32[24,128,128]{2,1,0:T(8,128)}, u32[]{:S(2)}) copy-start(f32[24,128,128]{2,1,0:T(8,128)} %param.9) | copy-start | bytes 4718596
Sparse Core Ops, SparseCore 0:
  9.8 33.5 all-gather.2
  68.1 74.0 all-gather.4
  144.7 73.8 reduce-scatter.1
